TPU v7x, 256 devices: a whole 4x4x8 slice. The times are simulated.
256 devices in a mesh: expert: 16 (over y_hi, z), mp: 8 (over y_lo, x), batch: 2 (over core).
Axes of the slice: x: 4, y: 4 (y_hi: 2, y_lo: 2; y = y_hi * 2 + y_lo), z: 8, core: 2. Of those that a mesh axis runs over, the one named last changes fastest.
Arguments:
- tokens: bfloat16 [2, 2048, 2880], P('batch', 'expert', 'mp'), may hold values from -6 to 6
- segments: int32 [2, 2048], P('batch'), may hold values from 0 to 63, never falling along the last dimension, each value on 1 to 1024 neighbouring positions
- attn_gain: float32 [2880], replicated, may hold values from 0.6 to 9
- w_query: bfloat16 [2880, 4096], P('expert', 'mp'), may hold values from -0.109375 to 0.109375
- key_weight: bfloat16 [2880, 512], P('expert', 'mp'), may hold values from -0.109375 to 0.109375
- value_weight: bfloat16 [2880, 512], P('expert', 'mp'), may hold values from -0.109375 to 0.109375
- w_out: bfloat16 [4096, 2880], P('mp', 'expert'), may hold values from -0.09375 to 0.09375
- sink_head_logit: float32 [64], P('mp'), may hold values from -4 to 4
- moe_gain: float32 [2880], replicated, may hold values from 0.5 to 1.5
- expert_in: bfloat16 [16, 2, 2880, 2880], P('expert', None, None, 'mp'), may hold values from -0.3125 to 0.3125
- expert_down: bfloat16 [16, 2880, 2880], P('expert', 'mp'), may hold values from -0.01953125 to 0.01953125
- routes: int32 [2, 2048, 4], P('batch', 'expert'), may hold values from 0 to 15, all different within a row; in each aligned block of 128 rows (0 to 127, 128 to 255, ..., all dimensions but the last counted through in order) at most 48 rows name the same one
- route_weights: float32 [2, 2048, 4], P('batch', 'expert'), may hold values from 0.1 to 1
Outputs:
- hidden: bfloat16 [2, 2048, 2880], P('batch', 'expert', 'mp')
- key_cache: bfloat16 [2, 2048, 512], P('batch', 'expert', 'mp')
- value_cache: bfloat16 [2, 2048, 512], P('batch', 'expert', 'mp')
Inputs may be any that keep to these rules, and one draw needn't show every extreme that they name: Within each aligned block of 128 tokens of a micro-batch (the tokens of one index of expert), no expert is named by more than 48 routes; a token's routes name different experts. `segments`: segment numbers never fall along a micro-batch; one segment holds at most 1024 tokens.
All inputs are finite; a program needn't handle non-finite values.
Results may differ from a plain program's by a relative error of at most 0.024.
The roundings to bfloat16 on the way count: a program that leaves them out, or rounds other values in their place, can miss the bound.
Values may be sent and summed in bfloat16 or wider, within the bound.
No kernel may reach another device: no remote copies, remote signals or barrier semaphores. Data moves between devices by JAX's collectives and lax.ppermute only.
A program may use at most 64 MiB of HBM per device.

v0:
```python
import math

import jax
import jax.numpy as jnp
from jax import lax
from jax.sharding import PartitionSpec as P

HEAD_SIZE = 64


eps = 1e-05
rope_base = 150000.0
clamp_limit = 7.0
glu_alpha = 1.702


def rms_norm(row_block, gain):
    values = row_block.astype(jnp.float32)
    inv_scale = lax.rsqrt(jnp.mean(values * values, axis=-1, keepdims=True) + eps)
    return (values * inv_scale * gain).astype(jnp.bfloat16)


def apply_rotary(values, token_positions):
    half_dim = values.shape[-1] // 2
    inv_freq = jnp.power(
        rope_base, -2.0 * jnp.arange(half_dim, dtype=jnp.float32) / values.shape[-1]
    )
    rot_angle = token_positions.astype(jnp.float32)[:, None] * inv_freq[None, :]
    cosine = jnp.cos(rot_angle)[:, None, :]
    sine_val = jnp.sin(rot_angle)[:, None, :]
    first_half = values[..., :half_dim]
    second_half = values[..., half_dim:]
    return jnp.concatenate(
        [
            first_half * cosine - second_half * sine_val,
            second_half * cosine + first_half * sine_val,
        ],
        axis=-1,
    )


def expert_rows(row_block, w_in, w_down):
    gate_val = jnp.dot(row_block, w_in[0], preferred_element_type=jnp.float32)
    up_val = jnp.dot(row_block, w_in[1], preferred_element_type=jnp.float32)
    gate_val = jnp.minimum(gate_val, clamp_limit)
    up_val = jnp.clip(up_val, -clamp_limit, clamp_limit)
    activated = ((up_val + 1.0) * gate_val * jax.nn.sigmoid(glu_alpha * gate_val)).astype(
        jnp.bfloat16
    )
    return jnp.dot(activated, w_down, preferred_element_type=jnp.float32)


def shards(
    tokens,
    segments,
    attn_gain,
    w_query,
    key_weight,
    value_weight,
    w_out,
    sink_head_logit,
    moe_gain,
    expert_in,
    expert_down,
    routes,
    route_weights,
):
    local_rows = tokens[0]
    tok_count = local_rows.shape[0]
    expert_devs = lax.axis_size("expert")
    row_start = lax.axis_index("expert") * tok_count
    whole_rows = lax.all_gather(local_rows, "mp", axis=1, tiled=True)
    input_normalised = rms_norm(whole_rows, attn_gain)
    query_cols = w_query.shape[1]
    kv_cols = key_weight.shape[1]
    weight_parts = (
        lax.all_gather(w_query, "expert", axis=0, tiled=True),
        lax.all_gather(key_weight, "expert", axis=0, tiled=True),
        lax.all_gather(value_weight, "expert", axis=0, tiled=True),
    )
    query_raw, key_raw, value_raw = tuple(
        (
            jnp.dot(input_normalised, weight_part, preferred_element_type=jnp.float32)
            for weight_part in weight_parts
        )
    )
    token_positions = row_start + jnp.arange(tok_count, dtype=jnp.int32)
    query_by_head = query_cols // HEAD_SIZE
    kv_heads = kv_cols // HEAD_SIZE
    heads_per_group = query_by_head // kv_heads
    query_matrix = apply_rotary(
        query_raw.reshape(tok_count, query_by_head, HEAD_SIZE), token_positions
    ).astype(jnp.bfloat16)
    key_rotary = (
        apply_rotary(key_raw.reshape(tok_count, kv_heads, HEAD_SIZE), token_positions)
        .astype(jnp.bfloat16)
        .reshape(tok_count, kv_cols)
    )
    value_fresh = value_raw.astype(jnp.bfloat16)
    keys_all, values_all = (
        lax.all_gather(key_rotary, "expert", axis=0, tiled=True),
        lax.all_gather(value_fresh, "expert", axis=0, tiled=True),
    )
    seq_len = keys_all.shape[0]
    seg_all = segments[0]
    seg_local = lax.dynamic_slice_in_dim(seg_all, row_start, tok_count)
    row_total = heads_per_group * tok_count
    query_rows = (
        query_matrix.reshape(tok_count, kv_heads, heads_per_group, HEAD_SIZE)
        .transpose(1, 2, 0, 3)
        .reshape(kv_heads, row_total, HEAD_SIZE)
    )
    key_by_head = keys_all.reshape(seq_len, kv_heads, HEAD_SIZE).transpose(1, 0, 2)
    value_by_head = values_all.reshape(seq_len, kv_heads, HEAD_SIZE).transpose(1, 0, 2)
    row_pos = jnp.tile(token_positions, heads_per_group)
    row_seg = jnp.tile(seg_local, heads_per_group)
    sink_rows = jnp.repeat(sink_head_logit.reshape(kv_heads, heads_per_group), tok_count, axis=1)
    key_block = math.gcd(seq_len, 512)
    block_count = seq_len // key_block
    score_scale = HEAD_SIZE ** (-0.5)

    def block_scores(index):
        key_first = index * key_block
        key_part = lax.dynamic_slice_in_dim(key_by_head, key_first, key_block, 1)
        scores = (
            jnp.einsum("hrd,hkd->hrk", query_rows, key_part, preferred_element_type=jnp.float32)
            * score_scale
        )
        key_pos = key_first + jnp.arange(key_block, dtype=jnp.int32)
        key_seg = lax.dynamic_slice_in_dim(seg_all, key_first, key_block, 0)
        allowed = (key_pos[None, :] <= row_pos[:, None]) & (key_seg[None, :] == row_seg[:, None])
        return jnp.where(allowed[None], scores, -jnp.inf)

    def max_step(index, running):
        return jnp.maximum(running, jnp.max(block_scores(index), axis=-1))

    row_max = lax.fori_loop(0, block_count, max_step, sink_rows)

    def sum_step(index, carried):
        weighted, denom = carried
        probs = jnp.exp(block_scores(index) - row_max[..., None]).astype(jnp.bfloat16)
        value_part = lax.dynamic_slice_in_dim(value_by_head, index * key_block, key_block, 1)
        weighted = weighted + jnp.einsum(
            "hrk,hkd->hrd", probs, value_part, preferred_element_type=jnp.float32
        )
        denom = denom + jnp.sum(probs, axis=-1, dtype=jnp.float32)
        return (weighted, denom)

    init_pair = (
        jnp.zeros((kv_heads, row_total, HEAD_SIZE), jnp.float32),
        jnp.zeros((kv_heads, row_total), jnp.float32),
    )
    weighted, denom = lax.fori_loop(0, block_count, sum_step, init_pair)
    denom = denom + jnp.exp(sink_rows - row_max)
    mixed = (weighted / denom[..., None]).astype(jnp.bfloat16)
    mixed = (
        mixed.reshape(kv_heads, heads_per_group, tok_count, HEAD_SIZE)
        .transpose(2, 0, 1, 3)
        .reshape(tok_count, query_cols)
    )
    out_terms = jnp.dot(
        mixed,
        lax.all_gather(w_out, "expert", axis=1, tiled=True),
        preferred_element_type=jnp.float32,
    )
    attn_part = lax.psum_scatter(
        out_terms.astype(jnp.bfloat16), "mp", scatter_dimension=1, tiled=True
    ).astype(jnp.float32)
    first_out = (local_rows.astype(jnp.float32) + attn_part).astype(jnp.bfloat16)
    top_count = routes.shape[2]
    local_experts = expert_in.shape[0]
    expert_count = local_experts * expert_devs
    capacity = 3 * tok_count * top_count // (2 * expert_count)
    chosen = routes[0].reshape(tok_count * top_count)
    onehot = (chosen[:, None] == jnp.arange(expert_count, dtype=jnp.int32)[None, :]).astype(
        jnp.int32
    )
    ranks = jnp.sum((jnp.cumsum(onehot, axis=0) - onehot) * onehot, axis=1)
    target = chosen * capacity + ranks
    source_row = (
        jnp.full((expert_count * capacity,), tok_count, jnp.int32)
        .at[target]
        .set(jnp.arange(tok_count * top_count, dtype=jnp.int32) // top_count)
    )
    moe_whole = lax.all_gather(first_out, "mp", axis=1, tiled=True)
    moe_normed = rms_norm(moe_whole, moe_gain)
    padded = jnp.concatenate(
        [moe_normed, jnp.zeros((1, moe_normed.shape[1]), jnp.bfloat16)], axis=0
    )
    outgoing = padded[source_row].reshape(expert_count, capacity, padded.shape[1])
    arrived = lax.all_to_all(outgoing, "expert", split_axis=0, concat_axis=0, tiled=True)
    model_width = arrived.shape[2]
    grouped = arrived.reshape(expert_devs, local_experts, capacity, model_width)
    inputs = grouped[:, 0].reshape(expert_devs * capacity, model_width)
    partial_list = [
        expert_rows(inputs, expert_in[0], expert_down[0]).reshape(
            expert_devs, capacity, model_width
        )
    ]
    partials = jnp.stack(partial_list, axis=1).reshape(expert_count, capacity, model_width)
    expert_out = lax.psum_scatter(
        partials.astype(jnp.bfloat16), "mp", scatter_dimension=2, tiled=True
    )
    returned = lax.all_to_all(expert_out, "expert", split_axis=0, concat_axis=0, tiled=True)
    local_width = returned.shape[2]
    picked = returned.reshape(expert_count * capacity, local_width)[target].reshape(
        tok_count, top_count, local_width
    )
    moe_sum = jnp.sum(picked.astype(jnp.float32) * route_weights[0][..., None], axis=1)
    hidden = (first_out.astype(jnp.float32) + moe_sum).astype(jnp.bfloat16)
    return (hidden[None], key_rotary[None], value_fresh[None])


def solution(mesh):
    placed = (
        P("batch", "expert", "mp"),
        P("batch", None),
        P(),
        P("expert", "mp"),
        P("expert", "mp"),
        P("expert", "mp"),
        P("mp", "expert"),
        P("mp"),
        P(),
        P("expert", None, None, "mp"),
        P("expert", "mp", None),
        P("batch", "expert", None),
        P("batch", "expert", None),
    )
    return jax.shard_map(
        shards,
        mesh=mesh,
        in_specs=placed,
        out_specs=(
            P("batch", "expert", "mp"),
            P("batch", "expert", "mp"),
            P("batch", "expert", "mp"),
        ),
        check_vma=False,
    )
```

profile of v0, /device:TPU:1, one launch (start us, length us, event | category | flops | bytes accessed | tf_op | source)
XLA Modules:
  0.0 570.1 jit_solution(6893705568752840482)
XLA Ops:
  7.2 0.7 all-gather.8.cloned.1.call-update
  8.0 0.7 all-gather.10.cloned.1.call-update
  8.8 25.6 %all-gather = bf16[1,128,2880]{1,2,0:T(8,128)(2,1)S(1)} all-gather(bf16[1,128,360]{1,2,0:T(8,128)(2,1)} %param.17), channel_id=2, replica_groups=mesh['expert'=16,'mp'=8,'batch'=2] {'mp'}, dimensions={2}, use_global_device_ids=true | all-gather | bytes 829440 | tf_op jit(solution)/shard_map/all_gather | solution.py:72
  34.4 0.4 fusion.35
  34.8 40.1 %all-gather.1 = bf16[16,180,64]{1,2,0:T(8,128)(2,1)S(1)} all-gather(bf16[1,180,64]{1,2,0:T(8,128)(2,1)} %bitcast.211), channel_id=1, replica_groups=mesh['expert'=16,'mp'=8,'batch'=2] {'expert'}, dimensions={0}, use_global_device_ids=true | all-gather | bytes 391680 | tf_op jit(solution)/shard_map/all_gather | solution.py:78
  74.9 1.1 copy.73
  76.0 1.8 reshape.396
  77.8 0.8 multiply_cosine_fusion
  78.5 0.6 convolution_bitcast_fusion.1
  79.1 0.1 fusion.70
  79.3 31.8 %all_gather.26 = bf16[2048,64]{0,1:T(8,128)(2,1)S(1)} all-gather(bf16[128,64]{0,1:T(8,128)(2,1)S(1)} %pad_maximum_fusion), channel_id=1, replica_groups=mesh['expert'=16,'mp'=8,'batch'=2] {'expert'}, dimensions={0}, use_global_device_ids=true | all-gather | bytes 278528 | tf_op jit(solution)/shard_map/all_gather | solution.py:101
  111.1 1.0 copy.79
  112.2 33.1 %all-gather.3 = bf16[16,180,64]{1,2,0:T(8,128)(2,1)S(1)} all-gather(bf16[1,180,64]{1,2,0:T(8,128)(2,1)} %bitcast.212), channel_id=1, replica_groups=mesh['expert'=16,'mp'=8,'batch'=2] {'expert'}, dimensions={0}, use_global_device_ids=true | all-gather | bytes 391680 | tf_op jit(solution)/shard_map/all_gather | solution.py:79
  145.3 1.1 copy.78
  146.4 1.8 reshape.400
  148.2 1.3 convolution_convert_fusion.2
  149.5 35.5 %all_gather.29 = bf16[2048,64]{0,1:T(8,128)(2,1)} all-gather(bf16[128,64]{0,1:T(8,128)(2,1)S(1)} %convolution_convert_fusion.2), channel_id=1, replica_groups=mesh['expert'=16,'mp'=8,'batch'=2] {'expert'}, dimensions={0}, use_global_device_ids=true | all-gather | bytes 278528 | tf_op jit(solution)/shard_map/all_gather | solution.py:102
  185.1 4.4 reshape.398
  189.5 3.5 fusion.80
  193.1 0.9 copy.96
  194.0 7.0 %while.30 = (s32[]{:T(128)}, f32[1,1024]{1,0:T(1,128)S(1)}, s32[2048]{0:T(1024)S(1)}, bf16[1,2048,64]{2,1,0:T(8,128)(2,1)}, bf16[1,1024,64]{2,1,0:T(8,128)(2,1)}...) while((s32[]{:T(128)}, f32[1,1024]{1,0:T(1,128)S(1)}, ...), condition=%wide.region_3.4_spmd.clone, body=%wide.region_1.3_spmd.clone.sunk | while | flops 70255112 | bytes 437415 | solution.py:137
  194.1 1.6 fusion.101
  195.8 1.6 fusion.101
  197.6 1.6 fusion.101
  199.3 1.6 fusion.101
  201.0 12.7 %while.31 = (s32[]{:T(128)}, f32[1,1024,64]{1,2,0:T(8,128)S(1)}, f32[1,1024]{1,0:T(1,128)S(1)}, s32[2048]{0:T(1024)S(1)}, bf16[1,2048,64]{2,1,0:T(8,128)(2,1)}, ...) while((s32[]{:T(128)}, f32[1,1024,64]{1,2,0:T(8,128)S(1)}, ...), condition=%wide.region_6.7_spmd.clone, body=%wide.region_4.6_spmd.clone.sunk | while | flops 139068928 | bytes 3128526 | solution.py:153
  201.1 1.9 convert_reduce_fusion.2
  202.9 1.2 fusion.104
  204.2 1.9 convert_reduce_fusion.2
  206.1 1.2 fusion.104
  207.4 1.9 convert_reduce_fusion.2
  209.3 1.2 fusion.104
  210.6 1.9 convert_reduce_fusion.2
  212.4 1.2 fusion.104
  213.8 4.3 reshape.402
  218.1 3.7 convolution_convert_fusion.1
  222.4 1.2 reduce-window.6
  223.5 0.2 slice_reduce_fusion
  224.2 2.4 scatter_custom_fusion
  226.6 58.4 %reduce-scatter.10.cloned.1.call-done = bf16[128,360]{0,1:T(8,128)(2,1)} async-done(((bf16[128,2880]{0,1:T(8,128)(2,1)}), bf16[128,360]{0,1:T(8,128)(2,1)}) %reduce-scatter.10.cloned.1.call-update) | async-done | bytes 92176
  285.1 1.0 copy.83
  286.1 0.1 copy.84
  286.3 26.1 %all_gather.31 = bf16[128,2880]{0,1:T(8,128)(2,1)} all-gather(bf16[128,360]{0,1:T(8,128)(2,1)S(1)} %copy.84), channel_id=1, replica_groups=mesh['expert'=16,'mp'=8,'batch'=2] {'mp'}, dimensions={1}, use_global_device_ids=true | all-gather | bytes 829440 | tf_op jit(solution)/shard_map/all_gather | solution.py:185
  312.4 1.5 copy.85
  313.8 0.2 fusion.32
  314.1 0.2 fusion.34
  314.4 4.8 gather_fusion
  319.2 100.2 %all_to_all.10 = bf16[16,48,2880]{2,1,0:T(8,128)(2,1)S(1)} all-to-all(bf16[16,48,2880]{2,1,0:T(8,128)(2,1)} %bitcast.189), channel_id=1, replica_groups=mesh['expert'=16,'mp'=8,'batch'=2] {'expert'}, dimensions={0} | all-to-all | bytes 8847360 | tf_op jit(solution)/shard_map/all_to_all | solution.py:191
  419.4 3.5 fusion.38
  423.0 2.1 fusion.53
  425.0 0.3 copy.90
  425.3 4.1 convolution_convert_fusion
  429.5 14.6 %copy.94 = bf16[16,48,2880]{1,0,2:T(8,128)(2,1)} copy(bf16[16,48,2880]{2,1,0:T(8,128)(2,1)} %convolution_convert_fusion) | data formatting | bytes 8847360
  444.1 17.1 %reshape.409 = bf16[2880,768]{1,0:T(8,128)(2,1)} reshape(bf16[2880,16,48]{2,1,0:T(8,128)(2,1)} %bitcast.187) | data formatting | bytes 8847360
  461.2 64.7 %reduce-scatter.8.cloned.1.call-done = bf16[360,768]{1,0:T(8,128)(2,1)} async-done(((bf16[2880,768]{1,0:T(8,128)(2,1)}), bf16[360,768]{1,0:T(8,128)(2,1)}) %reduce-scatter.8.cloned.1.call-update) | async-done | bytes 552976
  525.9 3.6 reshape.410
  529.5 2.6 copy.95
  532.1 9.0 %all-to-all-start.1 = ((bf16[16,48,360]{2,1,0:T(8,128)(2,1)}), bf16[16,48,360]{2,1,0:T(8,128)(2,1)S(1)}, u32[]{:S(2)}, u32[]{:S(2)}) async-start(bf16[16,48,360]{2,1,0:T(8,128)(2,1)} %copy.95), calls=%async_computation.1 | async-start | bytes 1179648 | tf_op jit(solution)/shard_map/all_to_all | solution.py:204
  541.2 0.6 pad_maximum_fusion.1
  541.8 16.6 %all-to-all-done.1 = bf16[16,48,360]{2,1,0:T(8,128)(2,1)S(1)} async-done(((bf16[16,48,360]{2,1,0:T(8,128)(2,1)}), bf16[16,48,360]{2,1,0:T(8,128)(2,1)S(1)}, u32[]{:S(2)}, u32[]{:S(2)}) %all-to-all-start.1) | async-done | bytes 552992 | tf_op jit(solution)/shard_map/all_to_all | solution.py:204
  558.4 2.6 gather_fusion.1
  561.0 1.2 reshape.366
  562.2 0.5 multiply_reduce_fusion
  562.8 0.8 copy.92
  (110 shorter events, 2.4 us)
Async XLA Ops:
  7.2 418.2 %copy-start = (bf16[1,360,2880]{2,1,0:T(8,128)(2,1)S(1)}, bf16[1,360,2880]{2,1,0:T(8,128)(2,1)}, u32[]{:S(2)}) copy-start(bf16[1,360,2880]{2,1,0:T(8,128)(2,1)} %param.27) | copy-start | bytes 6220804
  7.2 177.9 %all-gather.8.cloned.1.call-start = ((), (), s32[]{:S(2)}) async-start(), calls=%async_computation.4 | async-start | bytes 3203072 | tf_op jit(solution)/shard_map/all_gather | solution.py:77
  7.9 205.9 %all-gather.10.cloned.1.call-start = ((), (), s32[]{:S(2)}) async-start(), calls=%async_computation.5 | async-start | bytes 3203072 | tf_op jit(solution)/shard_map/all_gather | solution.py:163
  8.7 69.9 %copy-start.10 = (f32[2880]{0:T(1024)S(1)}, f32[2880]{0:T(1024)}, u32[]{:S(2)}) copy-start(f32[2880]{0:T(1024)} %param.19) | copy-start | bytes 34564
  8.7 276.4 %reduce-scatter.10.cloned.1.call-start = ((), (), s32[]{:S(2)}) async-start(), calls=%async_computation.7 | async-start | bytes 829440
  34.8 43.7 %copy-start.12 = (f32[128]{0:T(128)}, f32[128]{0:T(128)S(1)}, u32[]{:S(2)}) copy-start(f32[128]{0:T(128)S(1)} %add_rsqrt_fusion.1) | copy-start | bytes 1540
  74.9 37.3 %copy-start.9 = (f32[8]{0:T(128)S(1)}, f32[8]{0:T(128)}, u32[]{:S(2)}) copy-start(f32[8]{0:T(128)} %param.24) | copy-start | bytes 100
  112.2 72.8 %copy-start.4 = (s32[1,2048]{1,0:T(1,128)S(1)}, s32[1,2048]{1,0:T(1,128)}, u32[]{:S(2)}) copy-start(s32[1,2048]{1,0:T(1,128)} %param.18) | copy-start | bytes 24580
  149.5 35.6 %copy-start.5 = (bf16[128,64]{0,1:T(8,128)(2,1)}, bf16[128,64]{0,1:T(8,128)(2,1)S(1)}, u32[]{:S(2)}) copy-start(bf16[128,64]{0,1:T(8,128)(2,1)S(1)} %convolution_convert_fusion.2) | copy-start | bytes 49156
  185.0 4.5 copy-start.11
  185.1 4.5 copy-start.13
  189.5 3.5 copy-start.2
  189.5 3.5 copy-start.3
  218.1 3.8 copy-start.1
  218.1 3.9 copy-start.7
  221.8 304.0 %reduce-scatter.8.cloned.1.call-start = ((), (), s32[]{:S(2)}) async-start(), calls=%async_computation.6 | async-start | bytes 4976640
  222.3 91.8 %copy-start.6 = (f32[2880]{0:T(1024)S(1)}, f32[2880]{0:T(1024)}, u32[]{:S(2)}) copy-start(f32[2880]{0:T(1024)} %param.25) | copy-start | bytes 34564
  319.2 103.7 %slice-start = ((s8[4239360]{0:T(1024)(128)(4,1)}), s8[4194304]{0:T(1024)(128)(4,1)S(1)}, s32[]{:S(2)}) async-start(s8[4239360]{0:T(1024)(128)(4,1)} %bitcast.219), calls=%async_computation.8 | async-start | bytes 8388608
  419.4 3.6 slice-start.1
  529.5 11.6 %copy-start.8 = (f32[1,128,4]{1,2,0:T(4,128)S(1)}, f32[1,128,4]{1,2,0:T(4,128)}, u32[]{:S(2)}) copy-start(f32[1,128,4]{1,2,0:T(4,128)} %param.29) | copy-start | bytes 6148
  532.1 26.4 %all-to-all-start.1 = ((bf16[16,48,360]{2,1,0:T(8,128)(2,1)}), bf16[16,48,360]{2,1,0:T(8,128)(2,1)S(1)}, u32[]{:S(2)}, u32[]{:S(2)}) async-start(bf16[16,48,360]{2,1,0:T(8,128)(2,1)} %copy.95), calls=%async_computation.1 | async-start | bytes 1179648 | tf_op jit(solution)/shard_map/all_to_all | solution.py:204
Sparse Core Ops, SparseCore 0:
  10.6 93.6 all-gather.7
  106.9 90.0 all-gather.9
  222.0 63.0 reduce-scatter.9
  461.3 64.5 reduce-scatter.7
where the time goes:
time: 572 us; the launch traced here: 570 us
  blocking collectives  292 us (51%)
  waiting for transfers between devices  141 us (25%)
  local copies, waits for them, and re-layouts  70.9 us (12%)
  matrix products  37.3 us (7%)
  between operations  14.2 us (2%)
  starting transfers between devices  9.14 us (2%)
    unnamed x6, waiting for transfers between devices  125 us
    all_to_all x1, blocking collectives, shards(): lax.all_to_all(outgoing, 'expert', split_axis=0, concat_axis=0, tiled=True)  100 us
    unnamed x47, local copies, waits for them, and re-layouts  53.2 us
    all_gather x1, blocking collectives, shards(): lax.all_gather(key_weight, 'expert', axis=0, tiled=True)  40.1 us
    all_gather x1, blocking collectives, shards(): lax.all_gather(value_fresh, 'expert', axis=0, tiled=True)  35.5 us
    all_gather x1, blocking collectives, shards(): lax.all_gather(value_weight, 'expert', axis=0, tiled=True)  33.1 us
    all_gather x1, blocking collectives, shards(): lax.all_gather(key_rotary, 'expert', axis=0, tiled=True)  31.8 us
    all_gather x1, blocking collectives, shards(): moe_whole = lax.all_gather(first_out, 'mp', axis=1, tiled=True)  26.1 us
  transfers between devices with their start and end apart: 5, of which 3 were waited for; matrix products, arithmetic and copies ran while one was open for 8% of the time, Pallas kernels for 0%

commit v1 on v0

--- a/solution.py
+++ b/solution.py
@@ -73,17 +73,14 @@
     input_normalised = rms_norm(whole_rows, attn_gain)
     query_cols = w_query.shape[1]
     kv_cols = key_weight.shape[1]
-    weight_parts = (
-        lax.all_gather(w_query, "expert", axis=0, tiled=True),
-        lax.all_gather(key_weight, "expert", axis=0, tiled=True),
-        lax.all_gather(value_weight, "expert", axis=0, tiled=True),
-    )
-    query_raw, key_raw, value_raw = tuple(
-        (
-            jnp.dot(input_normalised, weight_part, preferred_element_type=jnp.float32)
-            for weight_part in weight_parts
-        )
-    )
+    query_weight = lax.all_gather(w_query, "expert", axis=0, tiled=True)
+    kv_weight = lax.all_gather(
+        jnp.concatenate([key_weight, value_weight], axis=1), "expert", axis=0, tiled=True
+    )
+    query_raw = jnp.dot(input_normalised, query_weight, preferred_element_type=jnp.float32)
+    kv_raw = jnp.dot(input_normalised, kv_weight, preferred_element_type=jnp.float32)
+    key_raw = kv_raw[:, :kv_cols]
+    value_raw = kv_raw[:, kv_cols:]
     token_positions = row_start + jnp.arange(tok_count, dtype=jnp.int32)
     query_by_head = query_cols // HEAD_SIZE
     kv_heads = kv_cols // HEAD_SIZE
@@ -97,10 +94,11 @@
         .reshape(tok_count, kv_cols)
     )
     value_fresh = value_raw.astype(jnp.bfloat16)
-    keys_all, values_all = (
-        lax.all_gather(key_rotary, "expert", axis=0, tiled=True),
-        lax.all_gather(value_fresh, "expert", axis=0, tiled=True),
-    )
+    kv_all = lax.all_gather(
+        jnp.concatenate([key_rotary, value_fresh], axis=1), "expert", axis=0, tiled=True
+    )
+    keys_all = kv_all[:, :kv_cols]
+    values_all = kv_all[:, kv_cols:]
     seq_len = keys_all.shape[0]
     seg_all = segments[0]
     seg_local = lax.dynamic_slice_in_dim(seg_all, row_start, tok_count)
@@ -182,27 +180,30 @@
         .at[target]
         .set(jnp.arange(tok_count * top_count, dtype=jnp.int32) // top_count)
     )
-    moe_whole = lax.all_gather(first_out, "mp", axis=1, tiled=True)
-    moe_normed = rms_norm(moe_whole, moe_gain)
     padded = jnp.concatenate(
-        [moe_normed, jnp.zeros((1, moe_normed.shape[1]), jnp.bfloat16)], axis=0
+        [first_out, jnp.zeros((1, first_out.shape[1]), jnp.bfloat16)], axis=0
     )
     outgoing = padded[source_row].reshape(expert_count, capacity, padded.shape[1])
     arrived = lax.all_to_all(outgoing, "expert", split_axis=0, concat_axis=0, tiled=True)
-    model_width = arrived.shape[2]
-    grouped = arrived.reshape(expert_devs, local_experts, capacity, model_width)
-    inputs = grouped[:, 0].reshape(expert_devs * capacity, model_width)
-    partial_list = [
-        expert_rows(inputs, expert_in[0], expert_down[0]).reshape(
-            expert_devs, capacity, model_width
-        )
-    ]
-    partials = jnp.stack(partial_list, axis=1).reshape(expert_count, capacity, model_width)
-    expert_out = lax.psum_scatter(
-        partials.astype(jnp.bfloat16), "mp", scatter_dimension=2, tiled=True
-    )
+    arrived_rows = arrived.reshape(expert_count * capacity, arrived.shape[2])
+    inputs = rms_norm(lax.all_gather(arrived_rows, "mp", axis=1, tiled=True), moe_gain)
+    w_in = expert_in[0]
+    gate_val = jnp.dot(inputs, w_in[0], preferred_element_type=jnp.float32)
+    up_val = jnp.dot(inputs, w_in[1], preferred_element_type=jnp.float32)
+    gate_val = jnp.minimum(gate_val, clamp_limit)
+    up_val = jnp.clip(up_val, -clamp_limit, clamp_limit)
+    activated = ((up_val + 1.0) * gate_val * jax.nn.sigmoid(glu_alpha * gate_val)).astype(
+        jnp.bfloat16
+    )
+    partials_t = lax.dot_general(
+        expert_down[0], activated, (((0,), (1,)), ((), ())), preferred_element_type=jnp.float32
+    )
+    expert_out_t = lax.psum_scatter(
+        partials_t.astype(jnp.bfloat16), "mp", scatter_dimension=0, tiled=True
+    )
+    local_width = expert_out_t.shape[0]
+    expert_out = expert_out_t.T.reshape(expert_count, capacity, local_width)
     returned = lax.all_to_all(expert_out, "expert", split_axis=0, concat_axis=0, tiled=True)
-    local_width = returned.shape[2]
     picked = returned.reshape(expert_count * capacity, local_width)[target].reshape(
         tok_count, top_count, local_width
     )

time: 572 us -> 441 us (0.77)
  blocking collectives: 292 us -> 123 us
  waiting for transfers between devices: 141 us -> 212 us
  local copies, waits for them, and re-layouts: 70.9 us -> 31.3 us
    all_gather x5 -> x2, blocking collectives: 167 us -> 74.4 us  [the longest x1 41.8 us: shards(): lax.all_gather(jnp.concatenate([key_weight, value_weight], axis=1), 'expe...]
    unnamed x6, waiting for transfers between devices: 125 us -> 32.6 us
    all_to_all x1, blocking collectives: 100 us -> 23.3 us  [shards(): lax.all_to_all(outgoing, 'expert', split_axis=0, concat_axis=0, tiled=True)]
    reduce_scatter x0 -> x1, waiting for transfers between devices: none -> 57 us  [shards(): lax.psum_scatter(partials_t.astype(jnp.bfloat16), 'mp', scatter_dimension...]
    all_gather x1 -> x2, waiting for transfers between devices: 0.02 us -> 55.9 us  [the longest x1 55.9 us: shards(): lax.all_gather(arrived_rows, 'mp', axis=1, tiled=True)]
    all_gather x1, waiting for transfers between devices: 0.02 us -> 50.9 us  [shards(): lax.all_gather(w_out, 'expert', axis=1, tiled=True)]
    unnamed x47 -> x36, local copies, waits for them, and re-layouts: 53.2 us -> 16.3 us
    dot_general x6 -> x4, matrix products: 15.1 us -> 20.1 us  [the longest x1 10.6 us: shards(): lax.dot_general(expert_down[0], activated, (((0,), (1,)), ((), ())), pref...]
  transfers between devices with their start and end apart: 5 -> 6, of which waited for: 3 -> 5; matrix products, arithmetic and copies ran while one was open for 8% -> 10% of each run, Pallas kernels for 0% -> 0%
where the time goes in v1:
time: 441 us; the launch traced here: 439 us
  waiting for transfers between devices  212 us (48%)
  blocking collectives  123 us (28%)
  matrix products  42.4 us (10%)
  local copies, waits for them, and re-layouts  31.3 us (7%)
  between operations  14.1 us (3%)
  starting transfers between devices  9.37 us (2%)
  other arithmetic  6.94 us (2%)
    reduce_scatter x1, waiting for transfers between devices, shards(): lax.psum_scatter(partials_t.astype(jnp.bfloat16), 'mp', scatter_dimension...  57 us
    all_gather x1, waiting for transfers between devices, shards(): lax.all_gather(arrived_rows, 'mp', axis=1, tiled=True)  55.9 us
    all_gather x1, waiting for transfers between devices, shards(): lax.all_gather(w_out, 'expert', axis=1, tiled=True)  50.9 us
    all_gather x1, blocking collectives, shards(): lax.all_gather(jnp.concatenate([key_weight, value_weight], axis=1), 'expe...  41.8 us
    unnamed x6, waiting for transfers between devices  32.6 us
    all_gather x1, blocking collectives, shards(): lax.all_gather(jnp.concatenate([key_rotary, value_fresh], axis=1), 'exper...  32.5 us
    all_gather x1, blocking collectives, shards(): whole_rows = lax.all_gather(local_rows, 'mp', axis=1, tiled=True)  25.6 us
    all_to_all x1, blocking collectives, shards(): lax.all_to_all(outgoing, 'expert', split_axis=0, concat_axis=0, tiled=True)  23.3 us
  transfers between devices with their start and end apart: 6, of which 5 were waited for; matrix products, arithmetic and copies ran while one was open for 10% of the time, Pallas kernels for 0%

profile of v1, /device:TPU:1, one launch (start us, length us, event | category | flops | bytes accessed | tf_op | source)
XLA Modules:
  0.0 439.3 jit_solution(6514722214666441257)
XLA Ops:
  7.2 0.7 all-gather.10.cloned.1.call-update
  8.0 0.7 all-gather.12.cloned.1.call-update
  8.7 25.6 %all-gather = bf16[1,128,2880]{1,2,0:T(8,128)(2,1)S(1)} all-gather(bf16[1,128,360]{1,2,0:T(8,128)(2,1)} %param.17), channel_id=2, replica_groups=mesh['expert'=16,'mp'=8,'batch'=2] {'mp'}, dimensions={2}, use_global_device_ids=true | all-gather | bytes 829440 | tf_op jit(solution)/shard_map/all_gather | solution.py:72
  34.4 0.9 copy-done.2
  35.3 0.4 fusion.36
  35.7 0.9 copy.72
  36.6 0.9 copy.73
  37.5 41.8 %all-gather.1 = bf16[16,180,128]{2,1,0:T(8,128)(2,1)S(1)} all-gather(bf16[1,180,128]{2,1,0:T(8,128)(2,1)S(1)} %maximum_bitcast_fusion.1), channel_id=1, replica_groups=mesh['expert'=16,'mp'=8,'batch'=2] {'expert'}, dimensions={0}, use_global_device_ids=true | all-gather | bytes 783360 | tf_op jit(solution)/shard_map/all_gather | solution.py:77
  79.3 1.0 reshape.403
  80.4 2.2 fusion.69
  82.6 0.6 copy-done.5
  83.3 0.1 multiply_cosine_fusion
  83.4 0.1 fusion.85
  83.6 32.5 %all_gather.20 = bf16[2048,128]{0,1:T(8,128)(2,1)S(1)} all-gather(bf16[128,128]{0,1:T(8,128)(2,1)S(1)} %pad_maximum_fusion), channel_id=1, replica_groups=mesh['expert'=16,'mp'=8,'batch'=2] {'expert'}, dimensions={0}, use_global_device_ids=true | all-gather | bytes 557056 | tf_op jit(solution)/shard_map/all_gather | solution.py:97
  116.1 0.7 slice_bitcast_fusion
  116.8 1.0 copy.78
  118.0 4.5 %reshape.405 = bf16[2880,512]{1,0:T(8,128)(2,1)} reshape(bf16[16,180,512]{2,1,0:T(8,128)(2,1)} %all-gather.10.cloned.1.call-done) | data formatting | bytes 5898240
  122.4 3.5 fusion.67
  126.0 0.9 copy.92
  126.8 7.0 %while.30 = (s32[]{:T(128)}, f32[1,1024]{1,0:T(1,128)S(1)}, s32[2048]{0:T(1024)S(1)}, bf16[1,2048,64]{2,1,0:T(8,128)(2,1)}, bf16[1,1024,64]{2,1,0:T(8,128)(2,1)}...) while((s32[]{:T(128)}, f32[1,1024]{1,0:T(1,128)S(1)}, ...), condition=%wide.region_3.4_spmd.clone, body=%wide.region_1.3_spmd.clone.sunk | while | flops 70255112 | bytes 437415 | solution.py:135
  126.9 1.6 fusion.112
  128.7 1.6 fusion.112
  130.4 1.6 fusion.112
  132.2 1.6 fusion.112
  133.8 12.7 %while.31 = (s32[]{:T(128)}, f32[1,1024,64]{1,2,0:T(8,128)S(1)}, f32[1,1024]{1,0:T(1,128)S(1)}, s32[2048]{0:T(1024)S(1)}, bf16[1,2048,64]{2,1,0:T(8,128)(2,1)}, ...) while((s32[]{:T(128)}, f32[1,1024,64]{1,2,0:T(8,128)S(1)}, ...), condition=%wide.region_6.7_spmd.clone, body=%wide.region_4.6_spmd.clone.sunk | while | flops 139068928 | bytes 3128526 | solution.py:151
  133.9 1.9 convert_reduce_fusion.2
  135.8 1.2 fusion.115
  137.1 1.9 convert_reduce_fusion.2
  139.0 1.2 fusion.115
  140.3 1.9 convert_reduce_fusion.2
  142.1 1.2 fusion.115
  143.4 1.9 convert_reduce_fusion.2
  145.3 1.2 fusion.115
  146.6 50.9 %all-gather.12.cloned.1.call-done = bf16[16,180,512]{2,1,0:T(8,128)(2,1)} async-done(((bf16[1,180,512]{2,1,0:T(8,128)(2,1)}), bf16[16,180,512]{2,1,0:T(8,128)(2,1)}) %all-gather.12.cloned.1.call-update) | async-done | bytes 2949136 | tf_op jit(solution)/shard_map/all_gather | solution.py:161
  197.5 4.3 reshape.407
  201.8 3.7 convolution_convert_fusion.1
  205.6 0.1 copy.71
  205.7 0.1 copy.84
  206.1 1.2 reduce-window.6
  207.2 0.2 slice_reduce_fusion
  207.5 0.1 copy.83
  207.8 2.4 scatter_custom_fusion
  210.3 31.2 %reduce-scatter.8.cloned.1.call-done = bf16[128,360]{0,1:T(8,128)(2,1)} async-done(((bf16[128,2880]{0,1:T(8,128)(2,1)}), bf16[128,360]{0,1:T(8,128)(2,1)}) %reduce-scatter.8.cloned.1.call-update) | async-done | bytes 92176
  241.5 1.0 copy.82
  242.6 2.6 gather_fusion
  245.2 23.3 %all_to_all.10 = bf16[16,48,360]{2,1,0:T(8,128)(2,1)S(1)} all-to-all(bf16[16,48,360]{2,1,0:T(8,128)(2,1)S(1)} %bitcast.184), channel_id=1, replica_groups=mesh['expert'=16,'mp'=8,'batch'=2] {'expert'}, dimensions={0} | all-to-all | bytes 1105920 | tf_op jit(solution)/shard_map/all_to_all | solution.py:187
  268.5 1.1 copy.87
  269.6 0.2 reduce-scatter.6.cloned.1.call-start
  269.9 55.9 %all-gather.8.cloned.1.call-done = bf16[768,2880]{0,1:T(8,128)(2,1)} async-done(((bf16[768,360]{0,1:T(8,128)(2,1)}), bf16[768,2880]{0,1:T(8,128)(2,1)}) %all-gather.8.cloned.1.call-update) | async-done | bytes 4423696 | tf_op jit(solution)/shard_map/all_gather | solution.py:189
  325.7 3.3 fusion.25
  329.1 0.2 copy-done.1
  329.3 3.9 fusion.39
  333.2 10.6 %fusion.28 = bf16[2880,768]{1,0:T(8,128)(2,1)} fusion(bf16[1,360,2880]{2,1,0:T(8,128)(2,1)S(1)} %copy-done, f32[768,360]{0,1:T(8,128)S(1)} %fusion.39, bf16[1,2,2880,360]{2,3,1,0:T(8,128)(2,1)} %param.26, bf16[768,2880]{0,1:T(8,128)(2,1)} %all-gather.8.cloned.1.call-done, f32[2880]{0:T(1024)S(1)} %copy-done.11, f32[768]{0:T(1024)S(1)} %add_rsqrt_fusion), kind=kOutput, calls=%fused_computation.41 | convolution fusion | flops 3198597120 | bytes 14161152 | tf_op jit(solution)/shard_map/dot_general | solution.py:198
  343.8 57.0 %reduce-scatter.6.cloned.1.call-done = bf16[360,768]{1,0:T(8,128)(2,1)} async-done(((bf16[2880,768]{1,0:T(8,128)(2,1)}), bf16[360,768]{1,0:T(8,128)(2,1)}) %reduce-scatter.6.cloned.1.call-update) | async-done | bytes 552976 | tf_op jit(solution)/shard_map/reduce_scatter | solution.py:201
  400.9 2.1 copy.88
  403.0 9.0 %all-to-all-start.1 = ((bf16[16,48,360]{2,1,0:T(8,128)(2,1)}), bf16[16,48,360]{2,1,0:T(8,128)(2,1)S(1)}, u32[]{:S(2)}, u32[]{:S(2)}) async-start(bf16[16,48,360]{2,1,0:T(8,128)(2,1)} %bitcast.32), calls=%async_computation.2 | async-start | bytes 1179648 | tf_op jit(solution)/shard_map/all_to_all | solution.py:206
  412.0 0.1 copy.89
  412.1 0.6 pad_maximum_fusion.1
  412.7 1.4 slice_bitcast_fusion.3
  414.1 15.3 %all-to-all-done.1 = bf16[16,48,360]{2,1,0:T(8,128)(2,1)S(1)} async-done(((bf16[16,48,360]{2,1,0:T(8,128)(2,1)}), bf16[16,48,360]{2,1,0:T(8,128)(2,1)S(1)}, u32[]{:S(2)}, u32[]{:S(2)}) %all-to-all-start.1) | async-done | bytes 552992 | tf_op jit(solution)/shard_map/all_to_all | solution.py:206
  429.3 1.9 gather_fusion.1
  431.3 0.2 reshape.373
  431.5 0.5 multiply_reduce_fusion
  432.1 0.8 copy.90
  (97 shorter events, 2.0 us)
Async XLA Ops:
  7.2 326.0 %copy-start = (bf16[1,360,2880]{2,1,0:T(8,128)(2,1)S(1)}, bf16[1,360,2880]{2,1,0:T(8,128)(2,1)}, u32[]{:S(2)}) copy-start(bf16[1,360,2880]{2,1,0:T(8,128)(2,1)} %param.27) | copy-start | bytes 6220804
  7.2 110.8 %all-gather.10.cloned.1.call-start = ((), (), s32[]{:S(2)}) async-start(), calls=%async_computation.6 | async-start | bytes 3203072 | tf_op jit(solution)/shard_map/all_gather | solution.py:76
  7.9 189.6 %all-gather.12.cloned.1.call-start = ((), (), s32[]{:S(2)}) async-start(), calls=%async_computation.7 | async-start | bytes 3203072 | tf_op jit(solution)/shard_map/all_gather | solution.py:161
  8.7 71.7 %copy-start.10 = (f32[2880]{0:T(1024)S(1)}, f32[2880]{0:T(1024)}, u32[]{:S(2)}) copy-start(f32[2880]{0:T(1024)} %param.19) | copy-start | bytes 34564
  8.7 232.9 %reduce-scatter.8.cloned.1.call-start = ((), (), s32[]{:S(2)}) async-start(), calls=%async_computation.8 | async-start | bytes 829440
  34.4 0.9 copy-start.2
  80.4 37.5 %copy-start.9 = (f32[8]{0:T(128)S(1)}, f32[8]{0:T(128)}, u32[]{:S(2)}) copy-start(f32[8]{0:T(128)} %param.24) | copy-start | bytes 100
  80.4 37.6 %copy-start.6 = (s32[1,2048]{1,0:T(1,128)S(1)}, s32[1,2048]{1,0:T(1,128)}, u32[]{:S(2)}) copy-start(s32[1,2048]{1,0:T(1,128)} %param.18) | copy-start | bytes 24580
  82.6 0.6 copy-start.5
  117.9 4.5 %copy-start.3 = (bf16[1,128,2880]{1,2,0:T(8,128)(2,1)S(1)}, bf16[1,128,2880]{1,2,0:T(8,128)(2,1)}, u32[]{:S(2)}) copy-start(bf16[1,128,2880]{1,2,0:T(8,128)(2,1)} %copy-done.2) | copy-start | bytes 2211844
  201.8 3.8 copy-start.4
  201.8 3.9 copy-start.7
  205.5 120.2 %all-gather.8.cloned.1.call-start = ((), (), s32[]{:S(2)}) async-start(), calls=%async_computation.4 | async-start | bytes 4976640 | tf_op jit(solution)/shard_map/all_gather | solution.py:189
  269.6 59.5 %copy-start.11 = (f32[2880]{0:T(1024)S(1)}, f32[2880]{0:T(1024)}, u32[]{:S(2)}) copy-start(f32[2880]{0:T(1024)} %param.25) | copy-start | bytes 34564
  269.6 131.2 %reduce-scatter.6.cloned.1.call-start = ((), (), s32[]{:S(2)}) async-start(), calls=%async_computation.5 | async-start | bytes 4976640 | tf_op jit(solution)/shard_map/reduce_scatter | solution.py:201
  325.7 3.6 copy-start.1
  343.8 68.2 %copy-start.8 = (f32[1,128,4]{1,2,0:T(4,128)S(1)}, f32[1,128,4]{1,2,0:T(4,128)}, u32[]{:S(2)}) copy-start(f32[1,128,4]{1,2,0:T(4,128)} %param.29) | copy-start | bytes 6148
  403.0 26.4 %all-to-all-start.1 = ((bf16[16,48,360]{2,1,0:T(8,128)(2,1)}), bf16[16,48,360]{2,1,0:T(8,128)(2,1)S(1)}, u32[]{:S(2)}, u32[]{:S(2)}) async-start(bf16[16,48,360]{2,1,0:T(8,128)(2,1)} %bitcast.32), calls=%async_computation.2 | async-start | bytes 1179648 | tf_op jit(solution)/shard_map/all_to_all | solution.py:206
Sparse Core Ops, SparseCore 0:
  10.6 95.6 all-gather.9
  108.9 88.5 all-gather.11
  205.7 35.8 reduce-scatter.7
  269.7 55.9 all-gather.7
  343.9 56.8 reduce-scatter.5

commit v2 on v1

--- a/solution.py
+++ b/solution.py
@@ -37,6 +37,10 @@
         ],
         axis=-1,
     )
+
+
+def swap_cores(block):
+    return lax.ppermute(block, "batch", perm=[(0, 1), (1, 0)])
 
 
 def expert_rows(row_block, w_in, w_down):
@@ -73,14 +77,28 @@
     input_normalised = rms_norm(whole_rows, attn_gain)
     query_cols = w_query.shape[1]
     kv_cols = key_weight.shape[1]
-    query_weight = lax.all_gather(w_query, "expert", axis=0, tiled=True)
-    kv_weight = lax.all_gather(
-        jnp.concatenate([key_weight, value_weight], axis=1), "expert", axis=0, tiled=True
-    )
-    query_raw = jnp.dot(input_normalised, query_weight, preferred_element_type=jnp.float32)
-    kv_raw = jnp.dot(input_normalised, kv_weight, preferred_element_type=jnp.float32)
-    key_raw = kv_raw[:, :kv_cols]
-    value_raw = kv_raw[:, kv_cols:]
+    core = lax.axis_index("batch")
+    first_core = core == 0
+    half_q = query_cols // 2
+    query_mine = lax.all_gather(
+        lax.dynamic_slice_in_dim(w_query, core * half_q, half_q, 1), "expert", axis=0, tiled=True
+    )
+    query_other = swap_cores(query_mine)
+    kv_mine = lax.all_gather(
+        jnp.where(first_core, key_weight, value_weight), "expert", axis=0, tiled=True
+    )
+    kv_other = swap_cores(kv_mine)
+    q_mine = jnp.dot(input_normalised, query_mine, preferred_element_type=jnp.float32)
+    q_other = jnp.dot(input_normalised, query_other, preferred_element_type=jnp.float32)
+    query_raw = jnp.where(
+        first_core,
+        jnp.concatenate([q_mine, q_other], axis=1),
+        jnp.concatenate([q_other, q_mine], axis=1),
+    )
+    kv_mine_raw = jnp.dot(input_normalised, kv_mine, preferred_element_type=jnp.float32)
+    kv_other_raw = jnp.dot(input_normalised, kv_other, preferred_element_type=jnp.float32)
+    key_raw = jnp.where(first_core, kv_mine_raw, kv_other_raw)
+    value_raw = jnp.where(first_core, kv_other_raw, kv_mine_raw)
     token_positions = row_start + jnp.arange(tok_count, dtype=jnp.int32)
     query_by_head = query_cols // HEAD_SIZE
     kv_heads = kv_cols // HEAD_SIZE
@@ -156,10 +174,15 @@
         .transpose(2, 0, 1, 3)
         .reshape(tok_count, query_cols)
     )
-    out_terms = jnp.dot(
-        mixed,
-        lax.all_gather(w_out, "expert", axis=1, tiled=True),
-        preferred_element_type=jnp.float32,
+    half_o = w_out.shape[0] // 2
+    out_mine = lax.all_gather(
+        lax.dynamic_slice_in_dim(w_out, core * half_o, half_o, 0), "expert", axis=1, tiled=True
+    )
+    out_other = swap_cores(out_mine)
+    mixed_mine = lax.dynamic_slice_in_dim(mixed, core * half_o, half_o, 1)
+    mixed_other = lax.dynamic_slice_in_dim(mixed, (1 - core) * half_o, half_o, 1)
+    out_terms = jnp.dot(mixed_mine, out_mine, preferred_element_type=jnp.float32) + jnp.dot(
+        mixed_other, out_other, preferred_element_type=jnp.float32
     )
     attn_part = lax.psum_scatter(
         out_terms.astype(jnp.bfloat16), "mp", scatter_dimension=1, tiled=True

time: 441 us -> 446 us (1.011)
  starting transfers between devices: 9.37 us -> 25.4 us
  waiting for transfers between devices: 212 us -> 200 us
    ppermute x0 -> x3, starting transfers between devices: none -> 16.1 us  [swap_cores(): return lax.ppermute(block, 'batch', perm=[(0, 1), (1, 0)])]
    all_gather x2, waiting for transfers between devices: 50.9 us -> 42.8 us  [the longest x1 38 us: shards(): lax.all_gather(lax.dynamic_slice_in_dim(w_out, core * half_o, half_o, 0),...]
    unnamed x6, waiting for transfers between devices: 32.6 us -> 27.3 us
    dot_general x3 -> x6, matrix products: 9.36 us -> 12.5 us  [the longest x1 2.83 us: shards(): jnp.dot(mixed_other, out_other, preferred_element_type=jnp.float32)]
    unnamed x36 -> x54, local copies, waits for them, and re-layouts: 16.3 us -> 14 us
  transfers between devices with their start and end apart: 6 -> 9, of which waited for: 5 -> 6; matrix products, arithmetic and copies ran while one was open for 10% -> 11% of each run, Pallas kernels for 0% -> 0%
where the time goes in v2:
time: 446 us; the launch traced here: 445 us
  waiting for transfers between devices  200 us (45%)
  blocking collectives  123 us (28%)
  matrix products  45.5 us (10%)
  local copies, waits for them, and re-layouts  28.6 us (6%)
  starting transfers between devices  25.4 us (6%)
  between operations  14.3 us (3%)
  other arithmetic  8.23 us (2%)
    reduce_scatter x1, waiting for transfers between devices, shards(): lax.psum_scatter(partials_t.astype(jnp.bfloat16), 'mp', scatter_dimension...  57 us
    all_gather x1, waiting for transfers between devices, shards(): lax.all_gather(arrived_rows, 'mp', axis=1, tiled=True)  56 us
    all_gather x1, blocking collectives, shards(): lax.all_gather(jnp.where(first_core, key_weight, value_weight), 'expert',...  41.5 us
    all_gather x1, waiting for transfers between devices, shards(): lax.all_gather(lax.dynamic_slice_in_dim(w_out, core * half_o, half_o, 0),...  38 us
    all_gather x1, blocking collectives, shards(): lax.all_gather(jnp.concatenate([key_rotary, value_fresh], axis=1), 'exper...  33 us
    unnamed x6, waiting for transfers between devices  27.3 us
    all_gather x1, blocking collectives, shards(): whole_rows = lax.all_gather(local_rows, 'mp', axis=1, tiled=True)  24.8 us
    all_to_all x1, blocking collectives, shards(): lax.all_to_all(outgoing, 'expert', split_axis=0, concat_axis=0, tiled=True)  23.3 us
  transfers between devices with their start and end apart: 9, of which 6 were waited for; matrix products, arithmetic and copies ran while one was open for 11% of the time, Pallas kernels for 0%

profile of v2, /device:TPU:1, one launch (start us, length us, event | category | flops | bytes accessed | tf_op | source)
XLA Modules:
  0.0 444.8 jit_solution(10618321587649907036)
XLA Ops:
  7.2 1.7 dynamic-slice_bitcast_fusion.1
  9.0 0.8 select_bitcast_fusion.1
  9.8 41.5 %all-gather.1 = bf16[16,180,64]{1,2,0:T(8,128)(2,1)S(1)} all-gather(bf16[1,180,64]{1,2,0:T(8,128)(2,1)S(1)} %select_bitcast_fusion.1), channel_id=1, replica_groups=mesh['expert'=16,'mp'=8,'batch'=2] {'expert'}, dimensions={0}, use_global_device_ids=true | all-gather | bytes 391680 | tf_op jit(solution)/shard_map/all_gather | solution.py:87
  51.3 0.3 copy.74
  51.6 0.7 reshape.404
  52.3 7.5 %collective-permute-start = (bf16[2880,64]{0,1:T(8,128)(2,1)S(1)}, bf16[2880,64]{0,1:T(8,128)(2,1)}, u32[]{:S(2)}, u32[]{:S(2)}) collective-permute-start(bf16[2880,64]{0,1:T(8,128)(2,1)S(1)} %reshape.404), channel_id=1, source_target_pairs={{0,1},{1,0},{2,3},{3,2},{4,5},{5,4},{6,7},{7,6},{8,9},{9,8},{10,11... | collective-permute-start | bytes 1105928 | tf_op jit(solution)/shard_map/ppermute | solution.py:43
  59.8 0.6 dynamic-slice_bitcast_fusion
  60.5 24.8 %all-gather = bf16[1,128,2880]{1,2,0:T(8,128)(2,1)S(1)} all-gather(bf16[1,128,360]{1,2,0:T(8,128)(2,1)} %param.17), channel_id=2, replica_groups=mesh['expert'=16,'mp'=8,'batch'=2] {'mp'}, dimensions={2}, use_global_device_ids=true | all-gather | bytes 829440 | tf_op jit(solution)/shard_map/all_gather | solution.py:76
  85.3 0.4 fusion.37
  85.7 0.6 add_rsqrt_fusion.1
  86.5 0.7 broadcast_in_dim.74
  87.2 0.6 copy-done.5
  87.8 1.4 fusion.105
  89.2 0.6 copy-done.7
  89.8 1.6 select_convert_fusion
  91.5 4.8 %all-gather.10.cloned.1.call-done = bf16[16,180,256]{2,1,0:T(8,128)(2,1)} async-done(((bf16[1,180,256]{2,1,0:T(8,128)(2,1)}), bf16[16,180,256]{2,1,0:T(8,128)(2,1)}) %all-gather.10.cloned.1.call-update) | async-done | bytes 1474576 | tf_op jit(solution)/shard_map/all_gather | solution.py:83
  96.3 3.3 reshape.406
  99.6 4.5 %collective-permute-start.1 = (bf16[2880,256]{1,0:T(8,128)(2,1)}, bf16[2880,256]{1,0:T(8,128)(2,1)}, u32[]{:S(2)}, u32[]{:S(2)}) collective-permute-start(bf16[2880,256]{1,0:T(8,128)(2,1)} %reshape.406), channel_id=1, source_target_pairs={{0,1},{1,0},{2,3},{3,2},{4,5},{5,4},{6,7},{7,6},{8,9},{9,8},{10,11... | collective-permute-start | bytes 4423688 | tf_op jit(solution)/shard_map/ppermute | solution.py:43
  104.3 33.0 %all_gather.20 = bf16[2048,128]{0,1:T(8,128)(2,1)S(1)} all-gather(bf16[128,128]{0,1:T(8,128)(2,1)S(1)} %pad_maximum_fusion), channel_id=1, replica_groups=mesh['expert'=16,'mp'=8,'batch'=2] {'expert'}, dimensions={0}, use_global_device_ids=true | all-gather | bytes 557056 | tf_op jit(solution)/shard_map/all_gather | solution.py:115
  137.3 0.7 slice_bitcast_fusion
  138.1 1.0 copy.80
  139.1 38.0 %all-gather.12.cloned.1.call-done = bf16[16,180,256]{2,1,0:T(8,128)(2,1)} async-done(((bf16[1,180,256]{2,1,0:T(8,128)(2,1)}), bf16[16,180,256]{2,1,0:T(8,128)(2,1)}) %all-gather.12.cloned.1.call-update) | async-done | bytes 1474576 | tf_op jit(solution)/shard_map/all_gather | solution.py:178
  177.1 3.3 reshape.408
  180.4 4.0 collective-permute-start.2
  184.4 2.4 fusion.103
  186.8 2.4 fusion.101
  189.3 0.8 copy.95
  190.2 7.0 %while.30 = (s32[]{:T(128)}, f32[1,1024]{1,0:T(1,128)S(1)}, s32[2048]{0:T(1024)S(1)}, bf16[1,2048,64]{2,1,0:T(8,128)(2,1)}, bf16[1,1024,64]{2,1,0:T(8,128)(2,1)}...) while((s32[]{:T(128)}, f32[1,1024]{1,0:T(1,128)S(1)}, ...), condition=%wide.region_3.4_spmd.clone, body=%wide.region_1.3_spmd.clone.sunk | while | flops 70255112 | bytes 437415 | solution.py:153
  190.3 1.6 fusion.125
  192.0 1.6 fusion.125
  193.8 1.6 fusion.125
  195.5 1.6 fusion.125
  197.2 12.6 %while.31 = (s32[]{:T(128)}, f32[1,1024,64]{1,2,0:T(8,128)S(1)}, f32[1,1024]{1,0:T(1,128)S(1)}, s32[2048]{0:T(1024)S(1)}, bf16[1,2048,64]{2,1,0:T(8,128)(2,1)}, ...) while((s32[]{:T(128)}, f32[1,1024,64]{1,2,0:T(8,128)S(1)}, ...), condition=%wide.region_6.7_spmd.clone, body=%wide.region_4.6_spmd.clone.sunk | while | flops 139068928 | bytes 3128526 | solution.py:169
  197.3 1.9 convert_reduce_fusion.2
  199.1 1.2 fusion.128
  200.4 1.9 convert_reduce_fusion.2
  202.3 1.2 fusion.128
  203.6 1.9 convert_reduce_fusion.2
  205.5 1.2 fusion.128
  206.8 1.9 convert_reduce_fusion.2
  208.6 1.2 fusion.128
  209.9 1.9 fusion.74
  211.9 2.8 fusion.29
  214.8 0.2 all-gather.8.cloned.1.call-start
  215.5 1.2 reduce-window.6
  216.6 0.2 slice_reduce_fusion
  217.2 2.4 scatter_custom_fusion
  219.7 27.2 %reduce-scatter.8.cloned.1.call-done = bf16[128,360]{0,1:T(8,128)(2,1)} async-done(((bf16[128,2880]{0,1:T(8,128)(2,1)}), bf16[128,360]{0,1:T(8,128)(2,1)}) %reduce-scatter.8.cloned.1.call-update) | async-done | bytes 92176
  246.9 1.0 copy.84
  248.0 2.6 gather_fusion
  250.6 23.3 %all_to_all.10 = bf16[16,48,360]{2,1,0:T(8,128)(2,1)S(1)} all-to-all(bf16[16,48,360]{2,1,0:T(8,128)(2,1)S(1)} %bitcast.196), channel_id=1, replica_groups=mesh['expert'=16,'mp'=8,'batch'=2] {'expert'}, dimensions={0} | all-to-all | bytes 1105920 | tf_op jit(solution)/shard_map/all_to_all | solution.py:210
  273.9 1.1 copy.89
  275.1 56.0 %all-gather.8.cloned.1.call-done = bf16[768,2880]{0,1:T(8,128)(2,1)} async-done(((bf16[768,360]{0,1:T(8,128)(2,1)}), bf16[768,2880]{0,1:T(8,128)(2,1)}) %all-gather.8.cloned.1.call-update) | async-done | bytes 4423696 | tf_op jit(solution)/shard_map/all_gather | solution.py:212
  331.2 3.3 fusion.25
  334.7 3.9 fusion.40
  338.6 10.6 %fusion.28 = bf16[2880,768]{1,0:T(8,128)(2,1)} fusion(bf16[1,360,2880]{2,1,0:T(8,128)(2,1)S(1)} %copy-done, f32[768,360]{0,1:T(8,128)S(1)} %fusion.40, bf16[1,2,2880,360]{2,3,1,0:T(8,128)(2,1)} %param.26, bf16[768,2880]{0,1:T(8,128)(2,1)} %all-gather.8.cloned.1.call-done, f32[2880]{0:T(1024)S(1)} %copy-done.18, f32[768]{0:T(1024)S(1)} %add_rsqrt_fusion), kind=kOutput, calls=%fused_computation.41 | convolution fusion | flops 3198597120 | bytes 14161152 | tf_op jit(solution)/shard_map/dot_general | solution.py:221
  349.3 57.0 %reduce-scatter.6.cloned.1.call-done = bf16[360,768]{1,0:T(8,128)(2,1)} async-done(((bf16[2880,768]{1,0:T(8,128)(2,1)}), bf16[360,768]{1,0:T(8,128)(2,1)}) %reduce-scatter.6.cloned.1.call-update) | async-done | bytes 552976 | tf_op jit(solution)/shard_map/reduce_scatter | solution.py:224
  406.3 2.1 copy.90
  408.4 9.0 %all-to-all-start.1 = ((bf16[16,48,360]{2,1,0:T(8,128)(2,1)}), bf16[16,48,360]{2,1,0:T(8,128)(2,1)S(1)}, u32[]{:S(2)}, u32[]{:S(2)}) async-start(bf16[16,48,360]{2,1,0:T(8,128)(2,1)} %bitcast.34), calls=%async_computation.2 | async-start | bytes 1179648 | tf_op jit(solution)/shard_map/all_to_all | solution.py:229
  417.5 0.6 pad_maximum_fusion.1
  418.1 16.6 %all-to-all-done.1 = bf16[16,48,360]{2,1,0:T(8,128)(2,1)S(1)} async-done(((bf16[16,48,360]{2,1,0:T(8,128)(2,1)}), bf16[16,48,360]{2,1,0:T(8,128)(2,1)S(1)}, u32[]{:S(2)}, u32[]{:S(2)}) %all-to-all-start.1) | async-done | bytes 552992 | tf_op jit(solution)/shard_map/all_to_all | solution.py:229
  434.8 1.9 gather_fusion.1
  436.9 0.5 multiply_reduce_fusion
  437.5 0.8 copy.92
  (124 shorter events, 3.1 us)
Async XLA Ops:
  7.2 331.5 %copy-start = (bf16[1,360,2880]{2,1,0:T(8,128)(2,1)S(1)}, bf16[1,360,2880]{2,1,0:T(8,128)(2,1)}, u32[]{:S(2)}) copy-start(bf16[1,360,2880]{2,1,0:T(8,128)(2,1)} %param.27) | copy-start | bytes 6220804
  7.2 52.6 %copy-start.4 = (bf16[512,180]{0,1:T(8,128)(2,1)S(1)}, bf16[512,180]{0,1:T(8,128)(2,1)}, u32[]{:S(2)}) copy-start(bf16[512,180]{0,1:T(8,128)(2,1)} %param.23) | copy-start | bytes 552964
  7.2 89.1 %all-gather.10.cloned.1.call-start = ((), (), s32[]{:S(2)}) async-start(), calls=%async_computation.6 | async-start | bytes 1601536 | tf_op jit(solution)/shard_map/all_gather | solution.py:83
  9.0 168.1 %all-gather.12.cloned.1.call-start = ((), (), s32[]{:S(2)}) async-start(), calls=%async_computation.7 | async-start | bytes 1601536 | tf_op jit(solution)/shard_map/all_gather | solution.py:178
  51.6 36.3 %copy-start.3 = (s32[1,2048]{1,0:T(1,128)S(1)}, s32[1,2048]{1,0:T(1,128)}, u32[]{:S(2)}) copy-start(s32[1,2048]{1,0:T(1,128)} %param.18) | copy-start | bytes 24580
  52.3 36.9 %collective-permute-start = (bf16[2880,64]{0,1:T(8,128)(2,1)S(1)}, bf16[2880,64]{0,1:T(8,128)(2,1)}, u32[]{:S(2)}, u32[]{:S(2)}) collective-permute-start(bf16[2880,64]{0,1:T(8,128)(2,1)S(1)} %reshape.404), channel_id=1, source_target_pairs={{0,1},{1,0},{2,3},{3,2},{4,5},{5,4},{6,7},{7,6},{8,9},{9,8},{10,11... | collective-permute-start | bytes 1105928 | tf_op jit(solution)/shard_map/ppermute | solution.py:43
  60.5 186.5 %reduce-scatter.8.cloned.1.call-start = ((), (), s32[]{:S(2)}) async-start(), calls=%async_computation.8 | async-start | bytes 829440
  85.3 1.9 copy-start.11
  85.3 1.2 copy-start.13
  87.2 0.6 copy-start.5
  87.8 2.0 copy-start.16
  87.8 2.0 copy-start.19
  89.2 0.6 copy-start.7
  91.4 12.9 %copy-start.9 = (bf16[128,64]{0,1:T(8,128)(2,1)}, bf16[128,64]{0,1:T(8,128)(2,1)S(1)}, u32[]{:S(2)}) copy-start(bf16[128,64]{0,1:T(8,128)(2,1)S(1)} %get-tuple-element.497) | copy-start | bytes 49156
  91.4 12.7 %copy-start.8 = (f32[128,64]{0,1:T(8,128)S(1)}, f32[128,64]{0,1:T(8,128)}, u32[]{:S(2)}) copy-start(f32[128,64]{0,1:T(8,128)} %copy-done.7) | copy-start | bytes 98308
  91.4 12.7 %copy-start.12 = (f32[32]{0:T(128)S(1)}, f32[32]{0:T(128)}, u32[]{:S(2)}) copy-start(f32[32]{0:T(128)} %copy-done.11) | copy-start | bytes 388
  91.5 12.7 %copy-start.14 = (f32[128]{0:T(128)S(1)}, f32[128]{0:T(128)}, u32[]{:S(2)}) copy-start(f32[128]{0:T(128)} %copy-done.13) | copy-start | bytes 1540
  99.6 87.2 %collective-permute-start.1 = (bf16[2880,256]{1,0:T(8,128)(2,1)}, bf16[2880,256]{1,0:T(8,128)(2,1)}, u32[]{:S(2)}, u32[]{:S(2)}) collective-permute-start(bf16[2880,256]{1,0:T(8,128)(2,1)} %reshape.406), channel_id=1, source_target_pairs={{0,1},{1,0},{2,3},{3,2},{4,5},{5,4},{6,7},{7,6},{8,9},{9,8},{10,11... | collective-permute-start | bytes 4423688 | tf_op jit(solution)/shard_map/ppermute | solution.py:43
  139.1 45.3 %copy-start.17 = (f32[2880]{0:T(1024)S(1)}, f32[2880]{0:T(1024)}, u32[]{:S(2)}) copy-start(f32[2880]{0:T(1024)} %param.19) | copy-start | bytes 34564
  139.1 45.3 %copy-start.20 = (f32[128]{0:T(128)S(1)}, f32[128]{0:T(128)}, u32[]{:S(2)}) copy-start(f32[128]{0:T(128)} %add_rsqrt_fusion.1) | copy-start | bytes 1540
  180.4 31.5 %collective-permute-start.2 = (bf16[256,2880]{0,1:T(8,128)(2,1)}, bf16[256,2880]{0,1:T(8,128)(2,1)}, u32[]{:S(2)}, u32[]{:S(2)}) collective-permute-start(bf16[256,2880]{0,1:T(8,128)(2,1)} %bitcast.195), channel_id=1, source_target_pairs={{0,1},{1,0},{2,3},{3,2},{4,5},{5,4},{6,7},{7,6},{8,9},{9,8},{10,11... | collective-permute-start | bytes 4423688 | tf_op jit(solution)/shard_map/ppermute | solution.py:43
  197.2 12.6 %copy-start.6 = (f32[8,128]{1,0:T(8,128)S(1)}, f32[8,128]{1,0:T(8,128)}, u32[]{:S(2)}) copy-start(f32[8,128]{1,0:T(8,128)} %copy-done.5) | copy-start | bytes 12292
  211.9 3.1 copy-start.2
  211.9 3.3 copy-start.10
  214.8 116.4 %all-gather.8.cloned.1.call-start = ((), (), s32[]{:S(2)}) async-start(), calls=%async_computation.4 | async-start | bytes 4976640 | tf_op jit(solution)/shard_map/all_gather | solution.py:212
  275.1 59.5 %copy-start.18 = (f32[2880]{0:T(1024)S(1)}, f32[2880]{0:T(1024)}, u32[]{:S(2)}) copy-start(f32[2880]{0:T(1024)} %param.25) | copy-start | bytes 34564
  275.1 131.2 %reduce-scatter.6.cloned.1.call-start = ((), (), s32[]{:S(2)}) async-start(), calls=%async_computation.5 | async-start | bytes 4976640 | tf_op jit(solution)/shard_map/reduce_scatter | solution.py:224
  331.2 3.6 copy-start.1
  349.2 68.2 %copy-start.15 = (f32[1,128,4]{1,2,0:T(4,128)S(1)}, f32[1,128,4]{1,2,0:T(4,128)}, u32[]{:S(2)}) copy-start(f32[1,128,4]{1,2,0:T(4,128)} %param.29) | copy-start | bytes 6148
  408.4 26.4 %all-to-all-start.1 = ((bf16[16,48,360]{2,1,0:T(8,128)(2,1)}), bf16[16,48,360]{2,1,0:T(8,128)(2,1)S(1)}, u32[]{:S(2)}, u32[]{:S(2)}) async-start(bf16[16,48,360]{2,1,0:T(8,128)(2,1)} %bitcast.34), calls=%async_computation.2 | async-start | bytes 1179648 | tf_op jit(solution)/shard_map/all_to_all | solution.py:229
Sparse Core Ops, SparseCore 0:
  10.6 85.6 all-gather.9
  98.9 78.1 all-gather.11
  214.9 31.9 reduce-scatter.7
  275.2 55.9 all-gather.7
  349.4 56.8 reduce-scatter.5

commit v3 on v1

--- a/solution.py
+++ b/solution.py
@@ -37,6 +37,13 @@
         ],
         axis=-1,
     )
+
+
+def gather_by_exchange(block, axis_name):
+    count = lax.axis_size(axis_name)
+    spread = jnp.broadcast_to(block[None], (count,) + block.shape)
+    got = lax.all_to_all(spread, axis_name, split_axis=0, concat_axis=0, tiled=True)
+    return got.reshape((count * block.shape[0],) + block.shape[1:])
 
 
 def expert_rows(row_block, w_in, w_down):
@@ -69,14 +76,19 @@
     tok_count = local_rows.shape[0]
     expert_devs = lax.axis_size("expert")
     row_start = lax.axis_index("expert") * tok_count
-    whole_rows = lax.all_gather(local_rows, "mp", axis=1, tiled=True)
+    mp_devs = lax.axis_size("mp")
+    whole_rows = (
+        gather_by_exchange(local_rows.T, "mp").reshape(-1, tok_count).T
+    )
     input_normalised = rms_norm(whole_rows, attn_gain)
     query_cols = w_query.shape[1]
     kv_cols = key_weight.shape[1]
-    query_weight = lax.all_gather(w_query, "expert", axis=0, tiled=True)
-    kv_weight = lax.all_gather(
-        jnp.concatenate([key_weight, value_weight], axis=1), "expert", axis=0, tiled=True
-    )
+    big_weights = lax.all_gather(
+        jnp.concatenate([w_query, w_out.T], axis=1), "expert", axis=0, tiled=True
+    )
+    query_weight = big_weights[:, :query_cols]
+    out_weight_t = big_weights[:, query_cols:]
+    kv_weight = gather_by_exchange(jnp.concatenate([key_weight, value_weight], axis=1), "expert")
     query_raw = jnp.dot(input_normalised, query_weight, preferred_element_type=jnp.float32)
     kv_raw = jnp.dot(input_normalised, kv_weight, preferred_element_type=jnp.float32)
     key_raw = kv_raw[:, :kv_cols]
@@ -94,9 +106,7 @@
         .reshape(tok_count, kv_cols)
     )
     value_fresh = value_raw.astype(jnp.bfloat16)
-    kv_all = lax.all_gather(
-        jnp.concatenate([key_rotary, value_fresh], axis=1), "expert", axis=0, tiled=True
-    )
+    kv_all = gather_by_exchange(jnp.concatenate([key_rotary, value_fresh], axis=1), "expert")
     keys_all = kv_all[:, :kv_cols]
     values_all = kv_all[:, kv_cols:]
     seq_len = keys_all.shape[0]
@@ -156,14 +166,15 @@
         .transpose(2, 0, 1, 3)
         .reshape(tok_count, query_cols)
     )
-    out_terms = jnp.dot(
-        mixed,
-        lax.all_gather(w_out, "expert", axis=1, tiled=True),
-        preferred_element_type=jnp.float32,
-    )
-    attn_part = lax.psum_scatter(
-        out_terms.astype(jnp.bfloat16), "mp", scatter_dimension=1, tiled=True
-    ).astype(jnp.float32)
+    out_terms = lax.dot_general(
+        mixed, out_weight_t, (((1,), (1,)), ((), ())), preferred_element_type=jnp.float32
+    )
+    model_width = out_terms.shape[1]
+    out_pieces = out_terms.astype(jnp.bfloat16).reshape(tok_count, mp_devs, model_width // mp_devs)
+    out_got = lax.all_to_all(
+        out_pieces.transpose(1, 0, 2), "mp", split_axis=0, concat_axis=0, tiled=True
+    )
+    attn_part = jnp.sum(out_got.astype(jnp.float32), axis=0)
     first_out = (local_rows.astype(jnp.float32) + attn_part).astype(jnp.bfloat16)
     top_count = routes.shape[2]
     local_experts = expert_in.shape[0]

time: 441 us -> 390 us (0.88)
  blocking collectives: 123 us -> 24.2 us
  starting transfers between devices: 9.37 us -> 34.4 us
  waiting for transfers between devices: 212 us -> 235 us
  other arithmetic: 6.94 us -> 11.8 us
    all_gather x3 -> x0, blocking collectives: 100 us -> none  [the longest x1 41.8 us: shards(): lax.all_gather(jnp.concatenate([key_weight, value_weight], axis=1), 'expe...]
    all_to_all x0 -> x4, waiting for transfers between devices: none -> 68.5 us  [the longest x3 58.7 us: gather_by_exchange(): lax.all_to_all(spread, axis_name, split_axis=0, concat_axis=0, tiled=True)]
    unnamed x6 -> x3, waiting for transfers between devices: 32.6 us -> 0.05 us
    all_to_all x0 -> x4, starting transfers between devices: none -> 25.1 us  [the longest x3 21 us: gather_by_exchange(): lax.all_to_all(spread, axis_name, split_axis=0, concat_axis=0, tiled=True)]
    all_gather x2 -> x1, waiting for transfers between devices: 50.9 us -> 41.8 us  [shards(): lax.all_gather(jnp.concatenate([w_query, w_out.T], axis=1), 'expert', axi...]
    unnamed x36 -> x38, local copies, waits for them, and re-layouts: 16.3 us -> 8.77 us
  transfers between devices with their start and end apart: 6 -> 8, of which waited for: 5 -> 8; matrix products, arithmetic and copies ran while one was open for 10% -> 4% of each run, Pallas kernels for 0% -> 0%
where the time goes in v3:
time: 390 us; the launch traced here: 389 us
  waiting for transfers between devices  235 us (60%)
  matrix products  40.8 us (10%)
  starting transfers between devices  34.4 us (9%)
  local copies, waits for them, and re-layouts  28 us (7%)
  blocking collectives  24.2 us (6%)
  between operations  14.3 us (4%)
  other arithmetic  11.8 us (3%)
    all_to_all x3, waiting for transfers between devices, gather_by_exchange(): lax.all_to_all(spread, axis_name, split_axis=0, concat_axis=0, tiled=True)  58.7 us
    reduce_scatter x1, waiting for transfers between devices, shards(): lax.psum_scatter(partials_t.astype(jnp.bfloat16), 'mp', scatter_dimension...  57 us
    all_gather x1, waiting for transfers between devices, shards(): lax.all_gather(arrived_rows, 'mp', axis=1, tiled=True)  52 us
    all_gather x1, waiting for transfers between devices, shards(): lax.all_gather(jnp.concatenate([w_query, w_out.T], axis=1), 'expert', axi...  41.8 us
    all_to_all x1, blocking collectives, shards(): lax.all_to_all(outgoing, 'expert', split_axis=0, concat_axis=0, tiled=True)  24.2 us
    all_to_all x3, starting transfers between devices, gather_by_exchange(): lax.all_to_all(spread, axis_name, split_axis=0, concat_axis=0, tiled=True)  21 us
    all_to_all x1, waiting for transfers between devices, shards(): lax.all_to_all(expert_out, 'expert', split_axis=0, concat_axis=0, tiled=T...  16 us
    dot_general x8, matrix products, block_scores(): jnp.einsum('hrd,hkd->hrk', query_rows, key_part, preferred_element_type=j...  13 us
  transfers between devices with their start and end apart: 8, of which 8 were waited for; matrix products, arithmetic and copies ran while one was open for 4% of the time, Pallas kernels for 0%

profile of v3, /device:TPU:1, one launch (start us, length us, event | category | flops | bytes accessed | tf_op | source)
XLA Modules:
  0.0 389.1 jit_solution(5627423579040124694)
XLA Ops:
  7.2 1.9 maximum_bitcast_fusion
  9.2 1.9 broadcast_in_dim.90
  11.1 6.0 %all-to-all-start = ((bf16[8,360,128]{2,1,0:T(8,128)(2,1)}), bf16[8,360,128]{2,1,0:T(8,128)(2,1)S(1)}, u32[]{:S(2)}, u32[]{:S(2)}) async-start(bf16[8,360,128]{2,1,0:T(8,128)(2,1)} %broadcast_in_dim.90), calls=%async_computation | async-start | bytes 1474560 | tf_op jit(solution)/shard_map/all_to_all | solution.py:45
  17.2 12.3 %all-to-all-done = bf16[8,360,128]{2,1,0:T(8,128)(2,1)S(1)} async-done(((bf16[8,360,128]{2,1,0:T(8,128)(2,1)}), bf16[8,360,128]{2,1,0:T(8,128)(2,1)S(1)}, u32[]{:S(2)}, u32[]{:S(2)}) %all-to-all-start) | async-done | bytes 737312 | tf_op jit(solution)/shard_map/all_to_all | solution.py:45
  29.5 1.0 broadcast_in_dim.91
  30.5 10.7 %all-to-all-start.1 = ((bf16[16,180,128]{2,1,0:T(8,128)(2,1)}), bf16[16,180,128]{2,1,0:T(8,128)(2,1)}, u32[]{:S(2)}, u32[]{:S(2)}) async-start(bf16[16,180,128]{2,1,0:T(8,128)(2,1)} %broadcast_in_dim.91), calls=%async_computation.1 | async-start | bytes 1507328 | tf_op jit(solution)/shard_map/all_to_all | solution.py:45
  41.2 0.1 copy.118
  41.5 0.1 copy.107
  41.8 0.4 fusion.39
  42.3 1.4 fusion.41
  43.6 26.2 %all-to-all-done.1 = bf16[16,180,128]{2,1,0:T(8,128)(2,1)} async-done(((bf16[16,180,128]{2,1,0:T(8,128)(2,1)}), bf16[16,180,128]{2,1,0:T(8,128)(2,1)}, u32[]{:S(2)}, u32[]{:S(2)}) %all-to-all-start.1) | async-done | bytes 737312 | tf_op jit(solution)/shard_map/all_to_all | solution.py:45
  69.9 1.2 reshape.380
  71.1 1.6 fusion.97
  72.7 0.1 fusion.84
  73.0 0.9 broadcast_in_dim.92
  73.9 4.3 %all-to-all-start.2 = ((bf16[16,128,128]{2,1,0:T(8,128)(2,1)}), bf16[16,128,128]{2,1,0:T(8,128)(2,1)S(1)}, u32[]{:S(2)}, u32[]{:S(2)}) async-start(bf16[16,128,128]{2,1,0:T(8,128)(2,1)} %broadcast_in_dim.92), calls=%async_computation.2 | async-start | bytes 1048576 | tf_op jit(solution)/shard_map/all_to_all | solution.py:45
  78.5 1.2 reduce-window.6
  79.6 0.2 slice_reduce_fusion
  80.0 0.1 multiply_cosine_fusion
  80.1 20.2 %all-to-all-done.2 = bf16[16,128,128]{2,1,0:T(8,128)(2,1)S(1)} async-done(((bf16[16,128,128]{2,1,0:T(8,128)(2,1)}), bf16[16,128,128]{2,1,0:T(8,128)(2,1)S(1)}, u32[]{:S(2)}, u32[]{:S(2)}) %all-to-all-start.2) | async-done | bytes 524320 | tf_op jit(solution)/shard_map/all_to_all | solution.py:45
  100.3 1.2 slice_bitcast_fusion
  101.5 41.8 %all-gather.6.cloned.1.call-done = bf16[16,180,1024]{2,1,0:T(8,128)(2,1)} async-done(((bf16[1,180,1024]{2,1,0:T(8,128)(2,1)}), bf16[16,180,1024]{2,1,0:T(8,128)(2,1)}) %all-gather.6.cloned.1.call-update) | async-done | bytes 5898256 | tf_op jit(solution)/shard_map/all_gather | solution.py:86
  143.3 8.0 %reshape.421 = bf16[2880,1024]{1,0:T(8,128)(2,1)} reshape(bf16[16,180,1024]{2,1,0:T(8,128)(2,1)} %all-gather.6.cloned.1.call-done) | data formatting | bytes 11796480
  151.3 3.1 fusion.29
  154.5 0.2 copy.127
  154.7 6.6 %while.30 = (s32[]{:T(128)}, f32[1,1024]{1,0:T(1,128)S(1)}, s32[2048]{0:T(1024)S(1)}, bf16[1,2048,64]{2,1,0:T(8,128)(2,1)}, bf16[1,1024,64]{2,1,0:T(8,128)(2,1)S...) while((s32[]{:T(128)}, f32[1,1024]{1,0:T(1,128)S(1)}, ...), condition=%wide.region_3.4_spmd.clone, body=%wide.region_1.3_spmd.clone.sunk | while | flops 70255112 | bytes 306343 | solution.py:145
  154.8 1.5 fusion.112
  156.5 1.5 fusion.112
  158.1 1.5 fusion.112
  159.7 1.5 fusion.112
  161.3 12.7 %while.31 = (s32[]{:T(128)}, f32[1,1024,64]{1,2,0:T(8,128)S(1)}, f32[1,1024]{1,0:T(1,128)S(1)}, s32[2048]{0:T(1024)S(1)}, bf16[1,2048,64]{2,1,0:T(8,128)(2,1)}, ...) while((s32[]{:T(128)}, f32[1,1024,64]{1,2,0:T(8,128)S(1)}, ...), condition=%wide.region_6.7_spmd.clone, body=%wide.region_4.6_spmd.clone.sunk | while | flops 139068928 | bytes 3062998 | solution.py:161
  161.4 1.7 convert_reduce_fusion.3
  163.1 1.3 fusion.115
  164.6 1.7 convert_reduce_fusion.3
  166.3 1.3 fusion.115
  167.7 1.7 convert_reduce_fusion.3
  169.5 1.3 fusion.115
  170.9 1.7 convert_reduce_fusion.3
  172.6 1.3 fusion.115
  174.1 3.6 convolution_convert_fusion.1
  177.7 4.1 %all-to-all-start.3 = ((bf16[8,128,360]{1,2,0:T(8,128)(2,1)}), bf16[8,128,360]{1,2,0:T(8,128)(2,1)S(1)}, u32[]{:S(2)}, u32[]{:S(2)}) async-start(bf16[8,128,360]{1,2,0:T(8,128)(2,1)} %bitcast.195), calls=%async_computation.3 | async-start | bytes 1474560 | tf_op jit(solution)/shard_map/all_to_all | solution.py:174
  181.9 2.4 scatter_custom_fusion
  184.4 9.8 %all-to-all-done.3 = bf16[8,128,360]{1,2,0:T(8,128)(2,1)S(1)} async-done(((bf16[8,128,360]{1,2,0:T(8,128)(2,1)}), bf16[8,128,360]{1,2,0:T(8,128)(2,1)S(1)}, u32[]{:S(2)}, u32[]{:S(2)}) %all-to-all-start.3) | async-done | bytes 737312 | tf_op jit(solution)/shard_map/all_to_all | solution.py:174
  194.3 0.1 copy.116
  194.5 2.6 gather_fusion
  197.1 24.2 %all_to_all.30 = bf16[16,48,360]{2,1,0:T(8,128)(2,1)S(1)} all-to-all(bf16[16,48,360]{2,1,0:T(8,128)(2,1)S(1)} %bitcast.192), channel_id=1, replica_groups=mesh['expert'=16,'mp'=8,'batch'=2] {'expert'}, dimensions={0} | all-to-all | bytes 1105920 | tf_op jit(solution)/shard_map/all_to_all | solution.py:198
  221.3 1.1 copy.121
  222.4 0.2 reduce-scatter.2.cloned.1.call-start
  222.6 52.0 %all-gather.4.cloned.1.call-done = bf16[768,2880]{0,1:T(8,128)(2,1)} async-done(((bf16[768,360]{0,1:T(8,128)(2,1)}), bf16[768,2880]{0,1:T(8,128)(2,1)}) %all-gather.4.cloned.1.call-update) | async-done | bytes 4423696 | tf_op jit(solution)/shard_map/all_gather | solution.py:200
  274.6 3.3 fusion.25
  277.9 0.2 copy-done.1
  278.1 3.9 fusion.42
  282.0 10.6 %fusion.28 = bf16[2880,768]{1,0:T(8,128)(2,1)} fusion(bf16[1,360,2880]{2,1,0:T(8,128)(2,1)S(1)} %copy-done, f32[768,360]{0,1:T(8,128)S(1)} %fusion.42, bf16[1,2,2880,360]{2,3,1,0:T(8,128)(2,1)} %param.26, bf16[768,2880]{0,1:T(8,128)(2,1)} %all-gather.4.cloned.1.call-done, f32[2880]{0:T(1024)S(1)} %copy-done.15, f32[768]{0:T(1024)S(1)} %add_rsqrt_fusion), kind=kOutput, calls=%fused_computation.41 | convolution fusion | flops 3198597120 | bytes 14161152 | tf_op jit(solution)/shard_map/dot_general | solution.py:209
  292.7 57.0 %reduce-scatter.2.cloned.1.call-done = bf16[360,768]{1,0:T(8,128)(2,1)} async-done(((bf16[2880,768]{1,0:T(8,128)(2,1)}), bf16[360,768]{1,0:T(8,128)(2,1)}) %reduce-scatter.2.cloned.1.call-update) | async-done | bytes 552976 | tf_op jit(solution)/shard_map/reduce_scatter | solution.py:212
  349.7 2.1 copy.122
  351.8 9.0 %all-to-all-start.5 = ((bf16[16,48,360]{2,1,0:T(8,128)(2,1)}), bf16[16,48,360]{2,1,0:T(8,128)(2,1)S(1)}, u32[]{:S(2)}, u32[]{:S(2)}) async-start(bf16[16,48,360]{2,1,0:T(8,128)(2,1)} %bitcast.36), calls=%async_computation.6 | async-start | bytes 1179648 | tf_op jit(solution)/shard_map/all_to_all | solution.py:217
  360.9 0.6 pad_maximum_fusion.2
  361.5 0.6 slice_bitcast_fusion.3
  362.1 16.0 %all-to-all-done.5 = bf16[16,48,360]{2,1,0:T(8,128)(2,1)S(1)} async-done(((bf16[16,48,360]{2,1,0:T(8,128)(2,1)}), bf16[16,48,360]{2,1,0:T(8,128)(2,1)S(1)}, u32[]{:S(2)}, u32[]{:S(2)}) %all-to-all-start.5) | async-done | bytes 552992 | tf_op jit(solution)/shard_map/all_to_all | solution.py:217
  378.1 1.9 gather_fusion.1
  380.1 0.2 reshape.394
  380.3 0.6 multiply_reduce_fusion
  380.9 0.1 copy.124
  381.0 1.6 fusion.70
  (107 shorter events, 2.4 us)
Async XLA Ops:
  7.2 274.9 %copy-start = (bf16[1,360,2880]{2,1,0:T(8,128)(2,1)S(1)}, bf16[1,360,2880]{2,1,0:T(8,128)(2,1)}, u32[]{:S(2)}) copy-start(bf16[1,360,2880]{2,1,0:T(8,128)(2,1)} %param.27) | copy-start | bytes 6220804
  7.2 9.9 %copy-start.9 = (bf16[180,64]{0,1:T(8,128)(2,1)S(1)}, bf16[180,64]{0,1:T(8,128)(2,1)}, u32[]{:S(2)}) copy-start(bf16[180,64]{0,1:T(8,128)(2,1)} %param.22) | copy-start | bytes 69124
  7.2 9.9 %copy-start.10 = (bf16[180,64]{0,1:T(8,128)(2,1)S(1)}, bf16[180,64]{0,1:T(8,128)(2,1)}, u32[]{:S(2)}) copy-start(bf16[180,64]{0,1:T(8,128)(2,1)} %param.21) | copy-start | bytes 69124
  7.2 136.1 %all-gather.6.cloned.1.call-start = ((), (), s32[]{:S(2)}) async-start(), calls=%async_computation.9 | async-start | bytes 6406144 | tf_op jit(solution)/shard_map/all_gather | solution.py:86
  11.1 30.1 %copy-start.12 = (s32[1,128,4]{1,2,0:T(4,128)S(1)}, s32[1,128,4]{1,2,0:T(4,128)}, u32[]{:S(2)}) copy-start(s32[1,128,4]{1,2,0:T(4,128)} %param.28) | copy-start | bytes 6148
  11.1 30.5 %copy-start.5 = (bf16[1,128,360]{1,2,0:T(8,128)(2,1)S(1)}, bf16[1,128,360]{1,2,0:T(8,128)(2,1)}, u32[]{:S(2)}) copy-start(bf16[1,128,360]{1,2,0:T(8,128)(2,1)} %param.17) | copy-start | bytes 276484
  11.1 30.6 %copy-start.14 = (f32[8]{0:T(128)S(1)}, f32[8]{0:T(128)}, u32[]{:S(2)}) copy-start(f32[8]{0:T(128)} %param.24) | copy-start | bytes 100
  11.1 18.5 %all-to-all-start = ((bf16[8,360,128]{2,1,0:T(8,128)(2,1)}), bf16[8,360,128]{2,1,0:T(8,128)(2,1)S(1)}, u32[]{:S(2)}, u32[]{:S(2)}) async-start(bf16[8,360,128]{2,1,0:T(8,128)(2,1)} %broadcast_in_dim.90), calls=%async_computation | async-start | bytes 1474560 | tf_op jit(solution)/shard_map/all_to_all | solution.py:45
  17.1 25.2 %copy-start.11 = (f32[2880]{0:T(1024)S(1)}, f32[2880]{0:T(1024)}, u32[]{:S(2)}) copy-start(f32[2880]{0:T(1024)} %param.19) | copy-start | bytes 34564
  30.5 39.4 %all-to-all-start.1 = ((bf16[16,180,128]{2,1,0:T(8,128)(2,1)}), bf16[16,180,128]{2,1,0:T(8,128)(2,1)}, u32[]{:S(2)}, u32[]{:S(2)}) async-start(bf16[16,180,128]{2,1,0:T(8,128)(2,1)} %broadcast_in_dim.91), calls=%async_computation.1 | async-start | bytes 1507328 | tf_op jit(solution)/shard_map/all_to_all | solution.py:45
  71.1 8.8 %copy-start.8 = (s32[1,2048]{1,0:T(1,128)S(1)}, s32[1,2048]{1,0:T(1,128)}, u32[]{:S(2)}) copy-start(s32[1,2048]{1,0:T(1,128)} %param.18) | copy-start | bytes 24580
  72.8 28.6 %copy-start.6 = (bf16[128,1,32]{0,2,1:T(8,128)(2,1)}, bf16[128,1,32]{0,2,1:T(8,128)(2,1)S(1)}, u32[]{:S(2)}) copy-start(bf16[128,1,32]{0,2,1:T(8,128)(2,1)S(1)} %get-tuple-element.497) | copy-start | bytes 24580
  73.9 26.4 %all-to-all-start.2 = ((bf16[16,128,128]{2,1,0:T(8,128)(2,1)}), bf16[16,128,128]{2,1,0:T(8,128)(2,1)S(1)}, u32[]{:S(2)}, u32[]{:S(2)}) async-start(bf16[16,128,128]{2,1,0:T(8,128)(2,1)} %broadcast_in_dim.92), calls=%async_computation.2 | async-start | bytes 1048576 | tf_op jit(solution)/shard_map/all_to_all | solution.py:45
  101.5 49.8 %copy-start.2 = (bf16[2880,128]{1,0:T(8,128)(2,1)S(1)}, bf16[2880,128]{1,0:T(8,128)(2,1)}, u32[]{:S(2)}) copy-start(bf16[2880,128]{1,0:T(8,128)(2,1)} %fusion.41) | copy-start | bytes 2211844
  177.7 16.5 %all-to-all-start.3 = ((bf16[8,128,360]{1,2,0:T(8,128)(2,1)}), bf16[8,128,360]{1,2,0:T(8,128)(2,1)S(1)}, u32[]{:S(2)}, u32[]{:S(2)}) async-start(bf16[8,128,360]{1,2,0:T(8,128)(2,1)} %bitcast.195), calls=%async_computation.3 | async-start | bytes 1474560 | tf_op jit(solution)/shard_map/all_to_all | solution.py:174
  181.8 92.7 %all-gather.4.cloned.1.call-start = ((), (), s32[]{:S(2)}) async-start(), calls=%async_computation.7 | async-start | bytes 4976640 | tf_op jit(solution)/shard_map/all_gather | solution.py:200
  194.3 2.8 copy-start.3
  222.4 55.6 %copy-start.15 = (f32[2880]{0:T(1024)S(1)}, f32[2880]{0:T(1024)}, u32[]{:S(2)}) copy-start(f32[2880]{0:T(1024)} %param.25) | copy-start | bytes 34564
  222.4 127.3 %reduce-scatter.2.cloned.1.call-start = ((), (), s32[]{:S(2)}) async-start(), calls=%async_computation.8 | async-start | bytes 4976640 | tf_op jit(solution)/shard_map/reduce_scatter | solution.py:212
  274.6 3.6 copy-start.1
  292.6 68.2 %copy-start.13 = (f32[1,128,4]{1,2,0:T(4,128)S(1)}, f32[1,128,4]{1,2,0:T(4,128)}, u32[]{:S(2)}) copy-start(f32[1,128,4]{1,2,0:T(4,128)} %param.29) | copy-start | bytes 6148
  292.6 68.3 %copy-start.7 = (bf16[128,1,32]{0,2,1:T(8,128)(2,1)S(1)}, bf16[128,1,32]{0,2,1:T(8,128)(2,1)}, u32[]{:S(2)}) copy-start(bf16[128,1,32]{0,2,1:T(8,128)(2,1)} %copy-done.6) | copy-start | bytes 24580
  351.8 26.4 %all-to-all-start.5 = ((bf16[16,48,360]{2,1,0:T(8,128)(2,1)}), bf16[16,48,360]{2,1,0:T(8,128)(2,1)S(1)}, u32[]{:S(2)}, u32[]{:S(2)}) async-start(bf16[16,48,360]{2,1,0:T(8,128)(2,1)} %bitcast.36), calls=%async_computation.6 | async-start | bytes 1179648 | tf_op jit(solution)/shard_map/all_to_all | solution.py:217
  380.1 0.9 copy-start.4
Sparse Core Ops, SparseCore 0:
  10.6 132.6 all-gather.5
  222.5 52.0 all-gather.3
  292.8 56.8 reduce-scatter.1

commit v4 on v3

--- a/solution.py
+++ b/solution.py
@@ -84,10 +84,10 @@
     query_cols = w_query.shape[1]
     kv_cols = key_weight.shape[1]
     big_weights = lax.all_gather(
-        jnp.concatenate([w_query, w_out.T], axis=1), "expert", axis=0, tiled=True
-    )
-    query_weight = big_weights[:, :query_cols]
-    out_weight_t = big_weights[:, query_cols:]
+        jnp.stack([w_query, w_out.T], axis=0), "expert", axis=1, tiled=True
+    )
+    query_weight = big_weights[0]
+    out_weight_t = big_weights[1]
     kv_weight = gather_by_exchange(jnp.concatenate([key_weight, value_weight], axis=1), "expert")
     query_raw = jnp.dot(input_normalised, query_weight, preferred_element_type=jnp.float32)
     kv_raw = jnp.dot(input_normalised, kv_weight, preferred_element_type=jnp.float32)
@@ -194,9 +194,10 @@
     padded = jnp.concatenate(
         [first_out, jnp.zeros((1, first_out.shape[1]), jnp.bfloat16)], axis=0
     )
-    outgoing = padded[source_row].reshape(expert_count, capacity, padded.shape[1])
+    local_cols = padded.shape[1]
+    outgoing = padded[source_row].reshape(expert_count, capacity, local_cols)
     arrived = lax.all_to_all(outgoing, "expert", split_axis=0, concat_axis=0, tiled=True)
-    arrived_rows = arrived.reshape(expert_count * capacity, arrived.shape[2])
+    arrived_rows = arrived.reshape(expert_count * capacity, local_cols)
     inputs = rms_norm(lax.all_gather(arrived_rows, "mp", axis=1, tiled=True), moe_gain)
     w_in = expert_in[0]
     gate_val = jnp.dot(inputs, w_in[0], preferred_element_type=jnp.float32)
@@ -209,10 +210,14 @@
     partials_t = lax.dot_general(
         expert_down[0], activated, (((0,), (1,)), ((), ())), preferred_element_type=jnp.float32
     )
-    expert_out_t = lax.psum_scatter(
-        partials_t.astype(jnp.bfloat16), "mp", scatter_dimension=0, tiled=True
-    )
-    local_width = expert_out_t.shape[0]
+    local_width = model_width // mp_devs
+    partial_pieces = partials_t.astype(jnp.bfloat16).reshape(mp_devs, local_width, -1)
+    expert_out_t = jnp.sum(
+        lax.all_to_all(partial_pieces, "mp", split_axis=0, concat_axis=0, tiled=True).astype(
+            jnp.float32
+        ),
+        axis=0,
+    ).astype(jnp.bfloat16)
     expert_out = expert_out_t.T.reshape(expert_count, capacity, local_width)
     returned = lax.all_to_all(expert_out, "expert", split_axis=0, concat_axis=0, tiled=True)
     picked = returned.reshape(expert_count * capacity, local_width)[target].reshape(

time: 390 us -> 417 us (1.069)
  waiting for transfers between devices: 235 us -> 172 us
  blocking collectives: 24.2 us -> 80.2 us
  local copies, waits for them, and re-layouts: 28 us -> 54.6 us
    reduce_scatter x1 -> x0, waiting for transfers between devices: 57 us -> none  [shards(): lax.psum_scatter(partials_t.astype(jnp.bfloat16), 'mp', scatter_dimension...]
    all_to_all x0 -> x1, blocking collectives: none -> 55.5 us  [shards(): lax.all_to_all(partial_pieces, 'mp', split_axis=0, concat_axis=0, tiled=T...]
    dot_general x0 -> x1, local copies, waits for them, and re-layouts: none -> 13.6 us  [shards(): jnp.dot(input_normalised, query_weight, preferred_element_type=jnp.float32)]
    slice x1 -> x2, local copies, waits for them, and re-layouts: 0.22 us -> 13.2 us  [the longest x1 13 us: shards(): out_weight_t = big_weights[1]]
    unnamed x38 -> x45, local copies, waits for them, and re-layouts: 8.77 us -> 1.45 us
    dynamic_slice x8, local copies, waits for them, and re-layouts: 0.64 us -> 6.11 us  [block_scores(): key_seg = lax.dynamic_slice_in_dim(seg_all, key_first, key_block, 0)]
  transfers between devices with their start and end apart: 8 -> 7, of which waited for: 8 -> 7; matrix products, arithmetic and copies ran while one was open for 4% -> 5% of each run, Pallas kernels for 0% -> 0%
where the time goes in v4:
time: 417 us; the launch traced here: 413 us
  waiting for transfers between devices  172 us (41%)
  blocking collectives  80.2 us (19%)
  local copies, waits for them, and re-layouts  54.6 us (13%)
  matrix products  42.3 us (10%)
  starting transfers between devices  34.5 us (8%)
  other arithmetic  14.8 us (4%)
  between operations  14.6 us (4%)
    all_to_all x3, waiting for transfers between devices, gather_by_exchange(): lax.all_to_all(spread, axis_name, split_axis=0, concat_axis=0, tiled=True)  56.4 us
    all_to_all x1, blocking collectives, shards(): lax.all_to_all(partial_pieces, 'mp', split_axis=0, concat_axis=0, tiled=T...  55.5 us
    all_gather x1, waiting for transfers between devices, shards(): lax.all_gather(arrived_rows, 'mp', axis=1, tiled=True)  52.1 us
    all_gather x1, waiting for transfers between devices, shards(): lax.all_gather(jnp.stack([w_query, w_out.T], axis=0), 'expert', axis=1, t...  40.5 us
    all_to_all x1, blocking collectives, shards(): lax.all_to_all(outgoing, 'expert', split_axis=0, concat_axis=0, tiled=True)  24.7 us
    all_to_all x3, starting transfers between devices, gather_by_exchange(): lax.all_to_all(spread, axis_name, split_axis=0, concat_axis=0, tiled=True)  20.9 us
    dot_general x8, matrix products, block_scores(): jnp.einsum('hrd,hkd->hrk', query_rows, key_part, preferred_element_type=j...  13.9 us
    dot_general x1, local copies, waits for them, and re-layouts, shards(): jnp.dot(input_normalised, query_weight, preferred_element_type=jnp.float32)  13.6 us
  transfers between devices with their start and end apart: 7, of which 7 were waited for; matrix products, arithmetic and copies ran while one was open for 5% of the time, Pallas kernels for 0%

profile of v4, /device:TPU:1, one launch (start us, length us, event | category | flops | bytes accessed | tf_op | source)
XLA Modules:
  0.0 413.1 jit_solution(3432671593237052039)
XLA Ops:
  7.2 1.2 pad_maximum_fusion
  8.4 1.0 copy.96
  9.5 1.9 broadcast_in_dim.90
  11.4 6.0 %all-to-all-start = ((bf16[8,360,128]{2,1,0:T(8,128)(2,1)}), bf16[8,360,128]{2,1,0:T(8,128)(2,1)S(1)}, u32[]{:S(2)}, u32[]{:S(2)}) async-start(bf16[8,360,128]{2,1,0:T(8,128)(2,1)} %broadcast_in_dim.90), calls=%async_computation | async-start | bytes 1474560 | tf_op jit(solution)/shard_map/all_to_all | solution.py:45
  17.5 12.3 %all-to-all-done = bf16[8,360,128]{2,1,0:T(8,128)(2,1)S(1)} async-done(((bf16[8,360,128]{2,1,0:T(8,128)(2,1)}), bf16[8,360,128]{2,1,0:T(8,128)(2,1)S(1)}, u32[]{:S(2)}, u32[]{:S(2)}) %all-to-all-start) | async-done | bytes 737312 | tf_op jit(solution)/shard_map/all_to_all | solution.py:45
  29.8 1.0 broadcast_in_dim.91
  30.8 10.7 %all-to-all-start.1 = ((bf16[16,180,128]{2,1,0:T(8,128)(2,1)}), bf16[16,180,128]{2,1,0:T(8,128)(2,1)}, u32[]{:S(2)}, u32[]{:S(2)}) async-start(bf16[16,180,128]{2,1,0:T(8,128)(2,1)} %broadcast_in_dim.91), calls=%async_computation.1 | async-start | bytes 1507328 | tf_op jit(solution)/shard_map/all_to_all | solution.py:45
  42.6 1.4 fusion.37
  44.0 26.4 %all-to-all-done.1 = bf16[16,180,128]{2,1,0:T(8,128)(2,1)} async-done(((bf16[16,180,128]{2,1,0:T(8,128)(2,1)}), bf16[16,180,128]{2,1,0:T(8,128)(2,1)}, u32[]{:S(2)}, u32[]{:S(2)}) %all-to-all-start.1) | async-done | bytes 737312 | tf_op jit(solution)/shard_map/all_to_all | solution.py:45
  70.4 1.2 reshape.382
  71.6 1.5 fusion.96
  73.5 0.9 broadcast_in_dim.92
  74.4 4.2 %all-to-all-start.2 = ((bf16[16,128,128]{2,1,0:T(8,128)(2,1)}), bf16[16,128,128]{2,1,0:T(8,128)(2,1)S(1)}, u32[]{:S(2)}, u32[]{:S(2)}) async-start(bf16[16,128,128]{2,1,0:T(8,128)(2,1)} %broadcast_in_dim.92), calls=%async_computation.2 | async-start | bytes 1048576 | tf_op jit(solution)/shard_map/all_to_all | solution.py:45
  78.6 1.2 reduce-window.6
  80.2 0.7 mul.228
  81.5 0.7 fusion.75
  82.3 17.8 %all-to-all-done.2 = bf16[16,128,128]{2,1,0:T(8,128)(2,1)S(1)} async-done(((bf16[16,128,128]{2,1,0:T(8,128)(2,1)}), bf16[16,128,128]{2,1,0:T(8,128)(2,1)S(1)}, u32[]{:S(2)}, u32[]{:S(2)}) %all-to-all-start.2) | async-done | bytes 524320 | tf_op jit(solution)/shard_map/all_to_all | solution.py:45
  100.1 1.2 slice_bitcast_fusion
  101.3 40.5 %all-gather.3.cloned.1.call-done = bf16[2,2880,512]{2,0,1:T(2,128)(2,1)} async-done(((bf16[2,180,512]{2,0,1:T(2,128)(2,1)}), bf16[2,2880,512]{2,0,1:T(2,128)(2,1)}) %all-gather.3.cloned.1.call-update) | async-done | bytes 5898256 | tf_op jit(solution)/shard_map/all_gather | solution.py:86
  141.8 13.0 %fusion.95 = (bf16[1,2880,512]{2,0,1:T(2,128)(2,1)}, bf16[1,2880,512]{2,0,1:T(2,128)(2,1)}) fusion(bf16[2,2880,512]{2,0,1:T(2,128)(2,1)} %all-gather.3.cloned.1.call-done), kind=kLoop, calls=%fused_computation.135 | loop fusion | bytes 11796480 | tf_op jit(solution)/shard_map/slice | solution.py:90
  154.7 13.6 %copy.118 = bf16[1,2880,512]{1,2,0:T(8,128)(2,1)} copy(bf16[1,2880,512]{2,0,1:T(2,128)(2,1)} %get-tuple-element.493) | data formatting | bytes 5898240 | tf_op jit(solution)/shard_map/dot_general | solution.py:92
  168.3 2.8 fusion.62
  171.2 0.9 copy.114
  172.1 9.7 %while.30 = (s32[]{:T(128)}, f32[1,1024]{1,0:T(1,128)S(1)}, s32[2048]{0:T(1024)}, bf16[1,2048,64]{2,1,0:T(8,128)(2,1)}, bf16[1,1024,64]{2,1,0:T(8,128)(2,1)}, /*...) while((s32[]{:T(128)}, f32[1,1024]{1,0:T(1,128)S(1)}, ...), condition=%wide.region_3.4_spmd.clone, body=%wide.region_1.3_spmd.clone.sunk | while | flops 70255112 | bytes 437415 | solution.py:145
  172.1 0.8 dynamic_slice.65
  172.8 1.6 fusion.111
  174.5 0.8 dynamic_slice.65
  175.2 1.6 fusion.111
  176.9 0.8 dynamic_slice.65
  177.7 1.6 fusion.111
  179.3 0.8 dynamic_slice.65
  180.1 1.6 fusion.111
  181.8 15.9 %while.31 = (s32[]{:T(128)}, f32[1,1024,64]{1,2,0:T(8,128)S(1)}, f32[1,1024]{1,0:T(1,128)S(1)}, s32[2048]{0:T(1024)}, bf16[1,2048,64]{2,1,0:T(8,128)(2,1)}, /*in...) while((s32[]{:T(128)}, f32[1,1024,64]{1,2,0:T(8,128)S(1)}, ...), condition=%wide.region_6.7_spmd.clone, body=%wide.region_4.6_spmd.clone.sunk | while | flops 139068928 | bytes 3194062 | solution.py:161
  181.8 0.8 dynamic_slice.68
  182.6 1.9 convert_reduce_fusion.3
  184.4 1.3 fusion.114
  185.8 0.8 dynamic_slice.68
  186.5 1.9 convert_reduce_fusion.3
  188.4 1.3 fusion.114
  189.7 0.8 dynamic_slice.68
  190.5 1.9 convert_reduce_fusion.3
  192.4 1.3 fusion.114
  193.7 0.8 dynamic_slice.68
  194.5 1.9 convert_reduce_fusion.3
  196.3 1.3 fusion.114
  197.8 4.5 %convolution_convert_fusion.1 = bf16[128,2880]{0,1:T(8,128)(2,1)} fusion(bf16[128,512]{0,1:T(8,128)(2,1)S(1)} %bitcast.215, bf16[1,2880,512]{2,0,1:T(2,128)(2,1)} %get-tuple-element.492), kind=kOutput, calls=%fused_computation.41 | convolution fusion | flops 377856000 | bytes 3817472 | tf_op jit(solution)/shard_map/dot_general | solution.py:169
  202.3 4.5 %all-to-all-start.3 = ((bf16[8,128,360]{1,2,0:T(8,128)(2,1)}), bf16[8,128,360]{1,2,0:T(8,128)(2,1)S(1)}, u32[]{:S(2)}, u32[]{:S(2)}) async-start(bf16[8,128,360]{1,2,0:T(8,128)(2,1)} %bitcast.210), calls=%async_computation.3 | async-start | bytes 1474560 | tf_op jit(solution)/shard_map/all_to_all | solution.py:174
  206.9 2.4 scatter_custom_fusion
  209.4 9.4 %all-to-all-done.3 = bf16[8,128,360]{1,2,0:T(8,128)(2,1)S(1)} async-done(((bf16[8,128,360]{1,2,0:T(8,128)(2,1)}), bf16[8,128,360]{1,2,0:T(8,128)(2,1)S(1)}, u32[]{:S(2)}, u32[]{:S(2)}) %all-to-all-start.3) | async-done | bytes 737312 | tf_op jit(solution)/shard_map/all_to_all | solution.py:174
  219.1 2.6 gather_fusion
  221.7 24.7 %all_to_all.35 = bf16[16,48,360]{2,1,0:T(8,128)(2,1)S(1)} all-to-all(bf16[16,48,360]{2,1,0:T(8,128)(2,1)S(1)} %bitcast.206), channel_id=1, replica_groups=mesh['expert'=16,'mp'=8,'batch'=2] {'expert'}, dimensions={0} | all-to-all | bytes 1105920 | tf_op jit(solution)/shard_map/all_to_all | solution.py:199
  246.4 1.1 copy.109
  247.5 52.1 %all-gather.5.cloned.1.call-done = bf16[768,2880]{0,1:T(8,128)(2,1)} async-done(((bf16[768,360]{0,1:T(8,128)(2,1)}), bf16[768,2880]{0,1:T(8,128)(2,1)}) %all-gather.5.cloned.1.call-update) | async-done | bytes 4423696 | tf_op jit(solution)/shard_map/all_gather | solution.py:201
  299.7 3.3 fusion.25
  303.2 3.9 fusion.38
  307.1 10.6 %convolution_convert_fusion = bf16[768,2880]{0,1:T(8,128)(2,1)} fusion(bf16[1,360,2880]{2,1,0:T(8,128)(2,1)S(1)} %copy-done, f32[768,360]{0,1:T(8,128)S(1)} %fusion.38, bf16[1,2,2880,360]{2,3,1,0:T(8,128)(2,1)} %param.26, bf16[768,2880]{0,1:T(8,128)(2,1)} %all-gather.5.cloned.1.call-done, f32[2880]{0:T(1024)S(1)} %copy-done.19, f32[768]{0:T(1024)S(1)} %add_rsqrt_fusion), kind=kOutput, calls=%fused_computation.40 | convolution fusion | flops 3198597120 | bytes 14161152 | tf_op jit(solution)/shard_map/dot_general | solution.py:210
  317.7 55.5 %all_to_all.36 = bf16[8,360,768]{2,1,0:T(8,128)(2,1)} all-to-all(bf16[8,360,768]{2,1,0:T(8,128)(2,1)} %bitcast.205), channel_id=1, replica_groups=mesh['expert'=16,'mp'=8,'batch'=2] {'mp'}, dimensions={0} | all-to-all | bytes 8847360 | tf_op jit(solution)/shard_map/all_to_all | solution.py:216
  373.2 3.1 reduce_sum.82
  376.4 1.1 copy.110
  377.5 9.0 %all-to-all-start.6 = ((bf16[16,48,360]{2,1,0:T(8,128)(2,1)}), bf16[16,48,360]{2,1,0:T(8,128)(2,1)S(1)}, u32[]{:S(2)}, u32[]{:S(2)}) async-start(bf16[16,48,360]{2,1,0:T(8,128)(2,1)} %bitcast.42), calls=%async_computation.6 | async-start | bytes 1179648 | tf_op jit(solution)/shard_map/all_to_all | solution.py:222
  387.2 1.4 slice_bitcast_fusion.3
  388.6 13.2 %all-to-all-done.6 = bf16[16,48,360]{2,1,0:T(8,128)(2,1)S(1)} async-done(((bf16[16,48,360]{2,1,0:T(8,128)(2,1)}), bf16[16,48,360]{2,1,0:T(8,128)(2,1)S(1)}, u32[]{:S(2)}, u32[]{:S(2)}) %all-to-all-start.6) | async-done | bytes 552992 | tf_op jit(solution)/shard_map/all_to_all | solution.py:222
  401.8 1.9 gather_fusion.1
  404.7 1.6 fusion.68
  (116 shorter events, 5.2 us)
Async XLA Ops:
  7.2 299.9 %copy-start = (bf16[1,360,2880]{2,1,0:T(8,128)(2,1)S(1)}, bf16[1,360,2880]{2,1,0:T(8,128)(2,1)}, u32[]{:S(2)}) copy-start(bf16[1,360,2880]{2,1,0:T(8,128)(2,1)} %param.27) | copy-start | bytes 6220804
  7.2 10.2 %copy-start.12 = (bf16[180,64]{0,1:T(8,128)(2,1)S(1)}, bf16[180,64]{0,1:T(8,128)(2,1)}, u32[]{:S(2)}) copy-start(bf16[180,64]{0,1:T(8,128)(2,1)} %param.21) | copy-start | bytes 69124
  7.2 10.2 %copy-start.11 = (bf16[180,64]{0,1:T(8,128)(2,1)S(1)}, bf16[180,64]{0,1:T(8,128)(2,1)}, u32[]{:S(2)}) copy-start(bf16[180,64]{0,1:T(8,128)(2,1)} %param.22) | copy-start | bytes 69124
  7.2 134.6 %all-gather.3.cloned.1.call-start = ((), (), s32[]{:S(2)}) async-start(), calls=%async_computation.7 | async-start | bytes 6266880 | tf_op jit(solution)/shard_map/all_gather | solution.py:86
  11.4 30.2 %copy-start.5 = (bf16[1,128,360]{1,2,0:T(8,128)(2,1)S(1)}, bf16[1,128,360]{1,2,0:T(8,128)(2,1)}, u32[]{:S(2)}) copy-start(bf16[1,128,360]{1,2,0:T(8,128)(2,1)} %param.17) | copy-start | bytes 276484
  11.4 30.3 %copy-start.16 = (s32[1,128,4]{1,2,0:T(4,128)S(1)}, s32[1,128,4]{1,2,0:T(4,128)}, u32[]{:S(2)}) copy-start(s32[1,128,4]{1,2,0:T(4,128)} %param.28) | copy-start | bytes 6148
  11.4 30.6 %copy-start.18 = (f32[8]{0:T(128)S(1)}, f32[8]{0:T(128)}, u32[]{:S(2)}) copy-start(f32[8]{0:T(128)} %param.24) | copy-start | bytes 100
  11.4 18.5 %all-to-all-start = ((bf16[8,360,128]{2,1,0:T(8,128)(2,1)}), bf16[8,360,128]{2,1,0:T(8,128)(2,1)S(1)}, u32[]{:S(2)}, u32[]{:S(2)}) async-start(bf16[8,360,128]{2,1,0:T(8,128)(2,1)} %broadcast_in_dim.90), calls=%async_computation | async-start | bytes 1474560 | tf_op jit(solution)/shard_map/all_to_all | solution.py:45
  17.4 25.2 %copy-start.13 = (f32[2880]{0:T(1024)S(1)}, f32[2880]{0:T(1024)}, u32[]{:S(2)}) copy-start(f32[2880]{0:T(1024)} %param.19) | copy-start | bytes 34564
  30.8 39.5 %all-to-all-start.1 = ((bf16[16,180,128]{2,1,0:T(8,128)(2,1)}), bf16[16,180,128]{2,1,0:T(8,128)(2,1)}, u32[]{:S(2)}, u32[]{:S(2)}) async-start(bf16[16,180,128]{2,1,0:T(8,128)(2,1)} %broadcast_in_dim.91), calls=%async_computation.1 | async-start | bytes 1507328 | tf_op jit(solution)/shard_map/all_to_all | solution.py:45
  73.1 28.1 %copy-start.6 = (f32[128,128]{0,1:T(8,128)}, f32[128,128]{0,1:T(8,128)S(1)}, u32[]{:S(2)}) copy-start(f32[128,128]{0,1:T(8,128)S(1)} %fusion.96) | copy-start | bytes 196612
  73.3 81.4 %copy-start.7 = (bf16[128,1,32]{0,2,1:T(8,128)(2,1)}, bf16[128,1,32]{0,2,1:T(8,128)(2,1)S(1)}, u32[]{:S(2)}) copy-start(bf16[128,1,32]{0,2,1:T(8,128)(2,1)S(1)} %get-tuple-element.498) | copy-start | bytes 24580
  73.3 81.4 %copy-start.9 = (bf16[128,1,32]{0,2,1:T(8,128)(2,1)}, bf16[128,1,32]{0,2,1:T(8,128)(2,1)S(1)}, u32[]{:S(2)}) copy-start(bf16[128,1,32]{0,2,1:T(8,128)(2,1)S(1)} %get-tuple-element.499) | copy-start | bytes 24580
  74.4 25.7 %all-to-all-start.2 = ((bf16[16,128,128]{2,1,0:T(8,128)(2,1)}), bf16[16,128,128]{2,1,0:T(8,128)(2,1)S(1)}, u32[]{:S(2)}, u32[]{:S(2)}) async-start(bf16[16,128,128]{2,1,0:T(8,128)(2,1)} %broadcast_in_dim.92), calls=%async_computation.2 | async-start | bytes 1048576 | tf_op jit(solution)/shard_map/all_to_all | solution.py:45
  154.7 13.6 %copy-start.1 = (bf16[2880,128]{1,0:T(8,128)(2,1)S(1)}, bf16[2880,128]{1,0:T(8,128)(2,1)}, u32[]{:S(2)}) copy-start(bf16[2880,128]{1,0:T(8,128)(2,1)} %fusion.37) | copy-start | bytes 2211844
  197.8 9.1 %copy-start.14 = (s32[512,1]{0,1:T(1,128)S(1)}, s32[512,1]{0,1:T(1,128)}, u32[]{:S(2)}) copy-start(s32[512,1]{0,1:T(1,128)} %mul.228) | copy-start | bytes 6148
  197.8 9.1 %copy-start.15 = (s32[512]{0:T(512)S(1)}, s32[512]{0:T(512)}, u32[]{:S(2)}) copy-start(s32[512]{0:T(512)} %fusion.75) | copy-start | bytes 6148
  202.3 16.5 %all-to-all-start.3 = ((bf16[8,128,360]{1,2,0:T(8,128)(2,1)}), bf16[8,128,360]{1,2,0:T(8,128)(2,1)S(1)}, u32[]{:S(2)}, u32[]{:S(2)}) async-start(bf16[8,128,360]{1,2,0:T(8,128)(2,1)} %bitcast.210), calls=%async_computation.3 | async-start | bytes 1474560 | tf_op jit(solution)/shard_map/all_to_all | solution.py:174
  206.8 92.8 %all-gather.5.cloned.1.call-start = ((), (), s32[]{:S(2)}) async-start(), calls=%async_computation.8 | async-start | bytes 4976640 | tf_op jit(solution)/shard_map/all_gather | solution.py:201
  218.9 2.8 copy-start.3
  247.5 55.5 %copy-start.19 = (f32[2880]{0:T(1024)S(1)}, f32[2880]{0:T(1024)}, u32[]{:S(2)}) copy-start(f32[2880]{0:T(1024)} %param.25) | copy-start | bytes 34564
  299.7 3.6 copy-start.2
  376.4 10.1 %copy-start.17 = (f32[1,128,4]{1,2,0:T(4,128)S(1)}, f32[1,128,4]{1,2,0:T(4,128)}, u32[]{:S(2)}) copy-start(f32[1,128,4]{1,2,0:T(4,128)} %param.29) | copy-start | bytes 6148
  376.4 10.2 %copy-start.8 = (bf16[128,1,32]{0,2,1:T(8,128)(2,1)S(1)}, bf16[128,1,32]{0,2,1:T(8,128)(2,1)}, u32[]{:S(2)}) copy-start(bf16[128,1,32]{0,2,1:T(8,128)(2,1)} %copy-done.7) | copy-start | bytes 24580
  376.4 10.2 %copy-start.10 = (bf16[128,1,32]{0,2,1:T(8,128)(2,1)S(1)}, bf16[128,1,32]{0,2,1:T(8,128)(2,1)}, u32[]{:S(2)}) copy-start(bf16[128,1,32]{0,2,1:T(8,128)(2,1)} %copy-done.9) | copy-start | bytes 24580
  377.5 24.4 %all-to-all-start.6 = ((bf16[16,48,360]{2,1,0:T(8,128)(2,1)}), bf16[16,48,360]{2,1,0:T(8,128)(2,1)S(1)}, u32[]{:S(2)}, u32[]{:S(2)}) async-start(bf16[16,48,360]{2,1,0:T(8,128)(2,1)} %bitcast.42), calls=%async_computation.6 | async-start | bytes 1179648 | tf_op jit(solution)/shard_map/all_to_all | solution.py:222
  403.8 0.9 copy-start.4
Sparse Core Ops, SparseCore 0:
  10.6 131.0 all-gather.2
  247.6 51.9 all-gather.4

commit v5 on v3

--- a/solution.py
+++ b/solution.py
@@ -197,7 +197,10 @@
     outgoing = padded[source_row].reshape(expert_count, capacity, padded.shape[1])
     arrived = lax.all_to_all(outgoing, "expert", split_axis=0, concat_axis=0, tiled=True)
     arrived_rows = arrived.reshape(expert_count * capacity, arrived.shape[2])
-    inputs = rms_norm(lax.all_gather(arrived_rows, "mp", axis=1, tiled=True), moe_gain)
+    sc_rows = 256
+    rows_by_sc = lax.all_gather(arrived_rows[:sc_rows], "mp", axis=1, tiled=True)
+    rows_by_exchange = gather_by_exchange(arrived_rows[sc_rows:].T, "mp").T
+    inputs = rms_norm(jnp.concatenate([rows_by_sc, rows_by_exchange], axis=0), moe_gain)
     w_in = expert_in[0]
     gate_val = jnp.dot(inputs, w_in[0], preferred_element_type=jnp.float32)
     up_val = jnp.dot(inputs, w_in[1], preferred_element_type=jnp.float32)
@@ -209,10 +212,22 @@
     partials_t = lax.dot_general(
         expert_down[0], activated, (((0,), (1,)), ((), ())), preferred_element_type=jnp.float32
     )
-    expert_out_t = lax.psum_scatter(
-        partials_t.astype(jnp.bfloat16), "mp", scatter_dimension=0, tiled=True
-    )
-    local_width = expert_out_t.shape[0]
+    partials_bf = partials_t.astype(jnp.bfloat16)
+    local_width = partials_bf.shape[0] // mp_devs
+    out_by_sc = lax.psum_scatter(
+        partials_bf[:, :sc_rows], "mp", scatter_dimension=0, tiled=True
+    )
+    out_by_exchange = jnp.sum(
+        lax.all_to_all(
+            partials_bf[:, sc_rows:].reshape(mp_devs, local_width, -1),
+            "mp",
+            split_axis=0,
+            concat_axis=0,
+            tiled=True,
+        ).astype(jnp.float32),
+        axis=0,
+    ).astype(jnp.bfloat16)
+    expert_out_t = jnp.concatenate([out_by_sc, out_by_exchange], axis=1)
     expert_out = expert_out_t.T.reshape(expert_count, capacity, local_width)
     returned = lax.all_to_all(expert_out, "expert", split_axis=0, concat_axis=0, tiled=True)
     picked = returned.reshape(expert_count * capacity, local_width)[target].reshape(

time: 390 us -> 408 us (1.046)
  waiting for transfers between devices: 235 us -> 189 us
  blocking collectives: 24.2 us -> 68.8 us
  local copies, waits for them, and re-layouts: 28 us -> 33.6 us
  starting transfers between devices: 34.4 us -> 39.3 us
    reduce_scatter x1, waiting for transfers between devices: 57 us -> 7.82 us  [shards(): lax.psum_scatter(partials_bf[:, :sc_rows], 'mp', scatter_dimension=0, til...]
    all_to_all x0 -> x1, blocking collectives: none -> 44.7 us  [shards(): lax.all_to_all(partials_bf[:, sc_rows:].reshape(mp_devs, local_width, -1)...]
    all_gather x1, waiting for transfers between devices: 52 us -> 59.1 us  [shards(): lax.all_gather(arrived_rows[:sc_rows], 'mp', axis=1, tiled=True)]
    slice x1 -> x6, local copies, waits for them, and re-layouts: 0.22 us -> 5.51 us  [the longest x1 2.62 us: shards(): partials_bf[:, :sc_rows]]
    all_to_all x3 -> x4, starting transfers between devices: 21 us -> 25.4 us  [gather_by_exchange(): lax.all_to_all(spread, axis_name, split_axis=0, concat_axis=0, tiled=True)]
    unnamed x38 -> x32, local copies, waits for them, and re-layouts: 8.77 us -> 8.54 us
    all_to_all x3 -> x4, waiting for transfers between devices: 58.7 us -> 58.6 us  [gather_by_exchange(): lax.all_to_all(spread, axis_name, split_axis=0, concat_axis=0, tiled=True)]
  transfers between devices with their start and end apart: 8 -> 9, of which waited for: 8 -> 8; matrix products, arithmetic and copies ran while one was open for 4% -> 5% of each run, Pallas kernels for 0% -> 0%
where the time goes in v5:
time: 408 us; the launch traced here: 404 us
  waiting for transfers between devices  189 us (46%)
  blocking collectives  68.8 us (17%)
  matrix products  42.7 us (10%)
  starting transfers between devices  39.3 us (10%)
  local copies, waits for them, and re-layouts  33.6 us (8%)
  other arithmetic  15.2 us (4%)
  between operations  14.2 us (3%)
    all_gather x1, waiting for transfers between devices, shards(): lax.all_gather(arrived_rows[:sc_rows], 'mp', axis=1, tiled=True)  59.1 us
    all_to_all x4, waiting for transfers between devices, gather_by_exchange(): lax.all_to_all(spread, axis_name, split_axis=0, concat_axis=0, tiled=True)  58.6 us
    all_to_all x1, blocking collectives, shards(): lax.all_to_all(partials_bf[:, sc_rows:].reshape(mp_devs, local_width, -1)...  44.7 us
    all_gather x1, waiting for transfers between devices, shards(): lax.all_gather(jnp.concatenate([w_query, w_out.T], axis=1), 'expert', axi...  41.8 us
    all_to_all x4, starting transfers between devices, gather_by_exchange(): lax.all_to_all(spread, axis_name, split_axis=0, concat_axis=0, tiled=True)  25.4 us
    all_to_all x1, blocking collectives, shards(): lax.all_to_all(outgoing, 'expert', split_axis=0, concat_axis=0, tiled=True)  24.1 us
    dot_general x8, matrix products, block_scores(): jnp.einsum('hrd,hkd->hrk', query_rows, key_part, preferred_element_type=j...  12.9 us
    all_to_all x1, waiting for transfers between devices, shards(): lax.all_to_all(expert_out, 'expert', split_axis=0, concat_axis=0, tiled=T...  12.2 us
  transfers between devices with their start and end apart: 9, of which 8 were waited for; matrix products, arithmetic and copies ran while one was open for 5% of the time, Pallas kernels for 0%

profile of v5, /device:TPU:1, one launch (start us, length us, event | category | flops | bytes accessed | tf_op | source)
XLA Modules:
  0.0 403.7 jit_solution(14816158368169760713)
XLA Ops:
  7.2 1.9 maximum_bitcast_fusion.1
  9.2 1.9 broadcast_in_dim.96
  11.1 6.0 %all-to-all-start = ((bf16[8,360,128]{2,1,0:T(8,128)(2,1)}), bf16[8,360,128]{2,1,0:T(8,128)(2,1)S(1)}, u32[]{:S(2)}, u32[]{:S(2)}) async-start(bf16[8,360,128]{2,1,0:T(8,128)(2,1)} %broadcast_in_dim.96), calls=%async_computation | async-start | bytes 1474560 | tf_op jit(solution)/shard_map/all_to_all | solution.py:45
  17.2 12.3 %all-to-all-done = bf16[8,360,128]{2,1,0:T(8,128)(2,1)S(1)} async-done(((bf16[8,360,128]{2,1,0:T(8,128)(2,1)}), bf16[8,360,128]{2,1,0:T(8,128)(2,1)S(1)}, u32[]{:S(2)}, u32[]{:S(2)}) %all-to-all-start) | async-done | bytes 737312 | tf_op jit(solution)/shard_map/all_to_all | solution.py:45
  29.5 1.0 broadcast_in_dim.97
  30.5 10.7 %all-to-all-start.1 = ((bf16[16,180,128]{2,1,0:T(8,128)(2,1)}), bf16[16,180,128]{2,1,0:T(8,128)(2,1)}, u32[]{:S(2)}, u32[]{:S(2)}) async-start(bf16[16,180,128]{2,1,0:T(8,128)(2,1)} %broadcast_in_dim.97), calls=%async_computation.1 | async-start | bytes 1507328 | tf_op jit(solution)/shard_map/all_to_all | solution.py:45
  41.8 0.4 fusion.39
  42.3 1.4 fusion.41
  43.7 26.2 %all-to-all-done.1 = bf16[16,180,128]{2,1,0:T(8,128)(2,1)} async-done(((bf16[16,180,128]{2,1,0:T(8,128)(2,1)}), bf16[16,180,128]{2,1,0:T(8,128)(2,1)}, u32[]{:S(2)}, u32[]{:S(2)}) %all-to-all-start.1) | async-done | bytes 737312 | tf_op jit(solution)/shard_map/all_to_all | solution.py:45
  69.9 1.2 reshape.387
  71.1 1.6 fusion.96
  73.0 0.9 broadcast_in_dim.98
  73.9 4.3 %all-to-all-start.2 = ((bf16[16,128,128]{2,1,0:T(8,128)(2,1)}), bf16[16,128,128]{2,1,0:T(8,128)(2,1)S(1)}, u32[]{:S(2)}, u32[]{:S(2)}) async-start(bf16[16,128,128]{2,1,0:T(8,128)(2,1)} %broadcast_in_dim.98), calls=%async_computation.2 | async-start | bytes 1048576 | tf_op jit(solution)/shard_map/all_to_all | solution.py:45
  78.5 1.2 reduce-window.6
  79.6 0.2 slice_reduce_fusion
  80.1 20.1 %all-to-all-done.2 = bf16[16,128,128]{2,1,0:T(8,128)(2,1)S(1)} async-done(((bf16[16,128,128]{2,1,0:T(8,128)(2,1)}), bf16[16,128,128]{2,1,0:T(8,128)(2,1)S(1)}, u32[]{:S(2)}, u32[]{:S(2)}) %all-to-all-start.2) | async-done | bytes 524320 | tf_op jit(solution)/shard_map/all_to_all | solution.py:45
  100.2 1.2 slice_bitcast_fusion
  101.4 41.8 %all-gather.6.cloned.1.call-done = bf16[16,180,1024]{2,1,0:T(8,128)(2,1)} async-done(((bf16[1,180,1024]{2,1,0:T(8,128)(2,1)}), bf16[16,180,1024]{2,1,0:T(8,128)(2,1)}) %all-gather.6.cloned.1.call-update) | async-done | bytes 5898256 | tf_op jit(solution)/shard_map/all_gather | solution.py:86
  143.3 8.0 %reshape.430 = bf16[2880,1024]{1,0:T(8,128)(2,1)} reshape(bf16[16,180,1024]{2,1,0:T(8,128)(2,1)} %all-gather.6.cloned.1.call-done) | data formatting | bytes 11796480
  151.3 3.1 fusion.29
  154.7 6.6 %while.30 = (s32[]{:T(128)}, f32[1,1024]{1,0:T(1,128)S(1)}, s32[2048]{0:T(1024)S(1)}, bf16[1,2048,64]{2,1,0:T(8,128)(2,1)}, bf16[1,1024,64]{2,1,0:T(8,128)(2,1)S...) while((s32[]{:T(128)}, f32[1,1024]{1,0:T(1,128)S(1)}, ...), condition=%wide.region_3.4_spmd.clone, body=%wide.region_1.3_spmd.clone.sunk | while | flops 70255112 | bytes 306343 | solution.py:145
  154.8 1.5 fusion.111
  156.4 1.5 fusion.111
  158.1 1.5 fusion.111
  159.7 1.5 fusion.111
  161.3 12.6 %while.31 = (s32[]{:T(128)}, f32[1,1024,64]{1,2,0:T(8,128)S(1)}, f32[1,1024]{1,0:T(1,128)S(1)}, s32[2048]{0:T(1024)S(1)}, bf16[1,2048,64]{2,1,0:T(8,128)(2,1)}, ...) while((s32[]{:T(128)}, f32[1,1024,64]{1,2,0:T(8,128)S(1)}, ...), condition=%wide.region_6.7_spmd.clone, body=%wide.region_4.6_spmd.clone.sunk | while | flops 139068928 | bytes 3062998 | solution.py:161
  161.4 1.7 convert_reduce_fusion.3
  163.1 1.3 fusion.114
  164.5 1.7 convert_reduce_fusion.3
  166.3 1.3 fusion.114
  167.7 1.7 convert_reduce_fusion.3
  169.4 1.3 fusion.114
  170.9 1.7 convert_reduce_fusion.3
  172.6 1.3 fusion.114
  174.0 3.6 convolution_convert_fusion.1
  177.7 4.2 %all-to-all-start.3 = ((bf16[8,128,360]{1,2,0:T(8,128)(2,1)}), bf16[8,128,360]{1,2,0:T(8,128)(2,1)S(1)}, u32[]{:S(2)}, u32[]{:S(2)}) async-start(bf16[8,128,360]{1,2,0:T(8,128)(2,1)} %bitcast.204), calls=%async_computation.3 | async-start | bytes 1474560 | tf_op jit(solution)/shard_map/all_to_all | solution.py:174
  182.0 2.4 scatter_custom_fusion
  184.5 9.8 %all-to-all-done.3 = bf16[8,128,360]{1,2,0:T(8,128)(2,1)S(1)} async-done(((bf16[8,128,360]{1,2,0:T(8,128)(2,1)}), bf16[8,128,360]{1,2,0:T(8,128)(2,1)S(1)}, u32[]{:S(2)}, u32[]{:S(2)}) %all-to-all-start.3) | async-done | bytes 737312 | tf_op jit(solution)/shard_map/all_to_all | solution.py:174
  194.6 2.6 gather_fusion
  197.2 24.1 %all_to_all.40 = bf16[16,48,360]{2,1,0:T(8,128)(2,1)S(1)} all-to-all(bf16[16,48,360]{2,1,0:T(8,128)(2,1)S(1)} %bitcast.200), channel_id=1, replica_groups=mesh['expert'=16,'mp'=8,'batch'=2] {'expert'}, dimensions={0} | all-to-all | bytes 1105920 | tf_op jit(solution)/shard_map/all_to_all | solution.py:198
  221.6 0.8 copy.129
  222.4 1.8 broadcast_in_dim.103
  224.2 4.4 %all-to-all-start.5 = ((bf16[8,360,512]{2,1,0:T(8,128)(2,1)}), bf16[8,360,512]{2,1,0:T(8,128)(2,1)}, u32[]{:S(2)}, u32[]{:S(2)}) async-start(bf16[8,360,512]{2,1,0:T(8,128)(2,1)} %broadcast_in_dim.103), calls=%async_computation.5 | async-start | bytes 5898240 | tf_op jit(solution)/shard_map/all_to_all | solution.py:45
  228.6 0.2 reduce-scatter.2.cloned.1.call-start
  228.9 59.1 %all-gather.4.cloned.1.call-done = bf16[256,2880]{0,1:T(8,128)(2,1)} async-done(((bf16[256,360]{0,1:T(8,128)(2,1)}), bf16[256,2880]{0,1:T(8,128)(2,1)}) %all-gather.4.cloned.1.call-update) | async-done | bytes 1474576 | tf_op jit(solution)/shard_map/all_gather | solution.py:201
  288.0 3.3 fusion.25
  291.3 5.6 %fusion.42 = f32[768,360]{0,1:T(8,128)} fusion(bf16[1,2,2880,360]{2,3,1,0:T(8,128)(2,1)} %param.26, f32[2880]{0:T(1024)S(1)} %copy-done.12, f32[768]{0:T(1024)S(1)} %add_rsqrt_fusion, bf16[512,2880]{0,1:T(8,128)(2,1)} %bitcast.33, bf16[256,2880]{0,1:T(8,128)(2,1)S(1)} %copy-done.2), kind=kOutput, calls=%fused_computation.60 | convolution fusion | flops 1608284160 | bytes 7663872 | tf_op jit(solution)/shard_map/dot_general | solution.py:205
  296.9 10.7 %fusion.28 = bf16[2880,768]{1,0:T(8,128)(2,1)} fusion(bf16[1,360,2880]{2,1,0:T(8,128)(2,1)S(1)} %copy-done, f32[768,360]{0,1:T(8,128)} %fusion.42, bf16[1,2,2880,360]{2,3,1,0:T(8,128)(2,1)} %param.26, f32[2880]{0:T(1024)S(1)} %copy-done.12, f32[768]{0:T(1024)S(1)} %add_rsqrt_fusion, bf16[512,2880]{0,1:T(8,128)(2,1)} %bitcast.33, ...), kind=kOutput, calls=%fused_computation.41 | convolution fusion | flops 3205232640 | bytes 14161152 | tf_op jit(solution)/shard_map/dot_general | solution.py:212
  307.6 2.6 slice.92
  310.3 1.8 slice-done
  312.1 44.7 %all_to_all.41 = bf16[8,360,512]{2,1,0:T(8,128)(2,1)} all-to-all(bf16[8,360,512]{2,1,0:T(8,128)(2,1)S(1)} %bitcast.198), channel_id=1, replica_groups=mesh['expert'=16,'mp'=8,'batch'=2] {'mp'}, dimensions={0} | all-to-all | bytes 5898240 | tf_op jit(solution)/shard_map/all_to_all | solution.py:221
  356.8 2.4 reduce_sum.82
  359.3 7.8 %reduce-scatter.2.cloned.1.call-done = bf16[360,256]{1,0:T(8,128)(2,1)} async-done(((bf16[2880,256]{1,0:T(8,128)(2,1)}), bf16[360,256]{1,0:T(8,128)(2,1)}) %reduce-scatter.2.cloned.1.call-update) | async-done | bytes 184336 | tf_op jit(solution)/shard_map/reduce_scatter | solution.py:217
  367.1 1.0 maximum_bitcast_fusion
  368.1 1.1 copy.131
  369.1 9.4 %all-to-all-start.7 = ((bf16[16,48,360]{2,1,0:T(8,128)(2,1)}), bf16[16,48,360]{2,1,0:T(8,128)(2,1)S(1)}, u32[]{:S(2)}, u32[]{:S(2)}) async-start(bf16[16,48,360]{2,1,0:T(8,128)(2,1)} %bitcast.40), calls=%async_computation.8 | async-start | bytes 1179648 | tf_op jit(solution)/shard_map/all_to_all | solution.py:232
  378.5 0.7 copy.132
  379.3 0.6 pad_maximum_fusion.3
  379.9 0.6 slice_bitcast_fusion.4
  380.5 12.2 %all-to-all-done.7 = bf16[16,48,360]{2,1,0:T(8,128)(2,1)S(1)} async-done(((bf16[16,48,360]{2,1,0:T(8,128)(2,1)}), bf16[16,48,360]{2,1,0:T(8,128)(2,1)S(1)}, u32[]{:S(2)}, u32[]{:S(2)}) %all-to-all-start.7) | async-done | bytes 552992 | tf_op jit(solution)/shard_map/all_to_all | solution.py:232
  392.7 1.9 gather_fusion.1
  394.6 0.2 reshape.403
  394.9 0.6 multiply_reduce_fusion
  395.6 1.6 fusion.66
  (113 shorter events, 3.4 us)
Async XLA Ops:
  7.2 289.8 %copy-start = (bf16[1,360,2880]{2,1,0:T(8,128)(2,1)S(1)}, bf16[1,360,2880]{2,1,0:T(8,128)(2,1)}, u32[]{:S(2)}) copy-start(bf16[1,360,2880]{2,1,0:T(8,128)(2,1)} %param.27) | copy-start | bytes 6220804
  7.2 9.9 %copy-start.6 = (bf16[180,64]{0,1:T(8,128)(2,1)S(1)}, bf16[180,64]{0,1:T(8,128)(2,1)}, u32[]{:S(2)}) copy-start(bf16[180,64]{0,1:T(8,128)(2,1)} %param.22) | copy-start | bytes 69124
  7.2 9.9 %copy-start.7 = (bf16[180,64]{0,1:T(8,128)(2,1)S(1)}, bf16[180,64]{0,1:T(8,128)(2,1)}, u32[]{:S(2)}) copy-start(bf16[180,64]{0,1:T(8,128)(2,1)} %param.21) | copy-start | bytes 69124
  7.2 136.1 %all-gather.6.cloned.1.call-start = ((), (), s32[]{:S(2)}) async-start(), calls=%async_computation.11 | async-start | bytes 6406144 | tf_op jit(solution)/shard_map/all_gather | solution.py:86
  11.1 30.1 %copy-start.9 = (s32[1,128,4]{1,2,0:T(4,128)S(1)}, s32[1,128,4]{1,2,0:T(4,128)}, u32[]{:S(2)}) copy-start(s32[1,128,4]{1,2,0:T(4,128)} %param.28) | copy-start | bytes 6148
  11.1 30.5 %copy-start.3 = (bf16[1,128,360]{1,2,0:T(8,128)(2,1)S(1)}, bf16[1,128,360]{1,2,0:T(8,128)(2,1)}, u32[]{:S(2)}) copy-start(bf16[1,128,360]{1,2,0:T(8,128)(2,1)} %param.17) | copy-start | bytes 276484
  11.1 30.6 %copy-start.11 = (f32[8]{0:T(128)S(1)}, f32[8]{0:T(128)}, u32[]{:S(2)}) copy-start(f32[8]{0:T(128)} %param.24) | copy-start | bytes 100
  11.1 18.5 %all-to-all-start = ((bf16[8,360,128]{2,1,0:T(8,128)(2,1)}), bf16[8,360,128]{2,1,0:T(8,128)(2,1)S(1)}, u32[]{:S(2)}, u32[]{:S(2)}) async-start(bf16[8,360,128]{2,1,0:T(8,128)(2,1)} %broadcast_in_dim.96), calls=%async_computation | async-start | bytes 1474560 | tf_op jit(solution)/shard_map/all_to_all | solution.py:45
  17.1 25.2 %copy-start.8 = (f32[2880]{0:T(1024)S(1)}, f32[2880]{0:T(1024)}, u32[]{:S(2)}) copy-start(f32[2880]{0:T(1024)} %param.19) | copy-start | bytes 34564
  30.5 39.4 %all-to-all-start.1 = ((bf16[16,180,128]{2,1,0:T(8,128)(2,1)}), bf16[16,180,128]{2,1,0:T(8,128)(2,1)}, u32[]{:S(2)}, u32[]{:S(2)}) async-start(bf16[16,180,128]{2,1,0:T(8,128)(2,1)} %broadcast_in_dim.97), calls=%async_computation.1 | async-start | bytes 1507328 | tf_op jit(solution)/shard_map/all_to_all | solution.py:45
  71.1 8.8 %copy-start.5 = (s32[1,2048]{1,0:T(1,128)S(1)}, s32[1,2048]{1,0:T(1,128)}, u32[]{:S(2)}) copy-start(s32[1,2048]{1,0:T(1,128)} %param.18) | copy-start | bytes 24580
  73.9 26.3 %all-to-all-start.2 = ((bf16[16,128,128]{2,1,0:T(8,128)(2,1)}), bf16[16,128,128]{2,1,0:T(8,128)(2,1)S(1)}, u32[]{:S(2)}, u32[]{:S(2)}) async-start(bf16[16,128,128]{2,1,0:T(8,128)(2,1)} %broadcast_in_dim.98), calls=%async_computation.2 | async-start | bytes 1048576 | tf_op jit(solution)/shard_map/all_to_all | solution.py:45
  101.4 49.9 %copy-start.1 = (bf16[2880,128]{1,0:T(8,128)(2,1)S(1)}, bf16[2880,128]{1,0:T(8,128)(2,1)}, u32[]{:S(2)}) copy-start(bf16[2880,128]{1,0:T(8,128)(2,1)} %fusion.41) | copy-start | bytes 2211844
  177.7 16.6 %all-to-all-start.3 = ((bf16[8,128,360]{1,2,0:T(8,128)(2,1)}), bf16[8,128,360]{1,2,0:T(8,128)(2,1)S(1)}, u32[]{:S(2)}, u32[]{:S(2)}) async-start(bf16[8,128,360]{1,2,0:T(8,128)(2,1)} %bitcast.204), calls=%async_computation.3 | async-start | bytes 1474560 | tf_op jit(solution)/shard_map/all_to_all | solution.py:174
  181.9 106.0 %all-gather.4.cloned.1.call-start = ((), (), s32[]{:S(2)}) async-start(), calls=%async_computation.9 | async-start | bytes 1658880 | tf_op jit(solution)/shard_map/all_gather | solution.py:201
  224.2 63.8 %all-to-all-start.5 = ((bf16[8,360,512]{2,1,0:T(8,128)(2,1)}), bf16[8,360,512]{2,1,0:T(8,128)(2,1)}, u32[]{:S(2)}, u32[]{:S(2)}) async-start(bf16[8,360,512]{2,1,0:T(8,128)(2,1)} %broadcast_in_dim.103), calls=%async_computation.5 | async-start | bytes 5898240 | tf_op jit(solution)/shard_map/all_to_all | solution.py:45
  228.6 138.5 %reduce-scatter.2.cloned.1.call-start = ((), (), s32[]{:S(2)}) async-start(), calls=%async_computation.10 | async-start | bytes 1658880 | tf_op jit(solution)/shard_map/reduce_scatter | solution.py:217
  288.0 3.3 copy-start.2
  288.0 3.3 copy-start.12
  310.3 1.8 slice-start
  359.3 19.3 %copy-start.10 = (f32[1,128,4]{1,2,0:T(4,128)S(1)}, f32[1,128,4]{1,2,0:T(4,128)}, u32[]{:S(2)}) copy-start(f32[1,128,4]{1,2,0:T(4,128)} %param.29) | copy-start | bytes 6148
  369.1 23.6 %all-to-all-start.7 = ((bf16[16,48,360]{2,1,0:T(8,128)(2,1)}), bf16[16,48,360]{2,1,0:T(8,128)(2,1)S(1)}, u32[]{:S(2)}, u32[]{:S(2)}) async-start(bf16[16,48,360]{2,1,0:T(8,128)(2,1)} %bitcast.40), calls=%async_computation.8 | async-start | bytes 1179648 | tf_op jit(solution)/shard_map/all_to_all | solution.py:232
  392.7 2.2 copy-start.4
Sparse Core Ops, SparseCore 0:
  10.6 132.6 all-gather.5
  222.5 65.3 all-gather.3
  310.4 56.6 reduce-scatter.1

commit v6 on v3

--- a/solution.py
+++ b/solution.py
@@ -83,13 +83,16 @@
     input_normalised = rms_norm(whole_rows, attn_gain)
     query_cols = w_query.shape[1]
     kv_cols = key_weight.shape[1]
-    big_weights = lax.all_gather(
-        jnp.concatenate([w_query, w_out.T], axis=1), "expert", axis=0, tiled=True
-    )
-    query_weight = big_weights[:, :query_cols]
-    out_weight_t = big_weights[:, query_cols:]
+    big_weights = lax.all_gather(jnp.concatenate([w_query, w_out.T], axis=1), "expert", axis=0)
+    query_weight = big_weights[:, :, :query_cols]
+    out_weight_t = big_weights[:, :, query_cols:]
     kv_weight = gather_by_exchange(jnp.concatenate([key_weight, value_weight], axis=1), "expert")
-    query_raw = jnp.dot(input_normalised, query_weight, preferred_element_type=jnp.float32)
+    query_raw = jnp.einsum(
+        "tef,efc->tc",
+        input_normalised.reshape(tok_count, expert_devs, -1),
+        query_weight,
+        preferred_element_type=jnp.float32,
+    )
     kv_raw = jnp.dot(input_normalised, kv_weight, preferred_element_type=jnp.float32)
     key_raw = kv_raw[:, :kv_cols]
     value_raw = kv_raw[:, kv_cols:]
@@ -166,9 +169,9 @@
         .transpose(2, 0, 1, 3)
         .reshape(tok_count, query_cols)
     )
-    out_terms = lax.dot_general(
-        mixed, out_weight_t, (((1,), (1,)), ((), ())), preferred_element_type=jnp.float32
-    )
+    out_terms = jnp.einsum(
+        "tc,efc->tef", mixed, out_weight_t, preferred_element_type=jnp.float32
+    ).reshape(tok_count, -1)
     model_width = out_terms.shape[1]
     out_pieces = out_terms.astype(jnp.bfloat16).reshape(tok_count, mp_devs, model_width // mp_devs)
     out_got = lax.all_to_all(
@@ -206,14 +209,16 @@
     activated = ((up_val + 1.0) * gate_val * jax.nn.sigmoid(glu_alpha * gate_val)).astype(
         jnp.bfloat16
     )
-    partials_t = lax.dot_general(
-        expert_down[0], activated, (((0,), (1,)), ((), ())), preferred_element_type=jnp.float32
-    )
-    expert_out_t = lax.psum_scatter(
-        partials_t.astype(jnp.bfloat16), "mp", scatter_dimension=0, tiled=True
-    )
-    local_width = expert_out_t.shape[0]
-    expert_out = expert_out_t.T.reshape(expert_count, capacity, local_width)
+    partials = jnp.einsum(
+        "rh,hjf->jrf",
+        activated,
+        expert_down[0].reshape(expert_down.shape[1], mp_devs, -1),
+        preferred_element_type=jnp.float32,
+    )
+    expert_out = lax.psum_scatter(
+        partials.astype(jnp.bfloat16), "mp", scatter_dimension=0, tiled=True
+    ).reshape(expert_count, capacity, -1)
+    local_width = expert_out.shape[2]
     returned = lax.all_to_all(expert_out, "expert", split_axis=0, concat_axis=0, tiled=True)
     picked = returned.reshape(expert_count * capacity, local_width)[target].reshape(
         tok_count, top_count, local_width

time: 390 us -> 388 us (level)
  local copies, waits for them, and re-layouts: 28 us -> 38.3 us
  matrix products: 40.8 us -> 34.4 us
    dot_general x8, matrix products: 13 us -> 5.72 us  [block_scores(): jnp.einsum('hrd,hkd->hrk', query_rows, key_part, preferred_element_type=j...]
    all_to_all x3, waiting for transfers between devices: 58.7 us -> 52.1 us  [gather_by_exchange(): lax.all_to_all(spread, axis_name, split_axis=0, concat_axis=0, tiled=True)]
    all_gather x1, waiting for transfers between devices: 41.8 us -> 48.3 us  [shards(): lax.all_gather(jnp.concatenate([w_query, w_out.T], axis=1), 'expert', axi...]
    slice x1 -> x2, local copies, waits for them, and re-layouts: 0.22 us -> 5.17 us  [the longest x1 4.96 us: shards(): query_weight = big_weights[:, :, :query_cols]]
    unnamed x38 -> x46, local copies, waits for them, and re-layouts: 8.77 us -> 6.37 us
  transfers between devices with their start and end apart: 8 -> 8, of which waited for: 8 -> 8; matrix products, arithmetic and copies ran while one was open for 4% -> 5% of each run, Pallas kernels for 0% -> 0%
where the time goes in v6:
time: 388 us; the launch traced here: 387 us
  waiting for transfers between devices  232 us (60%)
  local copies, waits for them, and re-layouts  38.3 us (10%)
  matrix products  34.4 us (9%)
  starting transfers between devices  33.5 us (9%)
  blocking collectives  22.9 us (6%)
  between operations  14.3 us (4%)
  other arithmetic  11.1 us (3%)
    reduce_scatter x1, waiting for transfers between devices, shards(): lax.psum_scatter(partials.astype(jnp.bfloat16), 'mp', scatter_dimension=0...  57 us
    all_to_all x3, waiting for transfers between devices, gather_by_exchange(): lax.all_to_all(spread, axis_name, split_axis=0, concat_axis=0, tiled=True)  52.1 us
    all_gather x1, waiting for transfers between devices, shards(): lax.all_gather(arrived_rows, 'mp', axis=1, tiled=True)  48.8 us
    all_gather x1, waiting for transfers between devices, shards(): lax.all_gather(jnp.concatenate([w_query, w_out.T], axis=1), 'expert', axi...  48.3 us
    all_to_all x1, blocking collectives, shards(): lax.all_to_all(outgoing, 'expert', split_axis=0, concat_axis=0, tiled=True)  22.9 us
    all_to_all x3, starting transfers between devices, gather_by_exchange(): lax.all_to_all(spread, axis_name, split_axis=0, concat_axis=0, tiled=True)  20.6 us
    all_to_all x1, waiting for transfers between devices, shards(): lax.all_to_all(expert_out, 'expert', split_axis=0, concat_axis=0, tiled=T...  16 us
    dot_general x1, matrix products, shards(): jnp.einsum('rh,hjf->jrf', activated, expert_down[0].reshape(expert_down.s...  10.7 us
  transfers between devices with their start and end apart: 8, of which 8 were waited for; matrix products, arithmetic and copies ran while one was open for 5% of the time, Pallas kernels for 0%

profile of v6, /device:TPU:1, one launch (start us, length us, event | category | flops | bytes accessed | tf_op | source)
XLA Modules:
  0.0 386.8 jit_solution(10226617767321910699)
XLA Ops:
  7.2 1.8 maximum_bitcast_fusion
  9.1 1.9 broadcast_in_dim.90
  10.9 6.0 %all-to-all-start = ((bf16[8,360,128]{2,1,0:T(8,128)(2,1)}), bf16[8,360,128]{2,1,0:T(8,128)(2,1)S(1)}, u32[]{:S(2)}, u32[]{:S(2)}) async-start(bf16[8,360,128]{2,1,0:T(8,128)(2,1)} %broadcast_in_dim.90), calls=%async_computation | async-start | bytes 1474560 | tf_op jit(solution)/shard_map/all_to_all | solution.py:45
  17.1 12.3 %all-to-all-done = bf16[8,360,128]{2,1,0:T(8,128)(2,1)S(1)} async-done(((bf16[8,360,128]{2,1,0:T(8,128)(2,1)}), bf16[8,360,128]{2,1,0:T(8,128)(2,1)S(1)}, u32[]{:S(2)}, u32[]{:S(2)}) %all-to-all-start) | async-done | bytes 737312 | tf_op jit(solution)/shard_map/all_to_all | solution.py:45
  29.4 1.0 broadcast_in_dim.91
  30.4 10.6 %all-to-all-start.1 = ((bf16[16,180,128]{2,1,0:T(8,128)(2,1)}), bf16[16,180,128]{2,1,0:T(8,128)(2,1)S(1)}, u32[]{:S(2)}, u32[]{:S(2)}) async-start(bf16[16,180,128]{2,1,0:T(8,128)(2,1)} %broadcast_in_dim.91), calls=%async_computation.1 | async-start | bytes 1507328 | tf_op jit(solution)/shard_map/all_to_all | solution.py:45
  41.6 0.4 fusion.36
  42.1 0.4 fusion.38
  42.5 27.3 %all-to-all-done.1 = bf16[16,180,128]{2,1,0:T(8,128)(2,1)S(1)} async-done(((bf16[16,180,128]{2,1,0:T(8,128)(2,1)}), bf16[16,180,128]{2,1,0:T(8,128)(2,1)S(1)}, u32[]{:S(2)}, u32[]{:S(2)}) %all-to-all-start.1) | async-done | bytes 737312 | tf_op jit(solution)/shard_map/all_to_all | solution.py:45
  69.9 0.4 fusion.100
  70.7 0.9 broadcast_in_dim.92
  71.6 4.0 %all-to-all-start.2 = ((bf16[16,128,128]{2,1,0:T(8,128)(2,1)}), bf16[16,128,128]{2,1,0:T(8,128)(2,1)S(1)}, u32[]{:S(2)}, u32[]{:S(2)}) async-start(bf16[16,128,128]{2,1,0:T(8,128)(2,1)} %broadcast_in_dim.92), calls=%async_computation.2 | async-start | bytes 1048576 | tf_op jit(solution)/shard_map/all_to_all | solution.py:45
  75.7 0.7 mul.228
  76.4 1.1 reduce-window.6
  77.6 0.2 slice_reduce_fusion
  77.8 1.2 dynamic-slice_bitcast_fusion
  79.0 0.7 fusion.79
  79.7 0.8 multiply_cosine_fusion
  80.5 1.0 reshape.433
  81.4 12.6 %all-to-all-done.2 = bf16[16,128,128]{2,1,0:T(8,128)(2,1)S(1)} async-done(((bf16[16,128,128]{2,1,0:T(8,128)(2,1)}), bf16[16,128,128]{2,1,0:T(8,128)(2,1)S(1)}, u32[]{:S(2)}, u32[]{:S(2)}) %all-to-all-start.2) | async-done | bytes 524320 | tf_op jit(solution)/shard_map/all_to_all | solution.py:45
  94.0 1.2 slice_bitcast_fusion
  95.2 48.3 %all-gather.7.cloned.1.call-done = bf16[16,180,1024]{2,1,0:T(8,128)(2,1)} async-done(((bf16[1,180,1024]{2,1,0:T(8,128)(2,1)}), bf16[16,180,1024]{2,1,0:T(8,128)(2,1)}) %all-gather.7.cloned.1.call-update) | async-done | bytes 5898256 | tf_op jit(solution)/shard_map/all_gather | solution.py:86
  143.5 5.0 %fusion.99 = (bf16[16,180,512]{2,1,0:T(8,128)(2,1)S(1)}, bf16[16,180,512]{2,1,0:T(8,128)(2,1)}) fusion(bf16[16,180,1024]{2,1,0:T(8,128)(2,1)} %all-gather.7.cloned.1.call-done), kind=kLoop, calls=%fused_computation.132 | loop fusion | bytes 11796480 | tf_op jit(solution)/shard_map/slice | solution.py:87
  148.4 5.6 %copy.127 = bf16[16,180,512]{1,0,2:T(8,128)(2,1)} copy(bf16[16,180,512]{2,1,0:T(8,128)(2,1)S(1)} %get-tuple-element.492) | data formatting | bytes 5898240
  154.1 6.1 %fusion.64 = f32[128,8,64]{0,2,1:T(8,128)S(1)} fusion(bf16[128,16,180,1]{0,2,1,3:T(8,128)(2,1)} %reshape.433, bf16[8,64,16,180]{3,2,1,0:T(8,128)(2,1)} %bitcast.208), kind=kOutput, calls=%fused_computation.63 | convolution fusion | flops 377487360 | bytes 3948544 | tf_op jit(solution)/shard_map/tef,efc->tc/dot_general | solution.py:90
  160.5 2.9 while.30
  160.6 0.6 fusion.117
  161.3 0.6 fusion.117
  162.0 0.6 fusion.117
  162.8 0.6 fusion.117
  163.4 9.0 %while.31 = (s32[]{:T(128)}, f32[1,1024,64]{1,2,0:T(8,128)S(1)}, f32[1,1024]{1,0:T(1,128)S(1)}, s32[2048]{0:T(1024)S(1)}, bf16[1,2048,64]{2,1,0:T(8,128)(2,1)S(1...) while((s32[]{:T(128)}, f32[1,1024,64]{1,2,0:T(8,128)S(1)}, ...), condition=%wide.region_6.7_spmd.clone, body=%wide.region_4.6_spmd.clone.sunk | while | flops 139068928 | bytes 3194070 | solution.py:164
  163.5 0.8 convert_reduce_fusion.3
  164.4 1.3 fusion.120
  165.8 0.8 convert_reduce_fusion.3
  166.6 1.3 fusion.120
  168.0 0.8 convert_reduce_fusion.3
  168.9 1.3 fusion.120
  170.3 0.8 convert_reduce_fusion.3
  171.1 1.3 fusion.120
  172.6 2.8 dot_general.45
  175.4 1.8 convolution_convert_fusion
  177.2 3.5 all-to-all-start.3
  180.8 0.2 all-gather.5.cloned.1.call-start
  181.0 2.4 scatter_custom_fusion
  183.5 9.7 %all-to-all-done.3 = bf16[8,128,360]{1,2,0:T(8,128)(2,1)S(1)} async-done(((bf16[8,128,360]{1,2,0:T(8,128)(2,1)}), bf16[8,128,360]{1,2,0:T(8,128)(2,1)S(1)}, u32[]{:S(2)}, u32[]{:S(2)}) %all-to-all-start.3) | async-done | bytes 737312 | tf_op jit(solution)/shard_map/all_to_all | solution.py:177
  193.4 2.6 gather_fusion
  196.1 22.9 %all_to_all.30 = bf16[16,48,360]{2,1,0:T(8,128)(2,1)S(1)} all-to-all(bf16[16,48,360]{2,1,0:T(8,128)(2,1)S(1)} %bitcast.209), channel_id=1, replica_groups=mesh['expert'=16,'mp'=8,'batch'=2] {'expert'}, dimensions={0} | all-to-all | bytes 1105920 | tf_op jit(solution)/shard_map/all_to_all | solution.py:201
  218.9 1.1 copy.117
  220.1 3.4 copy.124
  223.5 48.8 %all-gather.5.cloned.1.call-done = bf16[768,2880]{0,1:T(8,128)(2,1)} async-done(((bf16[768,360]{0,1:T(8,128)(2,1)}), bf16[768,2880]{0,1:T(8,128)(2,1)}) %all-gather.5.cloned.1.call-update) | async-done | bytes 4423696 | tf_op jit(solution)/shard_map/all_gather | solution.py:203
  272.3 3.3 fusion.25
  275.7 0.2 copy-done
  275.9 4.7 %fusion.39 = f32[768,360]{0,1:T(8,128)} fusion(bf16[1,2,2880,360]{2,3,1,0:T(8,128)(2,1)} %param.26, bf16[768,2880]{0,1:T(8,128)(2,1)S(1)} %copy-done, f32[2880]{0:T(1024)S(1)} %copy-done.19, f32[768]{0:T(1024)S(1)} %add_rsqrt_fusion), kind=kOutput, calls=%fused_computation.56 | convolution fusion | flops 1601648640 | bytes 7663872 | tf_op jit(solution)/shard_map/dot_general | solution.py:205
  280.5 10.7 %convert_bitcast_fusion = bf16[8,768,360]{1,2,0:T(8,128)(2,1)} fusion(bf16[360,8,360]{0,2,1:T(8,128)(2,1)S(1)} %bitcast.211, f32[768,360]{0,1:T(8,128)} %fusion.39, bf16[1,2,2880,360]{2,3,1,0:T(8,128)(2,1)} %param.26, bf16[768,2880]{0,1:T(8,128)(2,1)} %all-gather.5.cloned.1.call-done, f32[2880]{0:T(1024)S(1)} %copy-done.19, f32[768]{0:T(1024)S(1)} %add_rsqrt_fusion), kind=kOutput, calls=%fused_computation.40 | convolution fusion | flops 3198597120 | bytes 14161152 | tf_op jit(solution)/shard_map/rh,hjf->jrf/dot_general | solution.py:212
  291.3 57.0 %reduce-scatter.2.cloned.1.call-done = bf16[1,768,360]{1,2,0:T(8,128)(2,1)} async-done(((bf16[8,768,360]{1,2,0:T(8,128)(2,1)}), bf16[1,768,360]{1,2,0:T(8,128)(2,1)}) %reduce-scatter.2.cloned.1.call-update) | async-done | bytes 552976 | tf_op jit(solution)/shard_map/reduce_scatter | solution.py:218
  348.3 2.1 copy.119
  350.4 9.0 %all-to-all-start.5 = ((bf16[16,48,360]{2,1,0:T(8,128)(2,1)}), bf16[16,48,360]{2,1,0:T(8,128)(2,1)S(1)}, u32[]{:S(2)}, u32[]{:S(2)}) async-start(bf16[16,48,360]{2,1,0:T(8,128)(2,1)} %bitcast.41), calls=%async_computation.6 | async-start | bytes 1179648 | tf_op jit(solution)/shard_map/all_to_all | solution.py:222
  359.6 0.6 pad_maximum_fusion.2
  360.2 0.6 slice_bitcast_fusion.3
  360.8 16.0 %all-to-all-done.5 = bf16[16,48,360]{2,1,0:T(8,128)(2,1)S(1)} async-done(((bf16[16,48,360]{2,1,0:T(8,128)(2,1)}), bf16[16,48,360]{2,1,0:T(8,128)(2,1)S(1)}, u32[]{:S(2)}, u32[]{:S(2)}) %all-to-all-start.5) | async-done | bytes 552992 | tf_op jit(solution)/shard_map/all_to_all | solution.py:222
  376.8 1.9 gather_fusion.1
  378.7 0.2 reshape.398
  378.9 0.6 multiply_reduce_fusion
  379.6 0.7 fusion.72
  (119 shorter events, 3.1 us)
Async XLA Ops:
  7.2 9.8 %copy-start.11 = (bf16[180,64]{0,1:T(8,128)(2,1)S(1)}, bf16[180,64]{0,1:T(8,128)(2,1)}, u32[]{:S(2)}) copy-start(bf16[180,64]{0,1:T(8,128)(2,1)} %param.22) | copy-start | bytes 69124
  7.2 9.8 %copy-start.12 = (bf16[180,64]{0,1:T(8,128)(2,1)S(1)}, bf16[180,64]{0,1:T(8,128)(2,1)}, u32[]{:S(2)}) copy-start(bf16[180,64]{0,1:T(8,128)(2,1)} %param.21) | copy-start | bytes 69124
  7.2 136.3 %all-gather.7.cloned.1.call-start = ((), (), s32[]{:S(2)}) async-start(), calls=%async_computation.9 | async-start | bytes 6406144 | tf_op jit(solution)/shard_map/all_gather | solution.py:86
  10.9 30.1 %copy-start.16 = (s32[1,128,4]{1,2,0:T(4,128)S(1)}, s32[1,128,4]{1,2,0:T(4,128)}, u32[]{:S(2)}) copy-start(s32[1,128,4]{1,2,0:T(4,128)} %param.28) | copy-start | bytes 6148
  10.9 30.4 %copy-start.1 = (bf16[1,128,360]{1,2,0:T(8,128)(2,1)S(1)}, bf16[1,128,360]{1,2,0:T(8,128)(2,1)}, u32[]{:S(2)}) copy-start(bf16[1,128,360]{1,2,0:T(8,128)(2,1)} %param.17) | copy-start | bytes 276484
  10.9 30.6 %copy-start.18 = (f32[8]{0:T(128)S(1)}, f32[8]{0:T(128)}, u32[]{:S(2)}) copy-start(f32[8]{0:T(128)} %param.24) | copy-start | bytes 100
  10.9 18.5 %all-to-all-start = ((bf16[8,360,128]{2,1,0:T(8,128)(2,1)}), bf16[8,360,128]{2,1,0:T(8,128)(2,1)S(1)}, u32[]{:S(2)}, u32[]{:S(2)}) async-start(bf16[8,360,128]{2,1,0:T(8,128)(2,1)} %broadcast_in_dim.90), calls=%async_computation | async-start | bytes 1474560 | tf_op jit(solution)/shard_map/all_to_all | solution.py:45
  17.0 25.1 %copy-start.13 = (f32[2880]{0:T(1024)S(1)}, f32[2880]{0:T(1024)}, u32[]{:S(2)}) copy-start(f32[2880]{0:T(1024)} %param.19) | copy-start | bytes 34564
  30.4 39.4 %all-to-all-start.1 = ((bf16[16,180,128]{2,1,0:T(8,128)(2,1)}), bf16[16,180,128]{2,1,0:T(8,128)(2,1)S(1)}, u32[]{:S(2)}, u32[]{:S(2)}) async-start(bf16[16,180,128]{2,1,0:T(8,128)(2,1)} %broadcast_in_dim.91), calls=%async_computation.1 | async-start | bytes 1507328 | tf_op jit(solution)/shard_map/all_to_all | solution.py:45
  41.6 28.2 %copy-start.9 = (f32[8,128]{1,0:T(8,128)}, f32[8,128]{1,0:T(8,128)S(1)}, u32[]{:S(2)}) copy-start(f32[8,128]{1,0:T(8,128)S(1)} %broadcast_in_dim.93) | copy-start | bytes 12292
  70.5 1.1 copy-start.3
  71.6 22.4 %all-to-all-start.2 = ((bf16[16,128,128]{2,1,0:T(8,128)(2,1)}), bf16[16,128,128]{2,1,0:T(8,128)(2,1)S(1)}, u32[]{:S(2)}, u32[]{:S(2)}) async-start(bf16[16,128,128]{2,1,0:T(8,128)(2,1)} %broadcast_in_dim.92), calls=%async_computation.2 | async-start | bytes 1048576 | tf_op jit(solution)/shard_map/all_to_all | solution.py:45
  154.1 6.1 %copy-start.5 = (f32[128,32]{0,1:T(8,128)S(1)}, f32[128,32]{0,1:T(8,128)}, u32[]{:S(2)}) copy-start(f32[128,32]{0,1:T(8,128)} %get-tuple-element.500) | copy-start | bytes 49156
  154.1 6.1 %copy-start.6 = (f32[128,32]{0,1:T(8,128)S(1)}, f32[128,32]{0,1:T(8,128)}, u32[]{:S(2)}) copy-start(f32[128,32]{0,1:T(8,128)} %get-tuple-element.501) | copy-start | bytes 49156
  154.1 6.4 %copy-start.2 = (bf16[1,2048,64]{2,1,0:T(8,128)(2,1)S(1)}, bf16[1,2048,64]{2,1,0:T(8,128)(2,1)}, u32[]{:S(2)}) copy-start(bf16[1,2048,64]{2,1,0:T(8,128)(2,1)} %get-tuple-element.657) | copy-start | bytes 786436
  154.1 6.4 %copy-start.7 = (s32[128]{0:T(128)S(1)}, s32[128]{0:T(128)}, u32[]{:S(2)}) copy-start(s32[128]{0:T(128)} %dynamic-slice_bitcast_fusion) | copy-start | bytes 1540
  154.1 6.4 %copy-start.8 = (s32[1,2048]{1,0:T(1,128)S(1)}, s32[1,2048]{1,0:T(1,128)}, u32[]{:S(2)}) copy-start(s32[1,2048]{1,0:T(1,128)} %param.18) | copy-start | bytes 24580
  163.4 9.0 %copy-start.10 = (f32[8,128]{1,0:T(8,128)S(1)}, f32[8,128]{1,0:T(8,128)}, u32[]{:S(2)}) copy-start(f32[8,128]{1,0:T(8,128)} %copy-done.9) | copy-start | bytes 12292
  175.4 5.6 %copy-start.14 = (s32[512,1]{0,1:T(1,128)S(1)}, s32[512,1]{0,1:T(1,128)}, u32[]{:S(2)}) copy-start(s32[512,1]{0,1:T(1,128)} %mul.228) | copy-start | bytes 6148
  175.4 5.6 %copy-start.15 = (s32[512]{0:T(512)S(1)}, s32[512]{0:T(512)}, u32[]{:S(2)}) copy-start(s32[512]{0:T(512)} %fusion.79) | copy-start | bytes 6148
  177.2 16.0 %all-to-all-start.3 = ((bf16[8,128,360]{1,2,0:T(8,128)(2,1)}), bf16[8,128,360]{1,2,0:T(8,128)(2,1)S(1)}, u32[]{:S(2)}, u32[]{:S(2)}) async-start(bf16[8,128,360]{1,2,0:T(8,128)(2,1)} %bitcast.206), calls=%async_computation.3 | async-start | bytes 1474560 | tf_op jit(solution)/shard_map/all_to_all | solution.py:177
  180.8 91.5 %all-gather.5.cloned.1.call-start = ((), (), s32[]{:S(2)}) async-start(), calls=%async_computation.7 | async-start | bytes 4976640 | tf_op jit(solution)/shard_map/all_gather | solution.py:203
  220.1 128.3 %reduce-scatter.2.cloned.1.call-start = ((), (), s32[]{:S(2)}) async-start(), calls=%async_computation.8 | async-start | bytes 4976640 | tf_op jit(solution)/shard_map/reduce_scatter | solution.py:218
  223.5 52.2 %copy-start.19 = (f32[2880]{0:T(1024)S(1)}, f32[2880]{0:T(1024)}, u32[]{:S(2)}) copy-start(f32[2880]{0:T(1024)} %param.25) | copy-start | bytes 34564
  272.3 3.6 copy-start
  291.3 68.2 %copy-start.17 = (f32[1,128,4]{1,2,0:T(4,128)S(1)}, f32[1,128,4]{1,2,0:T(4,128)}, u32[]{:S(2)}) copy-start(f32[1,128,4]{1,2,0:T(4,128)} %param.29) | copy-start | bytes 6148
  291.3 68.3 %copy-start.4 = (bf16[128,1,32]{0,2,1:T(8,128)(2,1)S(1)}, bf16[128,1,32]{0,2,1:T(8,128)(2,1)}, u32[]{:S(2)}) copy-start(bf16[128,1,32]{0,2,1:T(8,128)(2,1)} %copy-done.3) | copy-start | bytes 24580
  350.4 26.4 %all-to-all-start.5 = ((bf16[16,48,360]{2,1,0:T(8,128)(2,1)}), bf16[16,48,360]{2,1,0:T(8,128)(2,1)S(1)}, u32[]{:S(2)}, u32[]{:S(2)}) async-start(bf16[16,48,360]{2,1,0:T(8,128)(2,1)} %bitcast.41), calls=%async_computation.6 | async-start | bytes 1179648 | tf_op jit(solution)/shard_map/all_to_all | solution.py:222
Sparse Core Ops, SparseCore 0:
  10.6 132.8 all-gather.6
  220.2 52.0 all-gather.4
  291.4 56.8 reduce-scatter.1

commit v7 on v6

--- a/solution.py
+++ b/solution.py
@@ -83,9 +83,16 @@
     input_normalised = rms_norm(whole_rows, attn_gain)
     query_cols = w_query.shape[1]
     kv_cols = key_weight.shape[1]
-    big_weights = lax.all_gather(jnp.concatenate([w_query, w_out.T], axis=1), "expert", axis=0)
+    out_split = w_out.shape[0] // 2
+    out_t = w_out.T
+    big_weights = lax.all_gather(
+        jnp.concatenate([w_query, out_t[:, :out_split]], axis=1), "expert", axis=0
+    )
     query_weight = big_weights[:, :, :query_cols]
-    out_weight_t = big_weights[:, :, query_cols:]
+    out_weight_first = big_weights[:, :, query_cols:]
+    out_weight_second = gather_by_exchange(out_t[:, out_split:], "expert").reshape(
+        expert_devs, -1, w_out.shape[0] - out_split
+    )
     kv_weight = gather_by_exchange(jnp.concatenate([key_weight, value_weight], axis=1), "expert")
     query_raw = jnp.einsum(
         "tef,efc->tc",
@@ -169,8 +176,13 @@
         .transpose(2, 0, 1, 3)
         .reshape(tok_count, query_cols)
     )
-    out_terms = jnp.einsum(
-        "tc,efc->tef", mixed, out_weight_t, preferred_element_type=jnp.float32
+    out_terms = (
+        jnp.einsum(
+            "tc,efc->tef", mixed[:, :out_split], out_weight_first, preferred_element_type=jnp.float32
+        )
+        + jnp.einsum(
+            "tc,efc->tef", mixed[:, out_split:], out_weight_second, preferred_element_type=jnp.float32
+        )
     ).reshape(tok_count, -1)
     model_width = out_terms.shape[1]
     out_pieces = out_terms.astype(jnp.bfloat16).reshape(tok_count, mp_devs, model_width // mp_devs)

time: 388 us -> 398 us (1.026)
  starting transfers between devices: 33.5 us -> 39 us
    all_to_all x3 -> x4, starting transfers between devices: 20.6 us -> 26.1 us  [gather_by_exchange(): lax.all_to_all(spread, axis_name, split_axis=0, concat_axis=0, tiled=True)]
    all_to_all x3 -> x4, waiting for transfers between devices: 52.1 us -> 52.4 us  [gather_by_exchange(): lax.all_to_all(spread, axis_name, split_axis=0, concat_axis=0, tiled=True)]
  transfers between devices with their start and end apart: 8 -> 9, of which waited for: 8 -> 8; matrix products, arithmetic and copies ran while one was open for 5% -> 11% of each run, Pallas kernels for 0% -> 0%
where the time goes in v7:
time: 398 us; the launch traced here: 397 us
  waiting for transfers between devices  235 us (59%)
  starting transfers between devices  39 us (10%)
  matrix products  36.5 us (9%)
  local copies, waits for them, and re-layouts  35.7 us (9%)
  blocking collectives  24.8 us (6%)
  between operations  14.3 us (4%)
  other arithmetic  10.9 us (3%)
    reduce_scatter x1, waiting for transfers between devices, shards(): lax.psum_scatter(partials.astype(jnp.bfloat16), 'mp', scatter_dimension=0...  57 us
    all_to_all x4, waiting for transfers between devices, gather_by_exchange(): lax.all_to_all(spread, axis_name, split_axis=0, concat_axis=0, tiled=True)  52.4 us
    all_gather x1, waiting for transfers between devices, shards(): lax.all_gather(jnp.concatenate([w_query, out_t[:, :out_split]], axis=1),...  51.7 us
    all_gather x1, waiting for transfers between devices, shards(): lax.all_gather(arrived_rows, 'mp', axis=1, tiled=True)  48.7 us
    all_to_all x4, starting transfers between devices, gather_by_exchange(): lax.all_to_all(spread, axis_name, split_axis=0, concat_axis=0, tiled=True)  26.1 us
    all_to_all x1, blocking collectives, shards(): lax.all_to_all(outgoing, 'expert', split_axis=0, concat_axis=0, tiled=True)  24.8 us
    all_to_all x1, waiting for transfers between devices, shards(): lax.all_to_all(expert_out, 'expert', split_axis=0, concat_axis=0, tiled=T...  16 us
    dot_general x1, matrix products, shards(): jnp.einsum('rh,hjf->jrf', activated, expert_down[0].reshape(expert_down.s...  10.7 us
  transfers between devices with their start and end apart: 9, of which 8 were waited for; matrix products, arithmetic and copies ran while one was open for 11% of the time, Pallas kernels for 0%

profile of v7, /device:TPU:1, one launch (start us, length us, event | category | flops | bytes accessed | tf_op | source)
XLA Modules:
  0.0 397.0 jit_solution(12173482337522310285)
XLA Ops:
  7.2 1.0 fusion.104
  8.2 1.7 maximum_bitcast_fusion
  9.9 1.9 broadcast_in_dim.96
  11.7 6.0 %all-to-all-start = ((bf16[8,360,128]{2,1,0:T(8,128)(2,1)}), bf16[8,360,128]{2,1,0:T(8,128)(2,1)S(1)}, u32[]{:S(2)}, u32[]{:S(2)}) async-start(bf16[8,360,128]{2,1,0:T(8,128)(2,1)} %broadcast_in_dim.96), calls=%async_computation | async-start | bytes 1474560 | tf_op jit(solution)/shard_map/all_to_all | solution.py:45
  17.9 12.3 %all-to-all-done = bf16[8,360,128]{2,1,0:T(8,128)(2,1)S(1)} async-done(((bf16[8,360,128]{2,1,0:T(8,128)(2,1)}), bf16[8,360,128]{2,1,0:T(8,128)(2,1)S(1)}, u32[]{:S(2)}, u32[]{:S(2)}) %all-to-all-start) | async-done | bytes 737312 | tf_op jit(solution)/shard_map/all_to_all | solution.py:45
  30.2 1.0 broadcast_in_dim.97
  31.2 10.6 %all-to-all-start.1 = ((bf16[16,180,128]{2,1,0:T(8,128)(2,1)}), bf16[16,180,128]{2,1,0:T(8,128)(2,1)S(1)}, u32[]{:S(2)}, u32[]{:S(2)}) async-start(bf16[16,180,128]{2,1,0:T(8,128)(2,1)} %broadcast_in_dim.97), calls=%async_computation.1 | async-start | bytes 1507328 | tf_op jit(solution)/shard_map/all_to_all | solution.py:45
  42.5 0.4 fusion.40
  42.9 0.4 fusion.42
  43.4 25.1 %all-to-all-done.1 = bf16[16,180,128]{2,1,0:T(8,128)(2,1)S(1)} async-done(((bf16[16,180,128]{2,1,0:T(8,128)(2,1)}), bf16[16,180,128]{2,1,0:T(8,128)(2,1)S(1)}, u32[]{:S(2)}, u32[]{:S(2)}) %all-to-all-start.1) | async-done | bytes 737312 | tf_op jit(solution)/shard_map/all_to_all | solution.py:45
  68.6 0.4 fusion.105
  69.4 0.9 broadcast_in_dim.98
  70.3 4.5 %all-to-all-start.2 = ((bf16[16,128,128]{2,1,0:T(8,128)(2,1)}), bf16[16,128,128]{2,1,0:T(8,128)(2,1)S(1)}, u32[]{:S(2)}, u32[]{:S(2)}) async-start(bf16[16,128,128]{2,1,0:T(8,128)(2,1)} %broadcast_in_dim.98), calls=%async_computation.2 | async-start | bytes 1048576 | tf_op jit(solution)/shard_map/all_to_all | solution.py:45
  74.8 1.2 reduce-window.6
  76.3 0.7 mul.228
  77.0 1.2 dynamic-slice_bitcast_fusion
  78.3 0.7 fusion.84
  79.0 0.8 multiply_cosine_fusion
  79.7 1.0 reshape.432
  80.7 14.9 %all-to-all-done.2 = bf16[16,128,128]{2,1,0:T(8,128)(2,1)S(1)} async-done(((bf16[16,128,128]{2,1,0:T(8,128)(2,1)}), bf16[16,128,128]{2,1,0:T(8,128)(2,1)S(1)}, u32[]{:S(2)}, u32[]{:S(2)}) %all-to-all-start.2) | async-done | bytes 524320 | tf_op jit(solution)/shard_map/all_to_all | solution.py:45
  95.7 1.2 broadcast_in_dim.101
  96.9 5.0 %all-to-all-start.3 = ((bf16[16,180,256]{2,1,0:T(8,128)(2,1)}), bf16[16,180,256]{2,1,0:T(8,128)(2,1)}, u32[]{:S(2)}, u32[]{:S(2)}) async-start(bf16[16,180,256]{2,1,0:T(8,128)(2,1)} %broadcast_in_dim.101), calls=%async_computation.3 | async-start | bytes 3014656 | tf_op jit(solution)/shard_map/all_to_all | solution.py:45
  101.9 1.2 slice_bitcast_fusion
  103.1 51.7 %all-gather.7.cloned.1.call-done = bf16[16,180,768]{2,1,0:T(8,128)(2,1)} async-done(((bf16[1,180,768]{2,1,0:T(8,128)(2,1)}), bf16[16,180,768]{2,1,0:T(8,128)(2,1)}) %all-gather.7.cloned.1.call-update) | async-done | bytes 4423696 | tf_op jit(solution)/shard_map/all_gather | solution.py:88
  154.8 1.9 slice-done
  156.6 5.6 %copy.136 = bf16[16,180,512]{1,0,2:T(8,128)(2,1)} copy(bf16[16,180,512]{2,1,0:T(8,128)(2,1)S(1)} %slice-done) | data formatting | bytes 5898240
  162.3 6.1 %fusion.68 = f32[128,8,64]{0,2,1:T(8,128)S(1)} fusion(bf16[128,16,180,1]{0,2,1,3:T(8,128)(2,1)} %reshape.432, bf16[8,64,16,180]{3,2,1,0:T(8,128)(2,1)} %bitcast.213), kind=kOutput, calls=%fused_computation.65 | convolution fusion | flops 377487360 | bytes 3948544 | tf_op jit(solution)/shard_map/tef,efc->tc/dot_general | solution.py:97
  168.6 2.9 while.30
  168.7 0.6 fusion.121
  169.5 0.6 fusion.121
  170.2 0.6 fusion.121
  170.9 0.6 fusion.121
  171.5 9.0 %while.31 = (s32[]{:T(128)}, f32[1,1024,64]{1,2,0:T(8,128)S(1)}, f32[1,1024]{1,0:T(1,128)S(1)}, s32[2048]{0:T(1024)S(1)}, bf16[1,2048,64]{2,1,0:T(8,128)(2,1)S(1...) while((s32[]{:T(128)}, f32[1,1024,64]{1,2,0:T(8,128)S(1)}, ...), condition=%wide.region_6.7_spmd.clone, body=%wide.region_4.6_spmd.clone.sunk | while | flops 139068928 | bytes 3194062 | solution.py:171
  171.7 0.8 convert_reduce_fusion.3
  172.5 1.3 fusion.124
  173.9 0.8 convert_reduce_fusion.3
  174.8 1.3 fusion.124
  176.2 0.8 convert_reduce_fusion.3
  177.0 1.3 fusion.124
  178.4 0.8 convert_reduce_fusion.3
  179.3 1.3 fusion.124
  180.7 1.9 fusion.81
  182.6 2.0 add_convert_fusion
  184.6 1.0 convert_element_type.126
  185.6 3.5 all-to-all-start.4
  189.5 2.4 scatter_custom_fusion
  191.9 9.7 %all-to-all-done.4 = bf16[8,128,360]{1,2,0:T(8,128)(2,1)S(1)} async-done(((bf16[8,128,360]{1,2,0:T(8,128)(2,1)}), bf16[8,128,360]{1,2,0:T(8,128)(2,1)S(1)}, u32[]{:S(2)}, u32[]{:S(2)}) %all-to-all-start.4) | async-done | bytes 737312 | tf_op jit(solution)/shard_map/all_to_all | solution.py:189
  201.9 2.6 gather_fusion
  204.5 24.8 %all_to_all.35 = bf16[16,48,360]{2,1,0:T(8,128)(2,1)S(1)} all-to-all(bf16[16,48,360]{2,1,0:T(8,128)(2,1)S(1)} %bitcast.214), channel_id=1, replica_groups=mesh['expert'=16,'mp'=8,'batch'=2] {'expert'}, dimensions={0} | all-to-all | bytes 1105920 | tf_op jit(solution)/shard_map/all_to_all | solution.py:213
  229.3 1.1 copy.126
  230.5 3.4 copy.133
  233.9 48.7 %all-gather.5.cloned.1.call-done = bf16[768,2880]{0,1:T(8,128)(2,1)} async-done(((bf16[768,360]{0,1:T(8,128)(2,1)}), bf16[768,2880]{0,1:T(8,128)(2,1)}) %all-gather.5.cloned.1.call-update) | async-done | bytes 4423696 | tf_op jit(solution)/shard_map/all_gather | solution.py:215
  282.5 3.3 fusion.25
  286.1 4.7 %fusion.43 = f32[768,360]{0,1:T(8,128)} fusion(bf16[1,2,2880,360]{2,3,1,0:T(8,128)(2,1)} %param.26, bf16[768,2880]{0,1:T(8,128)(2,1)S(1)} %copy-done, f32[2880]{0:T(1024)S(1)} %copy-done.19, f32[768]{0:T(1024)S(1)} %add_rsqrt_fusion), kind=kOutput, calls=%fused_computation.58 | convolution fusion | flops 1601648640 | bytes 7663872 | tf_op jit(solution)/shard_map/dot_general | solution.py:217
  290.7 10.7 %convert_bitcast_fusion = bf16[8,768,360]{1,2,0:T(8,128)(2,1)} fusion(bf16[360,8,360]{0,2,1:T(8,128)(2,1)S(1)} %bitcast.216, f32[768,360]{0,1:T(8,128)} %fusion.43, bf16[1,2,2880,360]{2,3,1,0:T(8,128)(2,1)} %param.26, bf16[768,2880]{0,1:T(8,128)(2,1)} %all-gather.5.cloned.1.call-done, f32[2880]{0:T(1024)S(1)} %copy-done.19, f32[768]{0:T(1024)S(1)} %add_rsqrt_fusion), kind=kOutput, calls=%fused_computation.40 | convolution fusion | flops 3198597120 | bytes 14161152 | tf_op jit(solution)/shard_map/rh,hjf->jrf/dot_general | solution.py:224
  301.5 57.0 %reduce-scatter.2.cloned.1.call-done = bf16[1,768,360]{1,2,0:T(8,128)(2,1)} async-done(((bf16[8,768,360]{1,2,0:T(8,128)(2,1)}), bf16[1,768,360]{1,2,0:T(8,128)(2,1)}) %reduce-scatter.2.cloned.1.call-update) | async-done | bytes 552976 | tf_op jit(solution)/shard_map/reduce_scatter | solution.py:230
  358.5 2.1 copy.128
  360.6 9.0 %all-to-all-start.6 = ((bf16[16,48,360]{2,1,0:T(8,128)(2,1)}), bf16[16,48,360]{2,1,0:T(8,128)(2,1)S(1)}, u32[]{:S(2)}, u32[]{:S(2)}) async-start(bf16[16,48,360]{2,1,0:T(8,128)(2,1)} %bitcast.42), calls=%async_computation.7 | async-start | bytes 1179648 | tf_op jit(solution)/shard_map/all_to_all | solution.py:234
  369.8 0.6 pad_maximum_fusion.2
  370.4 0.6 slice_bitcast_fusion.7
  371.0 16.0 %all-to-all-done.6 = bf16[16,48,360]{2,1,0:T(8,128)(2,1)S(1)} async-done(((bf16[16,48,360]{2,1,0:T(8,128)(2,1)}), bf16[16,48,360]{2,1,0:T(8,128)(2,1)S(1)}, u32[]{:S(2)}, u32[]{:S(2)}) %all-to-all-start.6) | async-done | bytes 552992 | tf_op jit(solution)/shard_map/all_to_all | solution.py:234
  387.0 1.9 gather_fusion.1
  389.1 0.6 multiply_reduce_fusion
  389.8 0.7 fusion.76
  (125 shorter events, 4.0 us)
Async XLA Ops:
  7.2 10.6 %copy-start.12 = (bf16[180,64]{0,1:T(8,128)(2,1)S(1)}, bf16[180,64]{0,1:T(8,128)(2,1)}, u32[]{:S(2)}) copy-start(bf16[180,64]{0,1:T(8,128)(2,1)} %param.21) | copy-start | bytes 69124
  7.2 10.6 %copy-start.11 = (bf16[180,64]{0,1:T(8,128)(2,1)S(1)}, bf16[180,64]{0,1:T(8,128)(2,1)}, u32[]{:S(2)}) copy-start(bf16[180,64]{0,1:T(8,128)(2,1)} %param.22) | copy-start | bytes 69124
  7.2 147.6 %all-gather.7.cloned.1.call-start = ((), (), s32[]{:S(2)}) async-start(), calls=%async_computation.10 | async-start | bytes 4804608 | tf_op jit(solution)/shard_map/all_gather | solution.py:88
  11.7 30.1 %copy-start.1 = (bf16[1,128,360]{1,2,0:T(8,128)(2,1)S(1)}, bf16[1,128,360]{1,2,0:T(8,128)(2,1)}, u32[]{:S(2)}) copy-start(bf16[1,128,360]{1,2,0:T(8,128)(2,1)} %param.17) | copy-start | bytes 276484
  11.7 30.3 %copy-start.16 = (s32[1,128,4]{1,2,0:T(4,128)S(1)}, s32[1,128,4]{1,2,0:T(4,128)}, u32[]{:S(2)}) copy-start(s32[1,128,4]{1,2,0:T(4,128)} %param.28) | copy-start | bytes 6148
  11.7 30.6 %copy-start.18 = (f32[8]{0:T(128)S(1)}, f32[8]{0:T(128)}, u32[]{:S(2)}) copy-start(f32[8]{0:T(128)} %param.24) | copy-start | bytes 100
  11.7 18.5 %all-to-all-start = ((bf16[8,360,128]{2,1,0:T(8,128)(2,1)}), bf16[8,360,128]{2,1,0:T(8,128)(2,1)S(1)}, u32[]{:S(2)}, u32[]{:S(2)}) async-start(bf16[8,360,128]{2,1,0:T(8,128)(2,1)} %broadcast_in_dim.96), calls=%async_computation | async-start | bytes 1474560 | tf_op jit(solution)/shard_map/all_to_all | solution.py:45
  17.8 25.2 %copy-start.13 = (f32[2880]{0:T(1024)S(1)}, f32[2880]{0:T(1024)}, u32[]{:S(2)}) copy-start(f32[2880]{0:T(1024)} %param.19) | copy-start | bytes 34564
  31.2 37.3 %all-to-all-start.1 = ((bf16[16,180,128]{2,1,0:T(8,128)(2,1)}), bf16[16,180,128]{2,1,0:T(8,128)(2,1)S(1)}, u32[]{:S(2)}, u32[]{:S(2)}) async-start(bf16[16,180,128]{2,1,0:T(8,128)(2,1)} %broadcast_in_dim.97), calls=%async_computation.1 | async-start | bytes 1507328 | tf_op jit(solution)/shard_map/all_to_all | solution.py:45
  42.4 26.1 %copy-start.9 = (f32[8,128]{1,0:T(8,128)}, f32[8,128]{1,0:T(8,128)S(1)}, u32[]{:S(2)}) copy-start(f32[8,128]{1,0:T(8,128)S(1)} %broadcast_in_dim.99) | copy-start | bytes 12292
  69.2 7.0 %copy-start.3 = (bf16[128,1,32]{0,2,1:T(8,128)(2,1)}, bf16[128,1,32]{0,2,1:T(8,128)(2,1)S(1)}, u32[]{:S(2)}) copy-start(bf16[128,1,32]{0,2,1:T(8,128)(2,1)S(1)} %get-tuple-element.499) | copy-start | bytes 24580
  70.3 25.4 %all-to-all-start.2 = ((bf16[16,128,128]{2,1,0:T(8,128)(2,1)}), bf16[16,128,128]{2,1,0:T(8,128)(2,1)S(1)}, u32[]{:S(2)}, u32[]{:S(2)}) async-start(bf16[16,128,128]{2,1,0:T(8,128)(2,1)} %broadcast_in_dim.98), calls=%async_computation.2 | async-start | bytes 1048576 | tf_op jit(solution)/shard_map/all_to_all | solution.py:45
  96.9 83.8 %all-to-all-start.3 = ((bf16[16,180,256]{2,1,0:T(8,128)(2,1)}), bf16[16,180,256]{2,1,0:T(8,128)(2,1)}, u32[]{:S(2)}, u32[]{:S(2)}) async-start(bf16[16,180,256]{2,1,0:T(8,128)(2,1)} %broadcast_in_dim.101), calls=%async_computation.3 | async-start | bytes 3014656 | tf_op jit(solution)/shard_map/all_to_all | solution.py:45
  154.8 1.9 slice-start
  162.3 6.1 %copy-start.5 = (f32[128,32]{0,1:T(8,128)S(1)}, f32[128,32]{0,1:T(8,128)}, u32[]{:S(2)}) copy-start(f32[128,32]{0,1:T(8,128)} %get-tuple-element.500) | copy-start | bytes 49156
  162.3 6.1 %copy-start.6 = (f32[128,32]{0,1:T(8,128)S(1)}, f32[128,32]{0,1:T(8,128)}, u32[]{:S(2)}) copy-start(f32[128,32]{0,1:T(8,128)} %get-tuple-element.501) | copy-start | bytes 49156
  162.3 6.4 %copy-start.2 = (bf16[1,2048,64]{2,1,0:T(8,128)(2,1)S(1)}, bf16[1,2048,64]{2,1,0:T(8,128)(2,1)}, u32[]{:S(2)}) copy-start(bf16[1,2048,64]{2,1,0:T(8,128)(2,1)} %get-tuple-element.657) | copy-start | bytes 786436
  162.3 6.4 %copy-start.7 = (s32[128]{0:T(128)S(1)}, s32[128]{0:T(128)}, u32[]{:S(2)}) copy-start(s32[128]{0:T(128)} %dynamic-slice_bitcast_fusion) | copy-start | bytes 1540
  162.3 6.4 %copy-start.8 = (s32[1,2048]{1,0:T(1,128)S(1)}, s32[1,2048]{1,0:T(1,128)}, u32[]{:S(2)}) copy-start(s32[1,2048]{1,0:T(1,128)} %param.18) | copy-start | bytes 24580
  171.5 9.0 %copy-start.10 = (f32[8,128]{1,0:T(8,128)S(1)}, f32[8,128]{1,0:T(8,128)}, u32[]{:S(2)}) copy-start(f32[8,128]{1,0:T(8,128)} %copy-done.9) | copy-start | bytes 12292
  184.6 4.8 %copy-start.14 = (s32[512,1]{0,1:T(1,128)S(1)}, s32[512,1]{0,1:T(1,128)}, u32[]{:S(2)}) copy-start(s32[512,1]{0,1:T(1,128)} %mul.228) | copy-start | bytes 6148
  184.6 4.8 %copy-start.15 = (s32[512]{0:T(512)S(1)}, s32[512]{0:T(512)}, u32[]{:S(2)}) copy-start(s32[512]{0:T(512)} %fusion.84) | copy-start | bytes 6148
  185.6 16.0 %all-to-all-start.4 = ((bf16[8,128,360]{1,2,0:T(8,128)(2,1)}), bf16[8,128,360]{1,2,0:T(8,128)(2,1)S(1)}, u32[]{:S(2)}, u32[]{:S(2)}) async-start(bf16[8,128,360]{1,2,0:T(8,128)(2,1)} %bitcast.30), calls=%async_computation.4 | async-start | bytes 1474560 | tf_op jit(solution)/shard_map/all_to_all | solution.py:189
  189.2 93.3 %all-gather.5.cloned.1.call-start = ((), (), s32[]{:S(2)}) async-start(), calls=%async_computation.8 | async-start | bytes 4976640 | tf_op jit(solution)/shard_map/all_gather | solution.py:215
  230.4 128.1 %reduce-scatter.2.cloned.1.call-start = ((), (), s32[]{:S(2)}) async-start(), calls=%async_computation.9 | async-start | bytes 4976640 | tf_op jit(solution)/shard_map/reduce_scatter | solution.py:230
  233.8 52.0 %copy-start.19 = (f32[2880]{0:T(1024)S(1)}, f32[2880]{0:T(1024)}, u32[]{:S(2)}) copy-start(f32[2880]{0:T(1024)} %param.25) | copy-start | bytes 34564
  282.5 3.6 copy-start
  301.5 68.2 %copy-start.17 = (f32[1,128,4]{1,2,0:T(4,128)S(1)}, f32[1,128,4]{1,2,0:T(4,128)}, u32[]{:S(2)}) copy-start(f32[1,128,4]{1,2,0:T(4,128)} %param.29) | copy-start | bytes 6148
  301.5 68.3 %copy-start.4 = (bf16[128,1,32]{0,2,1:T(8,128)(2,1)S(1)}, bf16[128,1,32]{0,2,1:T(8,128)(2,1)}, u32[]{:S(2)}) copy-start(bf16[128,1,32]{0,2,1:T(8,128)(2,1)} %copy-done.3) | copy-start | bytes 24580
  360.6 26.4 %all-to-all-start.6 = ((bf16[16,48,360]{2,1,0:T(8,128)(2,1)}), bf16[16,48,360]{2,1,0:T(8,128)(2,1)S(1)}, u32[]{:S(2)}, u32[]{:S(2)}) async-start(bf16[16,48,360]{2,1,0:T(8,128)(2,1)} %bitcast.42), calls=%async_computation.7 | async-start | bytes 1179648 | tf_op jit(solution)/shard_map/all_to_all | solution.py:234
Sparse Core Ops, SparseCore 0:
  10.6 144.0 all-gather.6
  230.5 51.9 all-gather.4
  301.6 56.8 reduce-scatter.1

commit v8 on v6

--- a/solution.py
+++ b/solution.py
@@ -169,15 +169,13 @@
         .transpose(2, 0, 1, 3)
         .reshape(tok_count, query_cols)
     )
-    out_terms = jnp.einsum(
-        "tc,efc->tef", mixed, out_weight_t, preferred_element_type=jnp.float32
-    ).reshape(tok_count, -1)
-    model_width = out_terms.shape[1]
-    out_pieces = out_terms.astype(jnp.bfloat16).reshape(tok_count, mp_devs, model_width // mp_devs)
-    out_got = lax.all_to_all(
-        out_pieces.transpose(1, 0, 2), "mp", split_axis=0, concat_axis=0, tiled=True
-    )
-    attn_part = jnp.sum(out_got.astype(jnp.float32), axis=0)
+    out_terms_t = jnp.einsum(
+        "efc,tc->eft", out_weight_t, mixed, preferred_element_type=jnp.float32
+    )
+    model_width = out_terms_t.shape[0] * out_terms_t.shape[1]
+    out_pieces = out_terms_t.astype(jnp.bfloat16).reshape(mp_devs, model_width // mp_devs, tok_count)
+    out_got = lax.all_to_all(out_pieces, "mp", split_axis=0, concat_axis=0, tiled=True)
+    attn_part = jnp.sum(out_got.astype(jnp.float32), axis=0).T
     first_out = (local_rows.astype(jnp.float32) + attn_part).astype(jnp.bfloat16)
     top_count = routes.shape[2]
     local_experts = expert_in.shape[0]
@@ -209,6 +207,7 @@
     activated = ((up_val + 1.0) * gate_val * jax.nn.sigmoid(glu_alpha * gate_val)).astype(
         jnp.bfloat16
     )
+    activated = lax.optimization_barrier(activated)
     partials = jnp.einsum(
         "rh,hjf->jrf",
         activated,

time: 388 us -> 379 us (0.977)
  local copies, waits for them, and re-layouts: 38.3 us -> 32.3 us
    dot_general x1, matrix products: 10.7 us -> 4.48 us  [shards(): jnp.einsum('rh,hjf->jrf', activated, expert_down[0].reshape(expert_down.s...]
where the time goes in v8:
time: 379 us; the launch traced here: 378 us
  waiting for transfers between devices  235 us (62%)
  starting transfers between devices  34 us (9%)
  local copies, waits for them, and re-layouts  32.3 us (9%)
  matrix products  31 us (8%)
  blocking collectives  22.7 us (6%)
  between operations  14.2 us (4%)
  other arithmetic  9.23 us (2%)
    reduce_scatter x1, waiting for transfers between devices, shards(): lax.psum_scatter(partials.astype(jnp.bfloat16), 'mp', scatter_dimension=0...  57 us
    all_to_all x3, waiting for transfers between devices, gather_by_exchange(): lax.all_to_all(spread, axis_name, split_axis=0, concat_axis=0, tiled=True)  54.8 us
    all_gather x1, waiting for transfers between devices, shards(): lax.all_gather(arrived_rows, 'mp', axis=1, tiled=True)  48.9 us
    all_gather x1, waiting for transfers between devices, shards(): lax.all_gather(jnp.concatenate([w_query, w_out.T], axis=1), 'expert', axi...  48.1 us
    all_to_all x1, blocking collectives, shards(): lax.all_to_all(outgoing, 'expert', split_axis=0, concat_axis=0, tiled=True)  22.7 us
    all_to_all x3, starting transfers between devices, gather_by_exchange(): lax.all_to_all(spread, axis_name, split_axis=0, concat_axis=0, tiled=True)  21 us
    all_to_all x1, waiting for transfers between devices, shards(): lax.all_to_all(expert_out, 'expert', split_axis=0, concat_axis=0, tiled=T...  16 us
    all_to_all x1, waiting for transfers between devices, shards(): lax.all_to_all(out_pieces, 'mp', split_axis=0, concat_axis=0, tiled=True)  9.74 us
  transfers between devices with their start and end apart: 8, of which 8 were waited for; matrix products, arithmetic and copies ran while one was open for 5% of the time, Pallas kernels for 0%

profile of v8, /device:TPU:1, one launch (start us, length us, event | category | flops | bytes accessed | tf_op | source)
XLA Modules:
  0.0 378.4 jit_solution(7066076677444038869)
XLA Ops:
  7.2 1.8 maximum_bitcast_fusion
  9.1 1.9 broadcast_in_dim.92
  10.9 6.0 %all-to-all-start = ((bf16[8,360,128]{2,1,0:T(8,128)(2,1)}), bf16[8,360,128]{2,1,0:T(8,128)(2,1)S(1)}, u32[]{:S(2)}, u32[]{:S(2)}) async-start(bf16[8,360,128]{2,1,0:T(8,128)(2,1)} %broadcast_in_dim.92), calls=%async_computation | async-start | bytes 1474560 | tf_op jit(solution)/shard_map/all_to_all | solution.py:45
  17.1 12.3 %all-to-all-done = bf16[8,360,128]{2,1,0:T(8,128)(2,1)S(1)} async-done(((bf16[8,360,128]{2,1,0:T(8,128)(2,1)}), bf16[8,360,128]{2,1,0:T(8,128)(2,1)S(1)}, u32[]{:S(2)}, u32[]{:S(2)}) %all-to-all-start) | async-done | bytes 737312 | tf_op jit(solution)/shard_map/all_to_all | solution.py:45
  29.4 1.0 broadcast_in_dim.93
  30.4 10.6 %all-to-all-start.1 = ((bf16[16,180,128]{2,1,0:T(8,128)(2,1)}), bf16[16,180,128]{2,1,0:T(8,128)(2,1)S(1)}, u32[]{:S(2)}, u32[]{:S(2)}) async-start(bf16[16,180,128]{2,1,0:T(8,128)(2,1)} %broadcast_in_dim.93), calls=%async_computation.1 | async-start | bytes 1507328 | tf_op jit(solution)/shard_map/all_to_all | solution.py:45
  41.6 0.4 fusion.38
  42.1 0.5 fusion.40
  42.5 26.9 %all-to-all-done.1 = bf16[16,180,128]{2,1,0:T(8,128)(2,1)S(1)} async-done(((bf16[16,180,128]{2,1,0:T(8,128)(2,1)}), bf16[16,180,128]{2,1,0:T(8,128)(2,1)S(1)}, u32[]{:S(2)}, u32[]{:S(2)}) %all-to-all-start.1) | async-done | bytes 737312 | tf_op jit(solution)/shard_map/all_to_all | solution.py:45
  69.6 0.4 fusion.91
  70.1 0.1 fusion.82
  70.4 0.9 broadcast_in_dim.94
  71.3 4.4 %all-to-all-start.2 = ((bf16[16,128,128]{2,1,0:T(8,128)(2,1)}), bf16[16,128,128]{2,1,0:T(8,128)(2,1)S(1)}, u32[]{:S(2)}, u32[]{:S(2)}) async-start(bf16[16,128,128]{2,1,0:T(8,128)(2,1)} %broadcast_in_dim.94), calls=%async_computation.2 | async-start | bytes 1048576 | tf_op jit(solution)/shard_map/all_to_all | solution.py:45
  75.7 1.2 reduce-window.6
  76.8 0.2 slice_reduce_fusion
  77.4 0.1 multiply_cosine_fusion
  77.6 1.0 reshape.429
  78.6 15.5 %all-to-all-done.2 = bf16[16,128,128]{2,1,0:T(8,128)(2,1)S(1)} async-done(((bf16[16,128,128]{2,1,0:T(8,128)(2,1)}), bf16[16,128,128]{2,1,0:T(8,128)(2,1)S(1)}, u32[]{:S(2)}, u32[]{:S(2)}) %all-to-all-start.2) | async-done | bytes 524320 | tf_op jit(solution)/shard_map/all_to_all | solution.py:45
  94.1 1.1 slice_bitcast_fusion
  95.2 48.1 %all-gather.7.cloned.1.call-done = bf16[16,180,1024]{2,1,0:T(8,128)(2,1)} async-done(((bf16[1,180,1024]{2,1,0:T(8,128)(2,1)}), bf16[16,180,1024]{2,1,0:T(8,128)(2,1)}) %all-gather.7.cloned.1.call-update) | async-done | bytes 5898256 | tf_op jit(solution)/shard_map/all_gather | solution.py:86
  143.4 1.9 slice-done
  145.2 5.7 %copy.111 = bf16[16,180,512]{1,0,2:T(8,128)(2,1)} copy(bf16[16,180,512]{2,1,0:T(8,128)(2,1)S(1)} %slice-done) | data formatting | bytes 5898240
  150.9 6.1 %fusion.64 = f32[128,8,64]{0,2,1:T(8,128)S(1)} fusion(bf16[128,16,180,1]{0,2,1,3:T(8,128)(2,1)} %reshape.429, bf16[8,64,16,180]{3,2,1,0:T(8,128)(2,1)} %bitcast.195), kind=kOutput, calls=%fused_computation.64 | convolution fusion | flops 377487360 | bytes 3948544 | tf_op jit(solution)/shard_map/tef,efc->tc/dot_general | solution.py:90
  157.0 0.2 copy.109
  157.2 2.9 while.30
  157.3 0.6 fusion.107
  158.1 0.6 fusion.107
  158.8 0.6 fusion.107
  159.5 0.6 fusion.107
  160.1 9.0 %while.31 = (s32[]{:T(128)}, f32[1,1024,64]{1,2,0:T(8,128)S(1)}, f32[1,1024]{1,0:T(1,128)S(1)}, s32[2048]{0:T(1024)S(1)}, bf16[1,2048,64]{2,1,0:T(8,128)(2,1)S(1...) while((s32[]{:T(128)}, f32[1,1024,64]{1,2,0:T(8,128)S(1)}, ...), condition=%wide.region_6.7_spmd.clone, body=%wide.region_4.6_spmd.clone.sunk | while | flops 139068928 | bytes 3194062 | solution.py:164
  160.2 0.8 convert_reduce_fusion.3
  161.1 1.3 fusion.110
  162.5 0.8 convert_reduce_fusion.3
  163.3 1.3 fusion.110
  164.7 0.8 convert_reduce_fusion.3
  165.6 1.3 fusion.110
  167.0 0.8 convert_reduce_fusion.3
  167.8 1.3 fusion.110
  169.2 2.8 fusion.41
  172.1 1.0 reshape.387
  173.1 3.8 all-to-all-start.3
  176.8 0.2 all-gather.5.cloned.1.call-start
  177.1 2.4 scatter_custom_fusion
  179.5 9.7 %all-to-all-done.3 = bf16[8,360,128]{2,1,0:T(8,128)(2,1)S(1)} async-done(((bf16[8,360,128]{2,1,0:T(8,128)(2,1)}), bf16[8,360,128]{2,1,0:T(8,128)(2,1)S(1)}, u32[]{:S(2)}, u32[]{:S(2)}) %all-to-all-start.3) | async-done | bytes 737312 | tf_op jit(solution)/shard_map/all_to_all | solution.py:177
  189.6 2.6 gather_fusion
  192.2 22.7 %all_to_all.30 = bf16[16,48,360]{2,1,0:T(8,128)(2,1)S(1)} all-to-all(bf16[16,48,360]{2,1,0:T(8,128)(2,1)S(1)} %bitcast.196), channel_id=1, replica_groups=mesh['expert'=16,'mp'=8,'batch'=2] {'expert'}, dimensions={0} | all-to-all | bytes 1105920 | tf_op jit(solution)/shard_map/all_to_all | solution.py:199
  214.9 1.1 copy.99
  216.0 3.4 copy.108
  219.4 48.9 %all-gather.5.cloned.1.call-done = bf16[768,2880]{0,1:T(8,128)(2,1)} async-done(((bf16[768,360]{0,1:T(8,128)(2,1)}), bf16[768,2880]{0,1:T(8,128)(2,1)}) %all-gather.5.cloned.1.call-update) | async-done | bytes 4423696 | tf_op jit(solution)/shard_map/all_gather | solution.py:201
  268.3 3.3 fusion.25
  271.6 0.2 copy-done
  271.9 4.1 %fusion.44 = f32[768,360]{0,1:T(8,128)S(1)} fusion(bf16[1,2,2880,360]{2,3,1,0:T(8,128)(2,1)} %param.26, bf16[768,2880]{0,1:T(8,128)(2,1)S(1)} %copy-done, f32[2880]{0:T(1024)S(1)} %copy-done.10, f32[768]{0:T(1024)S(1)} %add_rsqrt_fusion), kind=kOutput, calls=%fused_computation.58 | convolution fusion | flops 1601648640 | bytes 7663872 | tf_op jit(solution)/shard_map/dot_general | solution.py:203
  276.0 2.4 fusion.59
  278.4 4.5 %convert_bitcast_fusion = bf16[8,768,360]{1,2,0:T(8,128)(2,1)} fusion(bf16[360,8,360]{0,2,1:T(8,128)(2,1)S(1)} %bitcast.198, bf16[768,360]{0,1:T(8,128)(2,1)S(1)} %fusion.59), kind=kOutput, calls=%fused_computation.40 | convolution fusion | flops 1594736640 | bytes 7050240 | tf_op jit(solution)/shard_map/rh,hjf->jrf/dot_general | solution.py:211
  282.9 57.0 %reduce-scatter.2.cloned.1.call-done = bf16[1,768,360]{1,2,0:T(8,128)(2,1)} async-done(((bf16[8,768,360]{1,2,0:T(8,128)(2,1)}), bf16[1,768,360]{1,2,0:T(8,128)(2,1)}) %reduce-scatter.2.cloned.1.call-update) | async-done | bytes 552976 | tf_op jit(solution)/shard_map/reduce_scatter | solution.py:217
  339.9 2.1 copy.101
  342.0 9.0 %all-to-all-start.5 = ((bf16[16,48,360]{2,1,0:T(8,128)(2,1)}), bf16[16,48,360]{2,1,0:T(8,128)(2,1)S(1)}, u32[]{:S(2)}, u32[]{:S(2)}) async-start(bf16[16,48,360]{2,1,0:T(8,128)(2,1)} %bitcast.40), calls=%async_computation.6 | async-start | bytes 1179648 | tf_op jit(solution)/shard_map/all_to_all | solution.py:221
  351.1 0.6 pad_maximum_fusion.2
  351.7 0.6 slice_bitcast_fusion.3
  352.4 16.0 %all-to-all-done.5 = bf16[16,48,360]{2,1,0:T(8,128)(2,1)S(1)} async-done(((bf16[16,48,360]{2,1,0:T(8,128)(2,1)}), bf16[16,48,360]{2,1,0:T(8,128)(2,1)S(1)}, u32[]{:S(2)}, u32[]{:S(2)}) %all-to-all-start.5) | async-done | bytes 552992 | tf_op jit(solution)/shard_map/all_to_all | solution.py:221
  368.4 1.9 gather_fusion.1
  370.3 0.2 reshape.394
  370.5 0.5 multiply_reduce_fusion
  371.1 0.7 copy.103
  (108 shorter events, 2.8 us)
Async XLA Ops:
  7.2 9.8 %copy-start.5 = (bf16[180,64]{0,1:T(8,128)(2,1)S(1)}, bf16[180,64]{0,1:T(8,128)(2,1)}, u32[]{:S(2)}) copy-start(bf16[180,64]{0,1:T(8,128)(2,1)} %param.21) | copy-start | bytes 69124
  7.2 9.8 %copy-start.4 = (bf16[180,64]{0,1:T(8,128)(2,1)S(1)}, bf16[180,64]{0,1:T(8,128)(2,1)}, u32[]{:S(2)}) copy-start(bf16[180,64]{0,1:T(8,128)(2,1)} %param.22) | copy-start | bytes 69124
  7.2 136.2 %all-gather.7.cloned.1.call-start = ((), (), s32[]{:S(2)}) async-start(), calls=%async_computation.9 | async-start | bytes 6406144 | tf_op jit(solution)/shard_map/all_gather | solution.py:86
  10.9 30.1 %copy-start.2 = (bf16[1,128,360]{1,2,0:T(8,128)(2,1)S(1)}, bf16[1,128,360]{1,2,0:T(8,128)(2,1)}, u32[]{:S(2)}) copy-start(bf16[1,128,360]{1,2,0:T(8,128)(2,1)} %param.17) | copy-start | bytes 276484
  10.9 30.3 %copy-start.7 = (s32[1,128,4]{1,2,0:T(4,128)S(1)}, s32[1,128,4]{1,2,0:T(4,128)}, u32[]{:S(2)}) copy-start(s32[1,128,4]{1,2,0:T(4,128)} %param.28) | copy-start | bytes 6148
  10.9 30.6 %copy-start.9 = (f32[8]{0:T(128)S(1)}, f32[8]{0:T(128)}, u32[]{:S(2)}) copy-start(f32[8]{0:T(128)} %param.24) | copy-start | bytes 100
  10.9 18.5 %all-to-all-start = ((bf16[8,360,128]{2,1,0:T(8,128)(2,1)}), bf16[8,360,128]{2,1,0:T(8,128)(2,1)S(1)}, u32[]{:S(2)}, u32[]{:S(2)}) async-start(bf16[8,360,128]{2,1,0:T(8,128)(2,1)} %broadcast_in_dim.92), calls=%async_computation | async-start | bytes 1474560 | tf_op jit(solution)/shard_map/all_to_all | solution.py:45
  17.0 25.1 %copy-start.6 = (f32[2880]{0:T(1024)S(1)}, f32[2880]{0:T(1024)}, u32[]{:S(2)}) copy-start(f32[2880]{0:T(1024)} %param.19) | copy-start | bytes 34564
  30.4 39.1 %all-to-all-start.1 = ((bf16[16,180,128]{2,1,0:T(8,128)(2,1)}), bf16[16,180,128]{2,1,0:T(8,128)(2,1)S(1)}, u32[]{:S(2)}, u32[]{:S(2)}) async-start(bf16[16,180,128]{2,1,0:T(8,128)(2,1)} %broadcast_in_dim.93), calls=%async_computation.1 | async-start | bytes 1507328 | tf_op jit(solution)/shard_map/all_to_all | solution.py:45
  69.6 7.7 %copy-start.3 = (s32[1,2048]{1,0:T(1,128)S(1)}, s32[1,2048]{1,0:T(1,128)}, u32[]{:S(2)}) copy-start(s32[1,2048]{1,0:T(1,128)} %param.18) | copy-start | bytes 24580
  71.3 22.8 %all-to-all-start.2 = ((bf16[16,128,128]{2,1,0:T(8,128)(2,1)}), bf16[16,128,128]{2,1,0:T(8,128)(2,1)S(1)}, u32[]{:S(2)}, u32[]{:S(2)}) async-start(bf16[16,128,128]{2,1,0:T(8,128)(2,1)} %broadcast_in_dim.94), calls=%async_computation.2 | async-start | bytes 1048576 | tf_op jit(solution)/shard_map/all_to_all | solution.py:45
  143.4 1.9 slice-start
  150.9 6.3 %copy-start.1 = (bf16[1,2048,64]{2,1,0:T(8,128)(2,1)S(1)}, bf16[1,2048,64]{2,1,0:T(8,128)(2,1)}, u32[]{:S(2)}) copy-start(bf16[1,2048,64]{2,1,0:T(8,128)(2,1)} %get-tuple-element.644) | copy-start | bytes 786436
  173.1 16.2 %all-to-all-start.3 = ((bf16[8,360,128]{2,1,0:T(8,128)(2,1)}), bf16[8,360,128]{2,1,0:T(8,128)(2,1)S(1)}, u32[]{:S(2)}, u32[]{:S(2)}) async-start(bf16[8,360,128]{2,1,0:T(8,128)(2,1)} %reshape.387), calls=%async_computation.3 | async-start | bytes 1474560 | tf_op jit(solution)/shard_map/all_to_all | solution.py:177
  176.8 91.5 %all-gather.5.cloned.1.call-start = ((), (), s32[]{:S(2)}) async-start(), calls=%async_computation.7 | async-start | bytes 4976640 | tf_op jit(solution)/shard_map/all_gather | solution.py:201
  216.0 124.0 %reduce-scatter.2.cloned.1.call-start = ((), (), s32[]{:S(2)}) async-start(), calls=%async_computation.8 | async-start | bytes 4976640 | tf_op jit(solution)/shard_map/reduce_scatter | solution.py:217
  219.4 52.3 %copy-start.10 = (f32[2880]{0:T(1024)S(1)}, f32[2880]{0:T(1024)}, u32[]{:S(2)}) copy-start(f32[2880]{0:T(1024)} %param.25) | copy-start | bytes 34564
  268.3 3.6 copy-start
  268.3 7.7 %slice-start.1 = ((s8[4239360]{0:T(1024)(128)(4,1)}), s8[4194304]{0:T(1024)(128)(4,1)S(1)}, s32[]{:S(2)}) async-start(s8[4239360]{0:T(1024)(128)(4,1)} %bitcast.219), calls=%async_computation.11 | async-start | bytes 8388608
  271.9 4.1 %slice-start.2 = ((s8[4239360]{0:T(1024)(128)(4,1)}), s8[45056]{0:T(1024)(128)(4,1)S(1)}, s32[]{:S(2)}) async-start(s8[4239360]{0:T(1024)(128)(4,1)} %bitcast.219), calls=%async_computation.12 | async-start | bytes 90112
  282.9 68.1 %copy-start.8 = (f32[1,128,4]{1,2,0:T(4,128)S(1)}, f32[1,128,4]{1,2,0:T(4,128)}, u32[]{:S(2)}) copy-start(f32[1,128,4]{1,2,0:T(4,128)} %param.29) | copy-start | bytes 6148
  342.0 26.4 %all-to-all-start.5 = ((bf16[16,48,360]{2,1,0:T(8,128)(2,1)}), bf16[16,48,360]{2,1,0:T(8,128)(2,1)S(1)}, u32[]{:S(2)}, u32[]{:S(2)}) async-start(bf16[16,48,360]{2,1,0:T(8,128)(2,1)} %bitcast.40), calls=%async_computation.6 | async-start | bytes 1179648 | tf_op jit(solution)/shard_map/all_to_all | solution.py:221
Sparse Core Ops, SparseCore 0:
  10.6 132.7 all-gather.6
  216.1 52.1 all-gather.4
  283.0 56.8 reduce-scatter.1

commit v9 on v8

--- a/solution.py
+++ b/solution.py
@@ -83,16 +83,23 @@
     input_normalised = rms_norm(whole_rows, attn_gain)
     query_cols = w_query.shape[1]
     kv_cols = key_weight.shape[1]
-    big_weights = lax.all_gather(jnp.concatenate([w_query, w_out.T], axis=1), "expert", axis=0)
-    query_weight = big_weights[:, :, :query_cols]
+    shard_rows = w_query.shape[0]
+    padded_rows = -(-shard_rows // 8) * 8
+    big_weights = lax.all_gather(
+        jnp.pad(
+            jnp.concatenate([w_query, w_out.T], axis=1), ((0, padded_rows - shard_rows), (0, 0))
+        ),
+        "expert",
+        axis=0,
+    )
+    query_weight = big_weights[:, :, :query_cols].reshape(expert_devs * padded_rows, query_cols)
     out_weight_t = big_weights[:, :, query_cols:]
     kv_weight = gather_by_exchange(jnp.concatenate([key_weight, value_weight], axis=1), "expert")
-    query_raw = jnp.einsum(
-        "tef,efc->tc",
-        input_normalised.reshape(tok_count, expert_devs, -1),
-        query_weight,
-        preferred_element_type=jnp.float32,
-    )
+    normed_padded = jnp.pad(
+        input_normalised.reshape(tok_count, expert_devs, shard_rows),
+        ((0, 0), (0, 0), (0, padded_rows - shard_rows)),
+    ).reshape(tok_count, expert_devs * padded_rows)
+    query_raw = jnp.dot(normed_padded, query_weight, preferred_element_type=jnp.float32)
     kv_raw = jnp.dot(input_normalised, kv_weight, preferred_element_type=jnp.float32)
     key_raw = kv_raw[:, :kv_cols]
     value_raw = kv_raw[:, kv_cols:]
@@ -171,7 +178,7 @@
     )
     out_terms_t = jnp.einsum(
         "efc,tc->eft", out_weight_t, mixed, preferred_element_type=jnp.float32
-    )
+    )[:, :shard_rows]
     model_width = out_terms_t.shape[0] * out_terms_t.shape[1]
     out_pieces = out_terms_t.astype(jnp.bfloat16).reshape(mp_devs, model_width // mp_devs, tok_count)
     out_got = lax.all_to_all(out_pieces, "mp", split_axis=0, concat_axis=0, tiled=True)

time: 379 us -> 382 us (level)
    dot_general x8, matrix products: 5.7 us -> 13 us  [block_scores(): jnp.einsum('hrd,hkd->hrk', query_rows, key_part, preferred_element_type=j...]
    unnamed x33 -> x30, local copies, waits for them, and re-layouts: 7.13 us -> 1.46 us
    dot_general x1, matrix products: 6.06 us -> 2.07 us  [shards(): jnp.dot(normed_padded, query_weight, preferred_element_type=jnp.float32)]
where the time goes in v9:
time: 382 us; the launch traced here: 381 us
  waiting for transfers between devices  235 us (62%)
  matrix products  34.3 us (9%)
  starting transfers between devices  33.9 us (9%)
  local copies, waits for them, and re-layouts  32 us (8%)
  blocking collectives  22.8 us (6%)
  between operations  14.3 us (4%)
  other arithmetic  9.24 us (2%)
    reduce_scatter x1, waiting for transfers between devices, shards(): lax.psum_scatter(partials.astype(jnp.bfloat16), 'mp', scatter_dimension=0...  57 us
    all_to_all x3, waiting for transfers between devices, gather_by_exchange(): lax.all_to_all(spread, axis_name, split_axis=0, concat_axis=0, tiled=True)  54.6 us
    all_gather x1, waiting for transfers between devices, shards(): lax.all_gather(arrived_rows, 'mp', axis=1, tiled=True)  48.7 us
    all_gather x1, waiting for transfers between devices, shards(): lax.all_gather(jnp.pad(jnp.concatenate([w_query, w_out.T], axis=1), ((0,...  48.2 us
    all_to_all x1, blocking collectives, shards(): lax.all_to_all(outgoing, 'expert', split_axis=0, concat_axis=0, tiled=True)  22.8 us
    all_to_all x3, starting transfers between devices, gather_by_exchange(): lax.all_to_all(spread, axis_name, split_axis=0, concat_axis=0, tiled=True)  21 us
    all_to_all x1, waiting for transfers between devices, shards(): lax.all_to_all(expert_out, 'expert', split_axis=0, concat_axis=0, tiled=T...  16 us
    dot_general x8, matrix products, block_scores(): jnp.einsum('hrd,hkd->hrk', query_rows, key_part, preferred_element_type=j...  13 us
  transfers between devices with their start and end apart: 8, of which 8 were waited for; matrix products, arithmetic and copies ran while one was open for 5% of the time, Pallas kernels for 0%

profile of v9, /device:TPU:1, one launch (start us, length us, event | category | flops | bytes accessed | tf_op | source)
XLA Modules:
  0.0 381.2 jit_solution(6319409999395095673)
XLA Ops:
  7.2 1.8 fusion.62
  9.1 1.9 broadcast_in_dim.92
  10.9 6.0 %all-to-all-start = ((bf16[8,360,128]{2,1,0:T(8,128)(2,1)}), bf16[8,360,128]{2,1,0:T(8,128)(2,1)S(1)}, u32[]{:S(2)}, u32[]{:S(2)}) async-start(bf16[8,360,128]{2,1,0:T(8,128)(2,1)} %broadcast_in_dim.92), calls=%async_computation | async-start | bytes 1474560 | tf_op jit(solution)/shard_map/all_to_all | solution.py:45
  17.1 12.3 %all-to-all-done = bf16[8,360,128]{2,1,0:T(8,128)(2,1)S(1)} async-done(((bf16[8,360,128]{2,1,0:T(8,128)(2,1)}), bf16[8,360,128]{2,1,0:T(8,128)(2,1)S(1)}, u32[]{:S(2)}, u32[]{:S(2)}) %all-to-all-start) | async-done | bytes 737312 | tf_op jit(solution)/shard_map/all_to_all | solution.py:45
  29.4 1.0 broadcast_in_dim.93
  30.4 10.6 %all-to-all-start.1 = ((bf16[16,180,128]{2,1,0:T(8,128)(2,1)}), bf16[16,180,128]{2,1,0:T(8,128)(2,1)S(1)}, u32[]{:S(2)}, u32[]{:S(2)}) async-start(bf16[16,180,128]{2,1,0:T(8,128)(2,1)} %broadcast_in_dim.93), calls=%async_computation.1 | async-start | bytes 1507328 | tf_op jit(solution)/shard_map/all_to_all | solution.py:45
  41.6 0.4 fusion.36
  42.1 0.5 fusion.38
  42.5 26.9 %all-to-all-done.1 = bf16[16,180,128]{2,1,0:T(8,128)(2,1)S(1)} async-done(((bf16[16,180,128]{2,1,0:T(8,128)(2,1)}), bf16[16,180,128]{2,1,0:T(8,128)(2,1)S(1)}, u32[]{:S(2)}, u32[]{:S(2)}) %all-to-all-start.1) | async-done | bytes 737312 | tf_op jit(solution)/shard_map/all_to_all | solution.py:45
  69.6 0.4 fusion.86
  70.0 0.1 fusion.77
  70.3 0.9 broadcast_in_dim.94
  71.2 4.4 %all-to-all-start.2 = ((bf16[16,128,128]{2,1,0:T(8,128)(2,1)}), bf16[16,128,128]{2,1,0:T(8,128)(2,1)S(1)}, u32[]{:S(2)}, u32[]{:S(2)}) async-start(bf16[16,128,128]{2,1,0:T(8,128)(2,1)} %broadcast_in_dim.94), calls=%async_computation.2 | async-start | bytes 1048576 | tf_op jit(solution)/shard_map/all_to_all | solution.py:45
  75.7 1.2 reduce-window.6
  76.8 0.2 slice_reduce_fusion
  77.4 0.1 multiply_cosine_fusion
  77.7 0.9 pad.10
  78.7 15.4 %all-to-all-done.2 = bf16[16,128,128]{2,1,0:T(8,128)(2,1)S(1)} async-done(((bf16[16,128,128]{2,1,0:T(8,128)(2,1)}), bf16[16,128,128]{2,1,0:T(8,128)(2,1)S(1)}, u32[]{:S(2)}, u32[]{:S(2)}) %all-to-all-start.2) | async-done | bytes 524320 | tf_op jit(solution)/shard_map/all_to_all | solution.py:45
  94.1 1.2 slice_bitcast_fusion
  95.3 48.2 %all-gather.6.cloned.1.call-done = bf16[2944,1024]{1,0:T(8,128)(2,1)} async-done(((bf16[184,1024]{1,0:T(8,128)(2,1)}), bf16[2944,1024]{1,0:T(8,128)(2,1)}) %all-gather.6.cloned.1.call-update) | async-done | bytes 6029328 | tf_op jit(solution)/shard_map/all_gather | solution.py:88
  143.4 3.8 slice.74
  147.2 3.3 copy.87
  150.6 2.1 fusion.87
  152.7 0.2 copy.110
  152.9 6.5 %while.30 = (s32[]{:T(128)}, f32[1,1024]{1,0:T(1,128)S(1)}, s32[2048]{0:T(1024)S(1)}, bf16[1,2048,64]{2,1,0:T(8,128)(2,1)}, bf16[1,1024,64]{2,1,0:T(8,128)(2,1)S...) while((s32[]{:T(128)}, f32[1,1024]{1,0:T(1,128)S(1)}, ...), condition=%wide.region_3.4_spmd.clone, body=%wide.region_1.3_spmd.clone.sunk | while | flops 70255112 | bytes 306343 | solution.py:155
  153.0 1.5 fusion.104
  154.6 1.5 fusion.104
  156.3 1.5 fusion.104
  157.9 1.5 fusion.104
  159.4 12.6 %while.31 = (s32[]{:T(128)}, f32[1,1024,64]{1,2,0:T(8,128)S(1)}, f32[1,1024]{1,0:T(1,128)S(1)}, s32[2048]{0:T(1024)S(1)}, bf16[1,2048,64]{2,1,0:T(8,128)(2,1)}, ...) while((s32[]{:T(128)}, f32[1,1024,64]{1,2,0:T(8,128)S(1)}, ...), condition=%wide.region_6.7_spmd.clone, body=%wide.region_4.6_spmd.clone.sunk | while | flops 139068928 | bytes 3062990 | solution.py:171
  159.5 1.7 convert_reduce_fusion.3
  161.3 1.3 fusion.107
  162.7 1.7 convert_reduce_fusion.3
  164.4 1.3 fusion.107
  165.8 1.7 convert_reduce_fusion.3
  167.6 1.3 fusion.107
  169.0 1.7 convert_reduce_fusion.3
  170.7 1.3 fusion.107
  172.1 2.8 fusion.28
  175.0 1.0 reshape.395
  176.0 3.6 all-to-all-start.3
  179.6 2.4 scatter_custom_fusion
  182.1 9.9 %all-to-all-done.3 = bf16[8,360,128]{2,1,0:T(8,128)(2,1)S(1)} async-done(((bf16[8,360,128]{2,1,0:T(8,128)(2,1)}), bf16[8,360,128]{2,1,0:T(8,128)(2,1)S(1)}, u32[]{:S(2)}, u32[]{:S(2)}) %all-to-all-start.3) | async-done | bytes 737312 | tf_op jit(solution)/shard_map/all_to_all | solution.py:184
  192.3 2.6 gather_fusion
  194.9 22.8 %all_to_all.30 = bf16[16,48,360]{2,1,0:T(8,128)(2,1)S(1)} all-to-all(bf16[16,48,360]{2,1,0:T(8,128)(2,1)S(1)} %bitcast.199), channel_id=1, replica_groups=mesh['expert'=16,'mp'=8,'batch'=2] {'expert'}, dimensions={0} | all-to-all | bytes 1105920 | tf_op jit(solution)/shard_map/all_to_all | solution.py:206
  217.7 1.1 copy.99
  218.8 0.2 reduce-scatter.2.cloned.1.call-start
  219.0 3.4 copy.109
  222.4 48.7 %all-gather.4.cloned.1.call-done = bf16[768,2880]{0,1:T(8,128)(2,1)} async-done(((bf16[768,360]{0,1:T(8,128)(2,1)}), bf16[768,2880]{0,1:T(8,128)(2,1)}) %all-gather.4.cloned.1.call-update) | async-done | bytes 4423696 | tf_op jit(solution)/shard_map/all_gather | solution.py:208
  271.1 3.3 fusion.25
  274.5 0.2 copy-done
  274.7 4.1 %fusion.39 = f32[768,360]{0,1:T(8,128)S(1)} fusion(bf16[1,2,2880,360]{2,3,1,0:T(8,128)(2,1)} %param.26, bf16[768,2880]{0,1:T(8,128)(2,1)S(1)} %copy-done, f32[2880]{0:T(1024)S(1)} %copy-done.9, f32[768]{0:T(1024)S(1)} %add_rsqrt_fusion), kind=kOutput, calls=%fused_computation.56 | convolution fusion | flops 1601648640 | bytes 7663872 | tf_op jit(solution)/shard_map/dot_general | solution.py:210
  278.8 2.4 fusion.54
  281.2 4.5 %convert_bitcast_fusion = bf16[8,768,360]{1,2,0:T(8,128)(2,1)} fusion(bf16[360,8,360]{0,2,1:T(8,128)(2,1)S(1)} %bitcast.201, bf16[768,360]{0,1:T(8,128)(2,1)S(1)} %fusion.54), kind=kOutput, calls=%fused_computation.40 | convolution fusion | flops 1594736640 | bytes 7050240 | tf_op jit(solution)/shard_map/rh,hjf->jrf/dot_general | solution.py:218
  285.7 57.0 %reduce-scatter.2.cloned.1.call-done = bf16[1,768,360]{1,2,0:T(8,128)(2,1)} async-done(((bf16[8,768,360]{1,2,0:T(8,128)(2,1)}), bf16[1,768,360]{1,2,0:T(8,128)(2,1)}) %reduce-scatter.2.cloned.1.call-update) | async-done | bytes 552976 | tf_op jit(solution)/shard_map/reduce_scatter | solution.py:224
  342.7 2.1 copy.101
  344.9 9.0 %all-to-all-start.5 = ((bf16[16,48,360]{2,1,0:T(8,128)(2,1)}), bf16[16,48,360]{2,1,0:T(8,128)(2,1)S(1)}, u32[]{:S(2)}, u32[]{:S(2)}) async-start(bf16[16,48,360]{2,1,0:T(8,128)(2,1)} %bitcast.40), calls=%async_computation.6 | async-start | bytes 1179648 | tf_op jit(solution)/shard_map/all_to_all | solution.py:228
  354.0 0.6 pad_maximum_fusion.2
  354.6 0.6 slice_bitcast_fusion.3
  355.2 16.0 %all-to-all-done.5 = bf16[16,48,360]{2,1,0:T(8,128)(2,1)S(1)} async-done(((bf16[16,48,360]{2,1,0:T(8,128)(2,1)}), bf16[16,48,360]{2,1,0:T(8,128)(2,1)S(1)}, u32[]{:S(2)}, u32[]{:S(2)}) %all-to-all-start.5) | async-done | bytes 552992 | tf_op jit(solution)/shard_map/all_to_all | solution.py:228
  371.2 1.9 gather_fusion.1
  373.2 0.2 reshape.402
  373.4 0.5 multiply_reduce_fusion
  373.9 0.7 copy.103
  (106 shorter events, 3.0 us)
Async XLA Ops:
  7.2 9.7 %copy-start.4 = (bf16[180,64]{0,1:T(8,128)(2,1)S(1)}, bf16[180,64]{0,1:T(8,128)(2,1)}, u32[]{:S(2)}) copy-start(bf16[180,64]{0,1:T(8,128)(2,1)} %param.21) | copy-start | bytes 69124
  7.2 9.7 %copy-start.3 = (bf16[180,64]{0,1:T(8,128)(2,1)S(1)}, bf16[180,64]{0,1:T(8,128)(2,1)}, u32[]{:S(2)}) copy-start(bf16[180,64]{0,1:T(8,128)(2,1)} %param.22) | copy-start | bytes 69124
  7.2 136.3 %all-gather.6.cloned.1.call-start = ((), (), s32[]{:S(2)}) async-start(), calls=%async_computation.9 | async-start | bytes 6406144 | tf_op jit(solution)/shard_map/all_gather | solution.py:88
  10.9 30.1 %copy-start.1 = (bf16[1,128,360]{1,2,0:T(8,128)(2,1)S(1)}, bf16[1,128,360]{1,2,0:T(8,128)(2,1)}, u32[]{:S(2)}) copy-start(bf16[1,128,360]{1,2,0:T(8,128)(2,1)} %param.17) | copy-start | bytes 276484
  10.9 30.3 %copy-start.6 = (s32[1,128,4]{1,2,0:T(4,128)S(1)}, s32[1,128,4]{1,2,0:T(4,128)}, u32[]{:S(2)}) copy-start(s32[1,128,4]{1,2,0:T(4,128)} %param.28) | copy-start | bytes 6148
  10.9 30.6 %copy-start.8 = (f32[8]{0:T(128)S(1)}, f32[8]{0:T(128)}, u32[]{:S(2)}) copy-start(f32[8]{0:T(128)} %param.24) | copy-start | bytes 100
  10.9 18.5 %all-to-all-start = ((bf16[8,360,128]{2,1,0:T(8,128)(2,1)}), bf16[8,360,128]{2,1,0:T(8,128)(2,1)S(1)}, u32[]{:S(2)}, u32[]{:S(2)}) async-start(bf16[8,360,128]{2,1,0:T(8,128)(2,1)} %broadcast_in_dim.92), calls=%async_computation | async-start | bytes 1474560 | tf_op jit(solution)/shard_map/all_to_all | solution.py:45
  16.9 25.2 %copy-start.5 = (f32[2880]{0:T(1024)S(1)}, f32[2880]{0:T(1024)}, u32[]{:S(2)}) copy-start(f32[2880]{0:T(1024)} %param.19) | copy-start | bytes 34564
  30.4 39.0 %all-to-all-start.1 = ((bf16[16,180,128]{2,1,0:T(8,128)(2,1)}), bf16[16,180,128]{2,1,0:T(8,128)(2,1)S(1)}, u32[]{:S(2)}, u32[]{:S(2)}) async-start(bf16[16,180,128]{2,1,0:T(8,128)(2,1)} %broadcast_in_dim.93), calls=%async_computation.1 | async-start | bytes 1507328 | tf_op jit(solution)/shard_map/all_to_all | solution.py:45
  69.6 7.8 %copy-start.2 = (s32[1,2048]{1,0:T(1,128)S(1)}, s32[1,2048]{1,0:T(1,128)}, u32[]{:S(2)}) copy-start(s32[1,2048]{1,0:T(1,128)} %param.18) | copy-start | bytes 24580
  71.2 22.8 %all-to-all-start.2 = ((bf16[16,128,128]{2,1,0:T(8,128)(2,1)}), bf16[16,128,128]{2,1,0:T(8,128)(2,1)S(1)}, u32[]{:S(2)}, u32[]{:S(2)}) async-start(bf16[16,128,128]{2,1,0:T(8,128)(2,1)} %broadcast_in_dim.94), calls=%async_computation.2 | async-start | bytes 1048576 | tf_op jit(solution)/shard_map/all_to_all | solution.py:45
  176.0 16.0 %all-to-all-start.3 = ((bf16[8,360,128]{2,1,0:T(8,128)(2,1)}), bf16[8,360,128]{2,1,0:T(8,128)(2,1)S(1)}, u32[]{:S(2)}, u32[]{:S(2)}) async-start(bf16[8,360,128]{2,1,0:T(8,128)(2,1)} %reshape.395), calls=%async_computation.3 | async-start | bytes 1474560 | tf_op jit(solution)/shard_map/all_to_all | solution.py:184
  179.5 91.6 %all-gather.4.cloned.1.call-start = ((), (), s32[]{:S(2)}) async-start(), calls=%async_computation.7 | async-start | bytes 4976640 | tf_op jit(solution)/shard_map/all_gather | solution.py:208
  218.8 124.0 %reduce-scatter.2.cloned.1.call-start = ((), (), s32[]{:S(2)}) async-start(), calls=%async_computation.8 | async-start | bytes 4976640 | tf_op jit(solution)/shard_map/reduce_scatter | solution.py:224
  222.4 52.1 %copy-start.9 = (f32[2880]{0:T(1024)S(1)}, f32[2880]{0:T(1024)}, u32[]{:S(2)}) copy-start(f32[2880]{0:T(1024)} %param.25) | copy-start | bytes 34564
  271.1 3.6 copy-start
  271.1 7.7 %slice-start = ((s8[4239360]{0:T(1024)(128)(4,1)}), s8[4194304]{0:T(1024)(128)(4,1)S(1)}, s32[]{:S(2)}) async-start(s8[4239360]{0:T(1024)(128)(4,1)} %bitcast.225), calls=%async_computation.10 | async-start | bytes 8388608
  274.7 4.1 %slice-start.1 = ((s8[4239360]{0:T(1024)(128)(4,1)}), s8[45056]{0:T(1024)(128)(4,1)S(1)}, s32[]{:S(2)}) async-start(s8[4239360]{0:T(1024)(128)(4,1)} %bitcast.225), calls=%async_computation.11 | async-start | bytes 90112
  285.7 68.2 %copy-start.7 = (f32[1,128,4]{1,2,0:T(4,128)S(1)}, f32[1,128,4]{1,2,0:T(4,128)}, u32[]{:S(2)}) copy-start(f32[1,128,4]{1,2,0:T(4,128)} %param.29) | copy-start | bytes 6148
  344.9 26.4 %all-to-all-start.5 = ((bf16[16,48,360]{2,1,0:T(8,128)(2,1)}), bf16[16,48,360]{2,1,0:T(8,128)(2,1)S(1)}, u32[]{:S(2)}, u32[]{:S(2)}) async-start(bf16[16,48,360]{2,1,0:T(8,128)(2,1)} %bitcast.40), calls=%async_computation.6 | async-start | bytes 1179648 | tf_op jit(solution)/shard_map/all_to_all | solution.py:228
Sparse Core Ops, SparseCore 0:
  10.6 132.7 all-gather.5
  218.9 52.1 all-gather.3
  285.8 56.8 reduce-scatter.1

commit v10 on v8

--- a/solution.py
+++ b/solution.py
@@ -126,7 +126,7 @@
     row_pos = jnp.tile(token_positions, heads_per_group)
     row_seg = jnp.tile(seg_local, heads_per_group)
     sink_rows = jnp.repeat(sink_head_logit.reshape(kv_heads, heads_per_group), tok_count, axis=1)
-    key_block = math.gcd(seq_len, 512)
+    key_block = math.gcd(seq_len, 1024)
     block_count = seq_len // key_block
     score_scale = HEAD_SIZE ** (-0.5)
 
@@ -195,7 +195,14 @@
     padded = jnp.concatenate(
         [first_out, jnp.zeros((1, first_out.shape[1]), jnp.bfloat16)], axis=0
     )
-    outgoing = padded[source_row].reshape(expert_count, capacity, padded.shape[1])
+    pick = (source_row[:, None] == jnp.arange(tok_count + 1, dtype=jnp.int32)[None, :]).astype(
+        jnp.bfloat16
+    )
+    outgoing = (
+        jnp.dot(pick, padded, preferred_element_type=jnp.float32)
+        .astype(jnp.bfloat16)
+        .reshape(expert_count, capacity, padded.shape[1])
+    )
     arrived = lax.all_to_all(outgoing, "expert", split_axis=0, concat_axis=0, tiled=True)
     arrived_rows = arrived.reshape(expert_count * capacity, arrived.shape[2])
     inputs = rms_norm(lax.all_gather(arrived_rows, "mp", axis=1, tiled=True), moe_gain)

time: 379 us -> 378 us (level)
    dot_general x8 -> x4, matrix products: 5.7 us -> 9.85 us  [block_scores(): jnp.einsum('hrd,hkd->hrk', query_rows, key_part, preferred_element_type=j...]
    dot_general x4 -> x2, matrix products: 5.08 us -> 1.12 us  [sum_step(): jnp.einsum('hrk,hkd->hrd', probs, value_part, preferred_element_type=jnp....]
where the time goes in v10:
time: 378 us; the launch traced here: 377 us
  waiting for transfers between devices  233 us (62%)
  starting transfers between devices  33.9 us (9%)
  matrix products  31.7 us (8%)
  local copies, waits for them, and re-layouts  30 us (8%)
  blocking collectives  22.1 us (6%)
  between operations  14.2 us (4%)
  other arithmetic  11.2 us (3%)
    reduce_scatter x1, waiting for transfers between devices, shards(): lax.psum_scatter(partials.astype(jnp.bfloat16), 'mp', scatter_dimension=0...  57.1 us
    all_to_all x3, waiting for transfers between devices, gather_by_exchange(): lax.all_to_all(spread, axis_name, split_axis=0, concat_axis=0, tiled=True)  54.8 us
    all_gather x1, waiting for transfers between devices, shards(): lax.all_gather(arrived_rows, 'mp', axis=1, tiled=True)  49.1 us
    all_gather x1, waiting for transfers between devices, shards(): lax.all_gather(jnp.concatenate([w_query, w_out.T], axis=1), 'expert', axi...  47.1 us
    all_to_all x1, blocking collectives, shards(): lax.all_to_all(outgoing, 'expert', split_axis=0, concat_axis=0, tiled=True)  22.1 us
    all_to_all x3, starting transfers between devices, gather_by_exchange(): lax.all_to_all(spread, axis_name, split_axis=0, concat_axis=0, tiled=True)  20.7 us
    all_to_all x1, waiting for transfers between devices, shards(): lax.all_to_all(expert_out, 'expert', split_axis=0, concat_axis=0, tiled=T...  16 us
    dot_general x4, matrix products, block_scores(): jnp.einsum('hrd,hkd->hrk', query_rows, key_part, preferred_element_type=j...  9.85 us
  transfers between devices with their start and end apart: 8, of which 8 were waited for; matrix products, arithmetic and copies ran while one was open for 5% of the time, Pallas kernels for 0%

profile of v10, /device:TPU:1, one launch (start us, length us, event | category | flops | bytes accessed | tf_op | source)
XLA Modules:
  0.0 376.8 jit_solution(10049264227437132683)
XLA Ops:
  7.2 1.8 maximum_bitcast_fusion
  9.1 1.9 broadcast_in_dim.91
  10.9 5.9 %all-to-all-start = ((bf16[8,360,128]{2,1,0:T(8,128)(2,1)}), bf16[8,360,128]{2,1,0:T(8,128)(2,1)S(1)}, u32[]{:S(2)}, u32[]{:S(2)}) async-start(bf16[8,360,128]{2,1,0:T(8,128)(2,1)} %broadcast_in_dim.91), calls=%async_computation | async-start | bytes 1474560 | tf_op jit(solution)/shard_map/all_to_all | solution.py:45
  16.8 0.8 pad_maximum_fusion
  17.7 11.6 %all-to-all-done = bf16[8,360,128]{2,1,0:T(8,128)(2,1)S(1)} async-done(((bf16[8,360,128]{2,1,0:T(8,128)(2,1)}), bf16[8,360,128]{2,1,0:T(8,128)(2,1)S(1)}, u32[]{:S(2)}, u32[]{:S(2)}) %all-to-all-start) | async-done | bytes 737312 | tf_op jit(solution)/shard_map/all_to_all | solution.py:45
  29.3 1.0 broadcast_in_dim.92
  30.2 10.8 %all-to-all-start.1 = ((bf16[16,180,128]{2,1,0:T(8,128)(2,1)}), bf16[16,180,128]{2,1,0:T(8,128)(2,1)S(1)}, u32[]{:S(2)}, u32[]{:S(2)}) async-start(bf16[16,180,128]{2,1,0:T(8,128)(2,1)} %broadcast_in_dim.92), calls=%async_computation.1 | async-start | bytes 1507328 | tf_op jit(solution)/shard_map/all_to_all | solution.py:45
  41.0 0.4 fusion.38
  41.5 0.5 fusion.40
  41.9 28.1 %all-to-all-done.1 = bf16[16,180,128]{2,1,0:T(8,128)(2,1)S(1)} async-done(((bf16[16,180,128]{2,1,0:T(8,128)(2,1)}), bf16[16,180,128]{2,1,0:T(8,128)(2,1)S(1)}, u32[]{:S(2)}, u32[]{:S(2)}) %all-to-all-start.1) | async-done | bytes 737312 | tf_op jit(solution)/shard_map/all_to_all | solution.py:45
  70.0 0.1 reshape.381
  70.2 0.4 fusion.94
  70.6 0.1 fusion.84
  70.9 0.9 broadcast_in_dim.93
  71.8 4.1 %all-to-all-start.2 = ((bf16[16,128,128]{2,1,0:T(8,128)(2,1)}), bf16[16,128,128]{2,1,0:T(8,128)(2,1)S(1)}, u32[]{:S(2)}, u32[]{:S(2)}) async-start(bf16[16,128,128]{2,1,0:T(8,128)(2,1)} %broadcast_in_dim.93), calls=%async_computation.2 | async-start | bytes 1048576 | tf_op jit(solution)/shard_map/all_to_all | solution.py:45
  75.9 0.1 copy.86
  76.1 0.7 eq.112
  76.9 1.2 reduce-window.6
  78.0 0.2 slice_reduce_fusion
  78.3 0.8 multiply_cosine_fusion
  79.1 1.0 reshape.421
  80.1 15.1 %all-to-all-done.2 = bf16[16,128,128]{2,1,0:T(8,128)(2,1)S(1)} async-done(((bf16[16,128,128]{2,1,0:T(8,128)(2,1)}), bf16[16,128,128]{2,1,0:T(8,128)(2,1)S(1)}, u32[]{:S(2)}, u32[]{:S(2)}) %all-to-all-start.2) | async-done | bytes 524320 | tf_op jit(solution)/shard_map/all_to_all | solution.py:45
  95.2 1.2 slice_bitcast_fusion
  96.3 47.1 %all-gather.7.cloned.1.call-done = bf16[16,180,1024]{2,1,0:T(8,128)(2,1)} async-done(((bf16[1,180,1024]{2,1,0:T(8,128)(2,1)}), bf16[16,180,1024]{2,1,0:T(8,128)(2,1)}) %all-gather.7.cloned.1.call-update) | async-done | bytes 5898256 | tf_op jit(solution)/shard_map/all_gather | solution.py:86
  143.4 2.1 slice.67
  145.5 5.7 %copy.101 = bf16[16,180,512]{1,0,2:T(8,128)(2,1)} copy(bf16[16,180,512]{2,1,0:T(8,128)(2,1)S(1)} %slice.67) | data formatting | bytes 5898240
  151.2 6.1 %fusion.64 = f32[128,8,64]{0,2,1:T(8,128)S(1)} fusion(bf16[128,16,180,1]{0,2,1,3:T(8,128)(2,1)} %reshape.421, bf16[8,64,16,180]{3,2,1,0:T(8,128)(2,1)} %bitcast.195), kind=kOutput, calls=%fused_computation.64 | convolution fusion | flops 377487360 | bytes 3948544 | tf_op jit(solution)/shard_map/tef,efc->tc/dot_general | solution.py:90
  157.4 0.9 copy.99
  158.2 4.6 %while.30 = (s32[]{:T(128)}, f32[1,1024]{1,0:T(1,128)S(1)}, s32[2048]{0:T(1024)S(1)}, bf16[1,2048,64]{2,1,0:T(8,128)(2,1)S(1)}, bf16[1,1024,64]{2,1,0:T(8,128)(2...) while((s32[]{:T(128)}, f32[1,1024]{1,0:T(1,128)S(1)}, ...), condition=%wide.region_3.4_spmd.clone, body=%wide.region_1.3_spmd.clone.sunk | while | flops 140510208 | bytes 447655 | solution.py:148
  158.2 2.2 fusion.110
  160.6 2.2 fusion.110
  162.8 6.7 %while.31 = (s32[]{:T(128)}, f32[1,1024,64]{1,2,0:T(8,128)S(1)}, f32[1,1024]{1,0:T(1,128)S(1)}, s32[2048]{0:T(1024)S(1)}, bf16[1,2048,64]{2,1,0:T(8,128)(2,1)S(1...) while((s32[]{:T(128)}, f32[1,1024,64]{1,2,0:T(8,128)S(1)}, ...), condition=%wide.region_6.7_spmd.clone, body=%wide.region_4.6_spmd.clone.sunk | while | flops 278005760 | bytes 5432526 | solution.py:164
  162.9 2.7 convert_reduce_fusion.3
  165.6 0.6 fusion.113
  166.2 2.7 convert_reduce_fusion.3
  168.9 0.6 fusion.113
  169.7 2.8 fusion.41
  172.5 1.0 reshape.388
  173.5 4.0 %all-to-all-start.3 = ((bf16[8,360,128]{2,1,0:T(8,128)(2,1)}), bf16[8,360,128]{2,1,0:T(8,128)(2,1)S(1)}, u32[]{:S(2)}, u32[]{:S(2)}) async-start(bf16[8,360,128]{2,1,0:T(8,128)(2,1)} %reshape.388), calls=%async_computation.3 | async-start | bytes 1474560 | tf_op jit(solution)/shard_map/all_to_all | solution.py:177
  177.5 0.2 all-gather.5.cloned.1.call-start
  178.1 2.4 scatter_custom_fusion
  180.6 9.4 %all-to-all-done.3 = bf16[8,360,128]{2,1,0:T(8,128)(2,1)S(1)} async-done(((bf16[8,360,128]{2,1,0:T(8,128)(2,1)}), bf16[8,360,128]{2,1,0:T(8,128)(2,1)S(1)}, u32[]{:S(2)}, u32[]{:S(2)}) %all-to-all-start.3) | async-done | bytes 737312 | tf_op jit(solution)/shard_map/all_to_all | solution.py:177
  190.1 0.4 convolution_convert_fusion
  190.6 0.3 copy.89
  190.9 22.1 %all_to_all.30 = bf16[16,48,360]{2,1,0:T(8,128)(2,1)S(1)} all-to-all(bf16[16,48,360]{2,1,0:T(8,128)(2,1)S(1)} %bitcast.196), channel_id=1, replica_groups=mesh['expert'=16,'mp'=8,'batch'=2] {'expert'}, dimensions={0} | all-to-all | bytes 1105920 | tf_op jit(solution)/shard_map/all_to_all | solution.py:206
  213.0 1.1 copy.90
  214.2 3.4 copy.98
  217.5 49.1 %all-gather.5.cloned.1.call-done = bf16[768,2880]{0,1:T(8,128)(2,1)} async-done(((bf16[768,360]{0,1:T(8,128)(2,1)}), bf16[768,2880]{0,1:T(8,128)(2,1)}) %all-gather.5.cloned.1.call-update) | async-done | bytes 4423696 | tf_op jit(solution)/shard_map/all_gather | solution.py:208
  266.7 3.3 fusion.25
  270.0 0.2 copy-done.1
  270.2 4.1 %fusion.44 = f32[768,360]{0,1:T(8,128)S(1)} fusion(bf16[1,2,2880,360]{2,3,1,0:T(8,128)(2,1)} %param.26, bf16[768,2880]{0,1:T(8,128)(2,1)S(1)} %copy-done.1, f32[2880]{0:T(1024)S(1)} %copy-done.14, f32[768]{0:T(1024)S(1)} %add_rsqrt_fusion), kind=kOutput, calls=%fused_computation.57 | convolution fusion | flops 1601648640 | bytes 7663872 | tf_op jit(solution)/shard_map/dot_general | solution.py:210
  274.3 2.4 fusion.59
  276.7 4.5 %convert_bitcast_fusion = bf16[8,768,360]{1,2,0:T(8,128)(2,1)} fusion(bf16[360,8,360]{0,2,1:T(8,128)(2,1)S(1)} %bitcast.198, bf16[768,360]{0,1:T(8,128)(2,1)S(1)} %fusion.59), kind=kOutput, calls=%fused_computation.39 | convolution fusion | flops 1594736640 | bytes 7050240 | tf_op jit(solution)/shard_map/rh,hjf->jrf/dot_general | solution.py:218
  281.3 57.1 %reduce-scatter.2.cloned.1.call-done = bf16[1,768,360]{1,2,0:T(8,128)(2,1)} async-done(((bf16[8,768,360]{1,2,0:T(8,128)(2,1)}), bf16[1,768,360]{1,2,0:T(8,128)(2,1)}) %reduce-scatter.2.cloned.1.call-update) | async-done | bytes 552976 | tf_op jit(solution)/shard_map/reduce_scatter | solution.py:224
  338.3 2.1 copy.92
  340.4 9.0 %all-to-all-start.5 = ((bf16[16,48,360]{2,1,0:T(8,128)(2,1)}), bf16[16,48,360]{2,1,0:T(8,128)(2,1)S(1)}, u32[]{:S(2)}, u32[]{:S(2)}) async-start(bf16[16,48,360]{2,1,0:T(8,128)(2,1)} %bitcast.39), calls=%async_computation.6 | async-start | bytes 1179648 | tf_op jit(solution)/shard_map/all_to_all | solution.py:228
  349.5 0.6 pad_maximum_fusion.2
  350.1 0.6 slice_bitcast_fusion.3
  350.8 16.0 %all-to-all-done.5 = bf16[16,48,360]{2,1,0:T(8,128)(2,1)S(1)} async-done(((bf16[16,48,360]{2,1,0:T(8,128)(2,1)}), bf16[16,48,360]{2,1,0:T(8,128)(2,1)S(1)}, u32[]{:S(2)}, u32[]{:S(2)}) %all-to-all-start.5) | async-done | bytes 552992 | tf_op jit(solution)/shard_map/all_to_all | solution.py:228
  366.8 1.9 gather_fusion
  368.7 0.2 reshape.395
  368.9 0.5 multiply_reduce_fusion
  369.5 0.1 copy.94
  369.6 0.7 fusion.72
  (90 shorter events, 1.5 us)
Async XLA Ops:
  7.2 34.3 %copy-start.7 = (f32[2880]{0:T(1024)S(1)}, f32[2880]{0:T(1024)}, u32[]{:S(2)}) copy-start(f32[2880]{0:T(1024)} %param.19) | copy-start | bytes 34564
  7.2 136.2 %all-gather.7.cloned.1.call-start = ((), (), s32[]{:S(2)}) async-start(), calls=%async_computation.9 | async-start | bytes 6406144 | tf_op jit(solution)/shard_map/all_gather | solution.py:86
  10.9 18.3 %all-to-all-start = ((bf16[8,360,128]{2,1,0:T(8,128)(2,1)}), bf16[8,360,128]{2,1,0:T(8,128)(2,1)S(1)}, u32[]{:S(2)}, u32[]{:S(2)}) async-start(bf16[8,360,128]{2,1,0:T(8,128)(2,1)} %broadcast_in_dim.91), calls=%async_computation | async-start | bytes 1474560 | tf_op jit(solution)/shard_map/all_to_all | solution.py:45
  30.2 45.7 %copy-start.10 = (s32[1,128,4]{1,2,0:T(4,128)S(1)}, s32[1,128,4]{1,2,0:T(4,128)}, u32[]{:S(2)}) copy-start(s32[1,128,4]{1,2,0:T(4,128)} %param.28) | copy-start | bytes 6148
  30.2 46.6 %copy-start.13 = (f32[8]{0:T(128)S(1)}, f32[8]{0:T(128)}, u32[]{:S(2)}) copy-start(f32[8]{0:T(128)} %param.24) | copy-start | bytes 100
  30.2 48.0 %copy-start.4 = (s32[1,2048]{1,0:T(1,128)S(1)}, s32[1,2048]{1,0:T(1,128)}, u32[]{:S(2)}) copy-start(s32[1,2048]{1,0:T(1,128)} %param.18) | copy-start | bytes 24580
  30.2 39.8 %all-to-all-start.1 = ((bf16[16,180,128]{2,1,0:T(8,128)(2,1)}), bf16[16,180,128]{2,1,0:T(8,128)(2,1)S(1)}, u32[]{:S(2)}, u32[]{:S(2)}) async-start(bf16[16,180,128]{2,1,0:T(8,128)(2,1)} %broadcast_in_dim.92), calls=%async_computation.1 | async-start | bytes 1507328 | tf_op jit(solution)/shard_map/all_to_all | solution.py:45
  71.8 23.3 %all-to-all-start.2 = ((bf16[16,128,128]{2,1,0:T(8,128)(2,1)}), bf16[16,128,128]{2,1,0:T(8,128)(2,1)S(1)}, u32[]{:S(2)}, u32[]{:S(2)}) async-start(bf16[16,128,128]{2,1,0:T(8,128)(2,1)} %broadcast_in_dim.93), calls=%async_computation.2 | async-start | bytes 1048576 | tf_op jit(solution)/shard_map/all_to_all | solution.py:45
  78.3 67.2 %copy-start.8 = (s32[16,5]{0,1:T(8,128)}, s32[16,5]{0,1:T(8,128)S(1)}, u32[]{:S(2)}) copy-start(s32[16,5]{0,1:T(8,128)S(1)} %reduce-window.9) | copy-start | bytes 964
  151.2 6.1 %copy-start.5 = (f32[128,32]{0,1:T(8,128)S(1)}, f32[128,32]{0,1:T(8,128)}, u32[]{:S(2)}) copy-start(f32[128,32]{0,1:T(8,128)} %get-tuple-element.475) | copy-start | bytes 49156
  151.2 6.1 %copy-start.6 = (f32[128,32]{0,1:T(8,128)S(1)}, f32[128,32]{0,1:T(8,128)}, u32[]{:S(2)}) copy-start(f32[128,32]{0,1:T(8,128)} %get-tuple-element.476) | copy-start | bytes 49156
  151.2 7.0 %copy-start.2 = (bf16[1,2048,64]{2,1,0:T(8,128)(2,1)S(1)}, bf16[1,2048,64]{2,1,0:T(8,128)(2,1)}, u32[]{:S(2)}) copy-start(bf16[1,2048,64]{2,1,0:T(8,128)(2,1)} %get-tuple-element.632) | copy-start | bytes 786436
  158.2 4.6 %copy-start = (bf16[1,2048,64]{2,1,0:T(8,128)(2,1)S(1)}, bf16[1,2048,64]{2,1,0:T(8,128)(2,1)}, u32[]{:S(2)}) copy-start(bf16[1,2048,64]{2,1,0:T(8,128)(2,1)} %get-tuple-element.635) | copy-start | bytes 786436
  169.6 8.2 %copy-start.11 = (s32[1,128,4]{1,2,0:T(4,128)S(1)}, s32[1,128,4]{1,2,0:T(4,128)}, u32[]{:S(2)}) copy-start(s32[1,128,4]{1,2,0:T(4,128)} %param.28) | copy-start | bytes 6148
  169.6 8.4 %slice-start = ((s32[16,5]{0,1:T(8,128)}), s32[16,4]{0,1:T(4,128)S(1)}, s32[]{:S(2)}) async-start(s32[16,5]{0,1:T(8,128)} %copy-done.8), calls=%async_computation.10 | async-start | bytes 4096 | tf_op jit(solution)/shard_map/slice.1
  169.6 8.4 %copy-start.9 = (s32[512]{0:T(512)S(1)}, s32[512]{0:T(512)}, u32[]{:S(2)}) copy-start(s32[512]{0:T(512)} %eq.112) | copy-start | bytes 6148
  169.7 20.4 %copy-start.3 = (bf16[1,128,360]{1,2,0:T(8,128)(2,1)S(1)}, bf16[1,128,360]{1,2,0:T(8,128)(2,1)}, u32[]{:S(2)}) copy-start(bf16[1,128,360]{1,2,0:T(8,128)(2,1)} %param.17) | copy-start | bytes 276484
  173.5 16.4 %all-to-all-start.3 = ((bf16[8,360,128]{2,1,0:T(8,128)(2,1)}), bf16[8,360,128]{2,1,0:T(8,128)(2,1)S(1)}, u32[]{:S(2)}, u32[]{:S(2)}) async-start(bf16[8,360,128]{2,1,0:T(8,128)(2,1)} %reshape.388), calls=%async_computation.3 | async-start | bytes 1474560 | tf_op jit(solution)/shard_map/all_to_all | solution.py:177
  177.5 89.1 %all-gather.5.cloned.1.call-start = ((), (), s32[]{:S(2)}) async-start(), calls=%async_computation.7 | async-start | bytes 4976640 | tf_op jit(solution)/shard_map/all_gather | solution.py:208
  214.1 55.9 %copy-start.14 = (f32[2880]{0:T(1024)S(1)}, f32[2880]{0:T(1024)}, u32[]{:S(2)}) copy-start(f32[2880]{0:T(1024)} %param.25) | copy-start | bytes 34564
  214.1 124.2 %reduce-scatter.2.cloned.1.call-start = ((), (), s32[]{:S(2)}) async-start(), calls=%async_computation.8 | async-start | bytes 4976640 | tf_op jit(solution)/shard_map/reduce_scatter | solution.py:224
  266.7 3.6 copy-start.1
  266.7 7.7 %slice-start.1 = ((s8[4239360]{0:T(1024)(128)(4,1)}), s8[4194304]{0:T(1024)(128)(4,1)S(1)}, s32[]{:S(2)}) async-start(s8[4239360]{0:T(1024)(128)(4,1)} %bitcast.218), calls=%async_computation.11 | async-start | bytes 8388608
  270.2 4.1 %slice-start.2 = ((s8[4239360]{0:T(1024)(128)(4,1)}), s8[45056]{0:T(1024)(128)(4,1)S(1)}, s32[]{:S(2)}) async-start(s8[4239360]{0:T(1024)(128)(4,1)} %bitcast.218), calls=%async_computation.12 | async-start | bytes 90112
  281.2 68.2 %copy-start.12 = (f32[1,128,4]{1,2,0:T(4,128)S(1)}, f32[1,128,4]{1,2,0:T(4,128)}, u32[]{:S(2)}) copy-start(f32[1,128,4]{1,2,0:T(4,128)} %param.29) | copy-start | bytes 6148
  340.4 26.3 %all-to-all-start.5 = ((bf16[16,48,360]{2,1,0:T(8,128)(2,1)}), bf16[16,48,360]{2,1,0:T(8,128)(2,1)S(1)}, u32[]{:S(2)}, u32[]{:S(2)}) async-start(bf16[16,48,360]{2,1,0:T(8,128)(2,1)} %bitcast.39), calls=%async_computation.6 | async-start | bytes 1179648 | tf_op jit(solution)/shard_map/all_to_all | solution.py:228
Sparse Core Ops, SparseCore 0:
  10.6 132.7 all-gather.6
  214.2 52.3 all-gather.4
  281.4 56.8 reduce-scatter.1

commit v11 on v10

--- a/solution.py
+++ b/solution.py
@@ -126,7 +126,7 @@
     row_pos = jnp.tile(token_positions, heads_per_group)
     row_seg = jnp.tile(seg_local, heads_per_group)
     sink_rows = jnp.repeat(sink_head_logit.reshape(kv_heads, heads_per_group), tok_count, axis=1)
-    key_block = math.gcd(seq_len, 1024)
+    key_block = math.gcd(seq_len, 2048)
     block_count = seq_len // key_block
     score_scale = HEAD_SIZE ** (-0.5)
 
@@ -226,9 +226,14 @@
     ).reshape(expert_count, capacity, -1)
     local_width = expert_out.shape[2]
     returned = lax.all_to_all(expert_out, "expert", split_axis=0, concat_axis=0, tiled=True)
-    picked = returned.reshape(expert_count * capacity, local_width)[target].reshape(
-        tok_count, top_count, local_width
-    )
+    slot_pick = (
+        target[:, None] == jnp.arange(expert_count * capacity, dtype=jnp.int32)[None, :]
+    ).astype(jnp.bfloat16)
+    picked = jnp.dot(
+        slot_pick,
+        returned.reshape(expert_count * capacity, local_width),
+        preferred_element_type=jnp.float32,
+    ).reshape(tok_count, top_count, local_width)
     moe_sum = jnp.sum(picked.astype(jnp.float32) * route_weights[0][..., None], axis=1)
     hidden = (first_out.astype(jnp.float32) + moe_sum).astype(jnp.bfloat16)
     return (hidden[None], key_rotary[None], value_fresh[None])

time: 378 us -> 369 us (0.976)
  matrix products: 31.7 us -> 23.9 us
    all_to_all x3, waiting for transfers between devices: 54.8 us -> 35.7 us  [gather_by_exchange(): lax.all_to_all(spread, axis_name, split_axis=0, concat_axis=0, tiled=True)]
    all_gather x1, waiting for transfers between devices: 47.1 us -> 65.4 us  [shards(): lax.all_gather(jnp.concatenate([w_query, w_out.T], axis=1), 'expert', axi...]
    dot_general x4 -> x1, matrix products: 9.85 us -> 2.93 us  [block_scores(): jnp.einsum('hrd,hkd->hrk', query_rows, key_part, preferred_element_type=j...]
  transfers between devices with their start and end apart: 8 -> 8, of which waited for: 8 -> 7; matrix products, arithmetic and copies ran while one was open for 5% -> 9% of each run, Pallas kernels for 0% -> 0%
where the time goes in v11:
time: 369 us; the launch traced here: 368 us
  waiting for transfers between devices  232 us (63%)
  starting transfers between devices  34.1 us (9%)
  local copies, waits for them, and re-layouts  28.1 us (8%)
  matrix products  23.9 us (6%)
  blocking collectives  22.2 us (6%)
  between operations  14.3 us (4%)
  other arithmetic  14.2 us (4%)
    all_gather x1, waiting for transfers between devices, shards(): lax.all_gather(jnp.concatenate([w_query, w_out.T], axis=1), 'expert', axi...  65.4 us
    reduce_scatter x1, waiting for transfers between devices, shards(): lax.psum_scatter(partials.astype(jnp.bfloat16), 'mp', scatter_dimension=0...  57.1 us
    all_gather x1, waiting for transfers between devices, shards(): lax.all_gather(arrived_rows, 'mp', axis=1, tiled=True)  48.8 us
    all_to_all x3, waiting for transfers between devices, gather_by_exchange(): lax.all_to_all(spread, axis_name, split_axis=0, concat_axis=0, tiled=True)  35.7 us
    all_to_all x1, blocking collectives, shards(): lax.all_to_all(outgoing, 'expert', split_axis=0, concat_axis=0, tiled=True)  22.2 us
    all_to_all x3, starting transfers between devices, gather_by_exchange(): lax.all_to_all(spread, axis_name, split_axis=0, concat_axis=0, tiled=True)  21 us
    all_to_all x1, waiting for transfers between devices, shards(): lax.all_to_all(expert_out, 'expert', split_axis=0, concat_axis=0, tiled=T...  15.2 us
    all_to_all x1, waiting for transfers between devices, shards(): lax.all_to_all(out_pieces, 'mp', split_axis=0, concat_axis=0, tiled=True)  9.47 us
  transfers between devices with their start and end apart: 8, of which 7 were waited for; matrix products, arithmetic and copies ran while one was open for 9% of the time, Pallas kernels for 0%

profile of v11, /device:TPU:1, one launch (start us, length us, event | category | flops | bytes accessed | tf_op | source)
XLA Modules:
  0.0 368.4 jit_solution(13217774373637550634)
XLA Ops:
  7.2 1.8 maximum_bitcast_fusion
  9.1 1.9 broadcast_in_dim.29
  10.9 5.9 %all-to-all-start = ((bf16[8,360,128]{2,1,0:T(8,128)(2,1)}), bf16[8,360,128]{2,1,0:T(8,128)(2,1)S(1)}, u32[]{:S(2)}, u32[]{:S(2)}) async-start(bf16[8,360,128]{2,1,0:T(8,128)(2,1)} %broadcast_in_dim.29), calls=%async_computation | async-start | bytes 1474560 | tf_op jit(solution)/shard_map/all_to_all | solution.py:45
  16.8 0.8 pad_maximum_fusion
  17.6 0.1 copy.39
  17.7 0.8 copy.43
  18.5 0.1 eq.114
  18.6 1.2 reduce-window.6
  19.8 9.5 %all-to-all-done = bf16[8,360,128]{2,1,0:T(8,128)(2,1)S(1)} async-done(((bf16[8,360,128]{2,1,0:T(8,128)(2,1)}), bf16[8,360,128]{2,1,0:T(8,128)(2,1)S(1)}, u32[]{:S(2)}, u32[]{:S(2)}) %all-to-all-start) | async-done | bytes 737312 | tf_op jit(solution)/shard_map/all_to_all | solution.py:45
  29.2 1.0 broadcast_in_dim.30
  30.2 10.6 %all-to-all-start.1 = ((bf16[16,180,128]{2,1,0:T(8,128)(2,1)}), bf16[16,180,128]{2,1,0:T(8,128)(2,1)S(1)}, u32[]{:S(2)}, u32[]{:S(2)}) async-start(bf16[16,180,128]{2,1,0:T(8,128)(2,1)} %broadcast_in_dim.30), calls=%async_computation.1 | async-start | bytes 1507328 | tf_op jit(solution)/shard_map/all_to_all | solution.py:45
  40.8 0.7 dynamic-slice_bitcast_fusion
  41.5 0.6 broadcast_bitcast_fusion
  42.1 0.4 fusion.18
  42.6 0.4 fusion.20
  43.0 26.2 %all-to-all-done.1 = bf16[16,180,128]{2,1,0:T(8,128)(2,1)S(1)} async-done(((bf16[16,180,128]{2,1,0:T(8,128)(2,1)}), bf16[16,180,128]{2,1,0:T(8,128)(2,1)S(1)}, u32[]{:S(2)}, u32[]{:S(2)}) %all-to-all-start.1) | async-done | bytes 737312 | tf_op jit(solution)/shard_map/all_to_all | solution.py:45
  69.2 0.1 reshape.415
  69.3 0.4 fusion.89
  69.8 0.1 fusion.77
  70.0 0.1 copy.40
  70.1 0.9 broadcast_in_dim.35
  71.0 4.5 %all-to-all-start.2 = ((bf16[16,128,128]{2,1,0:T(8,128)(2,1)}), bf16[16,128,128]{2,1,0:T(8,128)(2,1)S(1)}, u32[]{:S(2)}, u32[]{:S(2)}) async-start(bf16[16,128,128]{2,1,0:T(8,128)(2,1)} %broadcast_in_dim.35), calls=%async_computation.2 | async-start | bytes 1048576 | tf_op jit(solution)/shard_map/all_to_all | solution.py:45
  75.5 0.2 slice_reduce_fusion
  75.7 0.7 eq.110
  76.5 0.8 multiply_cosine_fusion.1
  77.2 1.0 reshape.439
  78.2 65.4 %all-gather.7.cloned.1.call-done = bf16[16,180,1024]{2,1,0:T(8,128)(2,1)} async-done(((bf16[1,180,1024]{2,1,0:T(8,128)(2,1)}), bf16[16,180,1024]{2,1,0:T(8,128)(2,1)}) %all-gather.7.cloned.1.call-update) | async-done | bytes 5898256 | tf_op jit(solution)/shard_map/all_gather | solution.py:86
  143.6 1.9 slice-done.2
  145.5 5.7 %copy.59 = bf16[16,180,512]{1,0,2:T(8,128)(2,1)} copy(bf16[16,180,512]{2,1,0:T(8,128)(2,1)S(1)} %slice-done.2) | data formatting | bytes 5898240
  151.2 6.0 %fusion.50 = f32[128,8,64]{0,2,1:T(8,128)S(1)} fusion(bf16[128,16,180,1]{0,2,1,3:T(8,128)(2,1)} %reshape.439, bf16[8,64,16,180]{3,2,1,0:T(8,128)(2,1)} %bitcast.149), kind=kOutput, calls=%fused_computation.42 | convolution fusion | flops 377487360 | bytes 3948544 | tf_op jit(solution)/shard_map/tef,efc->tc/dot_general | solution.py:90
  157.3 0.1 copy.38
  157.5 2.9 fusion.4
  160.5 3.5 convert_reduce_fusion
  164.0 0.1 fusion.81
  164.1 1.5 fusion.54
  165.7 1.0 fusion.21
  166.7 1.0 reshape.420
  167.7 3.8 %all-to-all-start.3 = ((bf16[8,360,128]{2,1,0:T(8,128)(2,1)}), bf16[8,360,128]{2,1,0:T(8,128)(2,1)S(1)}, u32[]{:S(2)}, u32[]{:S(2)}) async-start(bf16[8,360,128]{2,1,0:T(8,128)(2,1)} %reshape.420), calls=%async_computation.3 | async-start | bytes 1474560 | tf_op jit(solution)/shard_map/all_to_all | solution.py:177
  171.5 0.3 all-gather.5.cloned.1.call-start
  171.8 0.1 mul.212
  171.9 0.1 fusion.70
  172.0 2.4 scatter_custom_fusion
  174.5 9.5 %all-to-all-done.3 = bf16[8,360,128]{2,1,0:T(8,128)(2,1)S(1)} async-done(((bf16[8,360,128]{2,1,0:T(8,128)(2,1)}), bf16[8,360,128]{2,1,0:T(8,128)(2,1)S(1)}, u32[]{:S(2)}, u32[]{:S(2)}) %all-to-all-start.3) | async-done | bytes 737312 | tf_op jit(solution)/shard_map/all_to_all | solution.py:177
  183.9 0.1 convert_reduce_fusion.1
  184.1 0.4 convolution_convert_fusion
  184.5 0.3 copy.48
  184.8 22.2 %all_to_all.30 = bf16[16,48,360]{2,1,0:T(8,128)(2,1)S(1)} all-to-all(bf16[16,48,360]{2,1,0:T(8,128)(2,1)S(1)} %bitcast.150), channel_id=1, replica_groups=mesh['expert'=16,'mp'=8,'batch'=2] {'expert'}, dimensions={0} | all-to-all | bytes 1105920 | tf_op jit(solution)/shard_map/all_to_all | solution.py:206
  207.0 1.1 copy.49
  208.2 3.4 copy.57
  211.5 48.8 %all-gather.5.cloned.1.call-done = bf16[768,2880]{0,1:T(8,128)(2,1)} async-done(((bf16[768,360]{0,1:T(8,128)(2,1)}), bf16[768,2880]{0,1:T(8,128)(2,1)}) %all-gather.5.cloned.1.call-update) | async-done | bytes 4423696 | tf_op jit(solution)/shard_map/all_gather | solution.py:208
  260.4 3.3 fusion
  263.8 0.2 copy-done
  264.0 4.1 %fusion.24 = f32[768,360]{0,1:T(8,128)S(1)} fusion(bf16[1,2,2880,360]{2,3,1,0:T(8,128)(2,1)} %param.22, bf16[768,2880]{0,1:T(8,128)(2,1)S(1)} %copy-done, f32[2880]{0:T(1024)S(1)} %copy-done.16, f32[768]{0:T(1024)S(1)} %add_rsqrt_fusion), kind=kOutput, calls=%fused_computation.33 | convolution fusion | flops 1601648640 | bytes 7663872 | tf_op jit(solution)/shard_map/dot_general | solution.py:210
  268.1 2.4 fusion.39
  270.5 4.5 %convert_bitcast_fusion = bf16[8,768,360]{1,2,0:T(8,128)(2,1)} fusion(bf16[360,8,360]{0,2,1:T(8,128)(2,1)S(1)} %bitcast.152, bf16[768,360]{0,1:T(8,128)(2,1)S(1)} %fusion.39), kind=kOutput, calls=%fused_computation.12 | convolution fusion | flops 1594736640 | bytes 7050240 | tf_op jit(solution)/shard_map/rh,hjf->jrf/dot_general | solution.py:218
  275.0 57.1 %reduce-scatter.2.cloned.1.call-done = bf16[1,768,360]{1,2,0:T(8,128)(2,1)} async-done(((bf16[8,768,360]{1,2,0:T(8,128)(2,1)}), bf16[1,768,360]{1,2,0:T(8,128)(2,1)}) %reduce-scatter.2.cloned.1.call-update) | async-done | bytes 552976 | tf_op jit(solution)/shard_map/reduce_scatter | solution.py:224
  332.1 2.1 copy.51
  334.2 9.0 %all-to-all-start.5 = ((bf16[16,48,360]{2,1,0:T(8,128)(2,1)}), bf16[16,48,360]{2,1,0:T(8,128)(2,1)S(1)}, u32[]{:S(2)}, u32[]{:S(2)}) async-start(bf16[16,48,360]{2,1,0:T(8,128)(2,1)} %bitcast.40), calls=%async_computation.6 | async-start | bytes 1179648 | tf_op jit(solution)/shard_map/all_to_all | solution.py:228
  343.2 0.1 reduce_sum.63
  343.4 0.6 pad_maximum_fusion.2
  344.0 1.4 slice_bitcast_fusion.1
  345.4 15.2 %all-to-all-done.5 = bf16[16,48,360]{2,1,0:T(8,128)(2,1)S(1)} async-done(((bf16[16,48,360]{2,1,0:T(8,128)(2,1)}), bf16[16,48,360]{2,1,0:T(8,128)(2,1)S(1)}, u32[]{:S(2)}, u32[]{:S(2)}) %all-to-all-start.5) | async-done | bytes 552992 | tf_op jit(solution)/shard_map/all_to_all | solution.py:228
  360.5 0.6 fusion.47
  361.2 0.7 fusion.65
  (75 shorter events, 0.6 us)
Async XLA Ops:
  7.2 35.4 %copy-start.11 = (f32[2880]{0:T(1024)S(1)}, f32[2880]{0:T(1024)}, u32[]{:S(2)}) copy-start(f32[2880]{0:T(1024)} %param.15) | copy-start | bytes 34564
  7.2 136.4 %all-gather.7.cloned.1.call-start = ((), (), s32[]{:S(2)}) async-start(), calls=%async_computation.9 | async-start | bytes 6406144 | tf_op jit(solution)/shard_map/all_gather | solution.py:86
  10.9 18.3 %all-to-all-start = ((bf16[8,360,128]{2,1,0:T(8,128)(2,1)}), bf16[8,360,128]{2,1,0:T(8,128)(2,1)S(1)}, u32[]{:S(2)}, u32[]{:S(2)}) async-start(bf16[8,360,128]{2,1,0:T(8,128)(2,1)} %broadcast_in_dim.29), calls=%async_computation | async-start | bytes 1474560 | tf_op jit(solution)/shard_map/all_to_all | solution.py:45
  18.5 57.2 %copy-start.1 = (s32[1,128,4]{2,1,0:T(8,128)}, s32[1,128,4]{2,1,0:T(8,128)S(1)}, u32[]{:S(2)}) copy-start(s32[1,128,4]{2,1,0:T(8,128)S(1)} %copy.43) | copy-start | bytes 6148
  19.7 55.7 %copy-start.4 = (s32[16,4,128]{2,0,1:T(8,128)}, s32[16,4,128]{2,0,1:T(8,128)S(1)}, u32[]{:S(2)}) copy-start(s32[16,4,128]{2,0,1:T(8,128)S(1)} %reduce-window.6) | copy-start | bytes 98308
  30.2 39.0 %all-to-all-start.1 = ((bf16[16,180,128]{2,1,0:T(8,128)(2,1)}), bf16[16,180,128]{2,1,0:T(8,128)(2,1)S(1)}, u32[]{:S(2)}, u32[]{:S(2)}) async-start(bf16[16,180,128]{2,1,0:T(8,128)(2,1)} %broadcast_in_dim.30), calls=%async_computation.1 | async-start | bytes 1507328 | tf_op jit(solution)/shard_map/all_to_all | solution.py:45
  69.8 8.5 %copy-start.6 = (f32[128,128]{0,1:T(8,128)}, f32[128,128]{0,1:T(8,128)S(1)}, u32[]{:S(2)}) copy-start(f32[128,128]{0,1:T(8,128)S(1)} %fusion.89) | copy-start | bytes 196612
  71.0 86.4 %all-to-all-start.2 = ((bf16[16,128,128]{2,1,0:T(8,128)(2,1)}), bf16[16,128,128]{2,1,0:T(8,128)(2,1)S(1)}, u32[]{:S(2)}, u32[]{:S(2)}) async-start(bf16[16,128,128]{2,1,0:T(8,128)(2,1)} %broadcast_in_dim.35), calls=%async_computation.2 | async-start | bytes 1048576 | tf_op jit(solution)/shard_map/all_to_all | solution.py:45
  76.5 1.8 copy-start.12
  143.6 1.9 slice-start.2
  151.2 6.1 %copy-start.7 = (f32[128,32]{0,1:T(8,128)S(1)}, f32[128,32]{0,1:T(8,128)}, u32[]{:S(2)}) copy-start(f32[128,32]{0,1:T(8,128)} %get-tuple-element.55) | copy-start | bytes 49156
  151.2 6.1 %copy-start.8 = (f32[128,32]{0,1:T(8,128)S(1)}, f32[128,32]{0,1:T(8,128)}, u32[]{:S(2)}) copy-start(f32[128,32]{0,1:T(8,128)} %get-tuple-element.56) | copy-start | bytes 49156
  151.2 6.3 %copy-start.9 = (s32[1024]{0:T(1024)S(1)}, s32[1024]{0:T(1024)}, u32[]{:S(2)}) copy-start(s32[1024]{0:T(1024)} %get-tuple-element.59) | copy-start | bytes 12292
  151.2 6.3 %copy-start.10 = (s32[1024]{0:T(1024)S(1)}, s32[1024]{0:T(1024)}, u32[]{:S(2)}) copy-start(s32[1024]{0:T(1024)} %get-tuple-element.60) | copy-start | bytes 12292
  151.2 6.3 %copy-start.14 = (s32[1,2048]{1,0:T(1,128)S(1)}, s32[1,2048]{1,0:T(1,128)}, u32[]{:S(2)}) copy-start(s32[1,2048]{1,0:T(1,128)} %param.14) | copy-start | bytes 24580
  157.4 2.9 copy-start.15
  160.5 5.2 %slice-start = ((s8[6029312]{0:T(1024)(128)(4,1)}), s8[4194304]{0:T(1024)(128)(4,1)S(1)}, s32[]{:S(2)}) async-start(s8[6029312]{0:T(1024)(128)(4,1)} %bitcast.146), calls=%async_computation.10 | async-start | bytes 8388608
  160.5 5.2 %slice-start.1 = ((s8[6029312]{0:T(1024)(128)(4,1)}), s8[1835008]{0:T(1024)(128)(4,1)S(1)}, s32[]{:S(2)}) async-start(s8[6029312]{0:T(1024)(128)(4,1)} %bitcast.146), calls=%async_computation.11 | async-start | bytes 3670016
  165.6 6.2 %copy-start.2 = (s32[1,128,4]{2,1,0:T(8,128)S(1)}, s32[1,128,4]{2,1,0:T(8,128)}, u32[]{:S(2)}) copy-start(s32[1,128,4]{2,1,0:T(8,128)} %copy-done.1) | copy-start | bytes 6148
  165.6 6.3 %copy-start.5 = (s32[16,4,128]{2,0,1:T(8,128)S(1)}, s32[16,4,128]{2,0,1:T(8,128)}, u32[]{:S(2)}) copy-start(s32[16,4,128]{2,0,1:T(8,128)} %copy-done.4) | copy-start | bytes 98308
  165.6 6.3 %slice-start.3 = ((s32[16,5]{0,1:T(8,128)}), s32[16,4]{0,1:T(4,128)S(1)}, s32[]{:S(2)}) async-start(s32[16,5]{0,1:T(8,128)} %copy-done.12), calls=%async_computation.13 | async-start | bytes 4096 | tf_op jit(solution)/shard_map/slice.1
  165.6 6.3 %copy-start.13 = (s32[512]{0:T(512)S(1)}, s32[512]{0:T(512)}, u32[]{:S(2)}) copy-start(s32[512]{0:T(512)} %eq.110) | copy-start | bytes 6148
  165.7 18.4 %copy-start.3 = (bf16[1,128,360]{1,2,0:T(8,128)(2,1)S(1)}, bf16[1,128,360]{1,2,0:T(8,128)(2,1)}, u32[]{:S(2)}) copy-start(bf16[1,128,360]{1,2,0:T(8,128)(2,1)} %param.13) | copy-start | bytes 276484
  167.7 16.3 %all-to-all-start.3 = ((bf16[8,360,128]{2,1,0:T(8,128)(2,1)}), bf16[8,360,128]{2,1,0:T(8,128)(2,1)S(1)}, u32[]{:S(2)}, u32[]{:S(2)}) async-start(bf16[8,360,128]{2,1,0:T(8,128)(2,1)} %reshape.420), calls=%async_computation.3 | async-start | bytes 1474560 | tf_op jit(solution)/shard_map/all_to_all | solution.py:177
  171.5 88.9 %all-gather.5.cloned.1.call-start = ((), (), s32[]{:S(2)}) async-start(), calls=%async_computation.7 | async-start | bytes 4976640 | tf_op jit(solution)/shard_map/all_gather | solution.py:208
  208.1 55.6 %copy-start.16 = (f32[2880]{0:T(1024)S(1)}, f32[2880]{0:T(1024)}, u32[]{:S(2)}) copy-start(f32[2880]{0:T(1024)} %param.21) | copy-start | bytes 34564
  208.1 123.9 %reduce-scatter.2.cloned.1.call-start = ((), (), s32[]{:S(2)}) async-start(), calls=%async_computation.8 | async-start | bytes 4976640 | tf_op jit(solution)/shard_map/reduce_scatter | solution.py:224
  260.4 3.6 copy-start
  260.4 7.7 %slice-start.4 = ((s8[4239360]{0:T(1024)(128)(4,1)}), s8[4194304]{0:T(1024)(128)(4,1)S(1)}, s32[]{:S(2)}) async-start(s8[4239360]{0:T(1024)(128)(4,1)} %bitcast.169), calls=%async_computation.14 | async-start | bytes 8388608
  264.0 4.1 %slice-start.5 = ((s8[4239360]{0:T(1024)(128)(4,1)}), s8[45056]{0:T(1024)(128)(4,1)S(1)}, s32[]{:S(2)}) async-start(s8[4239360]{0:T(1024)(128)(4,1)} %bitcast.169), calls=%async_computation.15 | async-start | bytes 90112
  275.0 85.6 %copy-start.17 = (f32[1,128,4]{1,2,0:T(4,128)S(1)}, f32[1,128,4]{1,2,0:T(4,128)}, u32[]{:S(2)}) copy-start(f32[1,128,4]{1,2,0:T(4,128)} %param.25) | copy-start | bytes 6148
  334.2 26.4 %all-to-all-start.5 = ((bf16[16,48,360]{2,1,0:T(8,128)(2,1)}), bf16[16,48,360]{2,1,0:T(8,128)(2,1)S(1)}, u32[]{:S(2)}, u32[]{:S(2)}) async-start(bf16[16,48,360]{2,1,0:T(8,128)(2,1)} %bitcast.40), calls=%async_computation.6 | async-start | bytes 1179648 | tf_op jit(solution)/shard_map/all_to_all | solution.py:228
Sparse Core Ops, SparseCore 0:
  10.6 132.9 all-gather.6
  208.2 52.1 all-gather.4
  275.1 56.8 reduce-scatter.1

commit v12 on v9

--- a/solution.py
+++ b/solution.py
@@ -133,7 +133,7 @@
     row_pos = jnp.tile(token_positions, heads_per_group)
     row_seg = jnp.tile(seg_local, heads_per_group)
     sink_rows = jnp.repeat(sink_head_logit.reshape(kv_heads, heads_per_group), tok_count, axis=1)
-    key_block = math.gcd(seq_len, 512)
+    key_block = math.gcd(seq_len, 2048)
     block_count = seq_len // key_block
     score_scale = HEAD_SIZE ** (-0.5)
 
@@ -202,7 +202,14 @@
     padded = jnp.concatenate(
         [first_out, jnp.zeros((1, first_out.shape[1]), jnp.bfloat16)], axis=0
     )
-    outgoing = padded[source_row].reshape(expert_count, capacity, padded.shape[1])
+    pick = (source_row[:, None] == jnp.arange(tok_count + 1, dtype=jnp.int32)[None, :]).astype(
+        jnp.bfloat16
+    )
+    outgoing = (
+        jnp.dot(pick, padded, preferred_element_type=jnp.float32)
+        .astype(jnp.bfloat16)
+        .reshape(expert_count, capacity, padded.shape[1])
+    )
     arrived = lax.all_to_all(outgoing, "expert", split_axis=0, concat_axis=0, tiled=True)
     arrived_rows = arrived.reshape(expert_count * capacity, arrived.shape[2])
     inputs = rms_norm(lax.all_gather(arrived_rows, "mp", axis=1, tiled=True), moe_gain)
@@ -226,9 +233,14 @@
     ).reshape(expert_count, capacity, -1)
     local_width = expert_out.shape[2]
     returned = lax.all_to_all(expert_out, "expert", split_axis=0, concat_axis=0, tiled=True)
-    picked = returned.reshape(expert_count * capacity, local_width)[target].reshape(
-        tok_count, top_count, local_width
-    )
+    slot_pick = (
+        target[:, None] == jnp.arange(expert_count * capacity, dtype=jnp.int32)[None, :]
+    ).astype(jnp.bfloat16)
+    picked = jnp.dot(
+        slot_pick,
+        returned.reshape(expert_count * capacity, local_width),
+        preferred_element_type=jnp.float32,
+    ).reshape(tok_count, top_count, local_width)
     moe_sum = jnp.sum(picked.astype(jnp.float32) * route_weights[0][..., None], axis=1)
     hidden = (first_out.astype(jnp.float32) + moe_sum).astype(jnp.bfloat16)
     return (hidden[None], key_rotary[None], value_fresh[None])

time: 382 us -> 367 us (0.961)
  matrix products: 34.3 us -> 20.6 us
  other arithmetic: 9.24 us -> 15 us
  local copies, waits for them, and re-layouts: 32 us -> 27.6 us
    all_to_all x3, waiting for transfers between devices: 54.6 us -> 35 us  [gather_by_exchange(): lax.all_to_all(spread, axis_name, split_axis=0, concat_axis=0, tiled=True)]
    all_gather x1, waiting for transfers between devices: 48.2 us -> 66.1 us  [shards(): lax.all_gather(jnp.pad(jnp.concatenate([w_query, w_out.T], axis=1), ((0,...]
    dot_general x8 -> x1, matrix products: 13 us -> 3.67 us  [block_scores(): jnp.einsum('hrd,hkd->hrk', query_rows, key_part, preferred_element_type=j...]
    gather x2 -> x0, local copies, waits for them, and re-layouts: 4.56 us -> none  [the longest x1 2.63 us: shards(): padded[source_row].reshape(expert_count, capacity, padded.shape[1])]
  transfers between devices with their start and end apart: 8 -> 8, of which waited for: 8 -> 7; matrix products, arithmetic and copies ran while one was open for 5% -> 8% of each run, Pallas kernels for 0% -> 0%
where the time goes in v12:
time: 367 us; the launch traced here: 366 us
  waiting for transfers between devices  232 us (63%)
  starting transfers between devices  34 us (9%)
  local copies, waits for them, and re-layouts  27.6 us (8%)
  blocking collectives  22.2 us (6%)
  matrix products  20.6 us (6%)
  other arithmetic  15 us (4%)
  between operations  14.3 us (4%)
    all_gather x1, waiting for transfers between devices, shards(): lax.all_gather(jnp.pad(jnp.concatenate([w_query, w_out.T], axis=1), ((0,...  66.1 us
    reduce_scatter x1, waiting for transfers between devices, shards(): lax.psum_scatter(partials.astype(jnp.bfloat16), 'mp', scatter_dimension=0...  57.1 us
    all_gather x1, waiting for transfers between devices, shards(): lax.all_gather(arrived_rows, 'mp', axis=1, tiled=True)  48.8 us
    all_to_all x3, waiting for transfers between devices, gather_by_exchange(): lax.all_to_all(spread, axis_name, split_axis=0, concat_axis=0, tiled=True)  35 us
    all_to_all x1, blocking collectives, shards(): lax.all_to_all(outgoing, 'expert', split_axis=0, concat_axis=0, tiled=True)  22.2 us
    all_to_all x3, starting transfers between devices, gather_by_exchange(): lax.all_to_all(spread, axis_name, split_axis=0, concat_axis=0, tiled=True)  21 us
    all_to_all x1, waiting for transfers between devices, shards(): lax.all_to_all(expert_out, 'expert', split_axis=0, concat_axis=0, tiled=T...  15.2 us
    all_to_all x1, waiting for transfers between devices, shards(): lax.all_to_all(out_pieces, 'mp', split_axis=0, concat_axis=0, tiled=True)  9.69 us
  transfers between devices with their start and end apart: 8, of which 7 were waited for; matrix products, arithmetic and copies ran while one was open for 8% of the time, Pallas kernels for 0%

profile of v12, /device:TPU:1, one launch (start us, length us, event | category | flops | bytes accessed | tf_op | source)
XLA Modules:
  0.0 365.6 jit_solution(4205207677783432135)
XLA Ops:
  7.2 1.8 fusion.55
  9.1 1.9 broadcast_in_dim.29
  10.9 5.9 %all-to-all-start = ((bf16[8,360,128]{2,1,0:T(8,128)(2,1)}), bf16[8,360,128]{2,1,0:T(8,128)(2,1)S(1)}, u32[]{:S(2)}, u32[]{:S(2)}) async-start(bf16[8,360,128]{2,1,0:T(8,128)(2,1)} %broadcast_in_dim.29), calls=%async_computation | async-start | bytes 1474560 | tf_op jit(solution)/shard_map/all_to_all | solution.py:45
  16.8 0.8 copy.45
  17.6 0.1 eq.114
  17.7 0.7 eq.110
  18.4 0.8 pad_maximum_fusion
  19.1 0.1 copy.41
  19.3 1.2 reduce-window.6
  20.5 8.8 %all-to-all-done = bf16[8,360,128]{2,1,0:T(8,128)(2,1)S(1)} async-done(((bf16[8,360,128]{2,1,0:T(8,128)(2,1)}), bf16[8,360,128]{2,1,0:T(8,128)(2,1)S(1)}, u32[]{:S(2)}, u32[]{:S(2)}) %all-to-all-start) | async-done | bytes 737312 | tf_op jit(solution)/shard_map/all_to_all | solution.py:45
  29.2 1.0 broadcast_in_dim.30
  30.2 10.6 %all-to-all-start.1 = ((bf16[16,180,128]{2,1,0:T(8,128)(2,1)}), bf16[16,180,128]{2,1,0:T(8,128)(2,1)S(1)}, u32[]{:S(2)}, u32[]{:S(2)}) async-start(bf16[16,180,128]{2,1,0:T(8,128)(2,1)} %broadcast_in_dim.30), calls=%async_computation.1 | async-start | bytes 1507328 | tf_op jit(solution)/shard_map/all_to_all | solution.py:45
  40.8 0.7 dynamic-slice_bitcast_fusion
  41.5 0.6 broadcast_bitcast_fusion
  42.1 0.4 fusion.16
  42.6 0.4 fusion.18
  43.0 26.2 %all-to-all-done.1 = bf16[16,180,128]{2,1,0:T(8,128)(2,1)S(1)} async-done(((bf16[16,180,128]{2,1,0:T(8,128)(2,1)}), bf16[16,180,128]{2,1,0:T(8,128)(2,1)S(1)}, u32[]{:S(2)}, u32[]{:S(2)}) %all-to-all-start.1) | async-done | bytes 737312 | tf_op jit(solution)/shard_map/all_to_all | solution.py:45
  69.2 0.1 reshape.423
  69.3 0.4 fusion.85
  69.8 0.1 fusion.72
  70.0 0.1 copy.42
  70.1 0.9 broadcast_in_dim.35
  71.0 4.5 %all-to-all-start.2 = ((bf16[16,128,128]{2,1,0:T(8,128)(2,1)}), bf16[16,128,128]{2,1,0:T(8,128)(2,1)S(1)}, u32[]{:S(2)}, u32[]{:S(2)}) async-start(bf16[16,128,128]{2,1,0:T(8,128)(2,1)} %broadcast_in_dim.35), calls=%async_computation.2 | async-start | bytes 1048576 | tf_op jit(solution)/shard_map/all_to_all | solution.py:45
  75.5 0.2 slice_reduce_fusion
  75.7 0.8 multiply_cosine_fusion.1
  76.5 0.1 reshape.419
  76.6 0.9 pad.10
  77.6 66.1 %all-gather.6.cloned.1.call-done = bf16[2944,1024]{1,0:T(8,128)(2,1)} async-done(((bf16[184,1024]{1,0:T(8,128)(2,1)}), bf16[2944,1024]{1,0:T(8,128)(2,1)}) %all-gather.6.cloned.1.call-update) | async-done | bytes 6029328 | tf_op jit(solution)/shard_map/all_gather | solution.py:88
  143.6 3.7 %slice.65 = bf16[16,184,512]{2,1,0:T(8,128)(2,1)} slice(bf16[16,184,1024]{2,1,0:T(8,128)(2,1)} %bitcast.156), slice={[0:16], [0:184], [0:512]} | slice | bytes 6029312 | tf_op jit(solution)/shard_map/slice | solution.py:95
  147.4 3.3 copy.38
  150.7 2.1 fusion.84
  152.8 0.8 fusion.61
  153.6 0.1 copy.40
  153.8 3.7 %fusion.4 = (f32[1024]{0:T(1024)S(1)}, f32[1024,2048]{1,0:T(8,128)S(1)}) fusion(s32[2048]{0:T(1024)} %bitcast.172, s32[1024]{0:T(1024)} %get-tuple-element.60, s32[1024]{0:T(1024)} %get-tuple-element.59, bf16[2048,128]{1,0:T(8,128)(2,1)S(1)} %bitcast.154, bf16[8,8,8,128]{3,2,1,0:T(8,128)(2,1)S(1)} %bitcast.165), kind=kOutput, calls=%fused_computation.11 | convolution fusion | flops 281017344 | bytes 9064448 | tf_op jit(solution)/shard_map/while/body/eval_jaxpr/hrd,hkd->hrk/dot_general | solution.py:144
  157.5 3.5 convert_reduce_fusion
  161.2 1.5 fusion.46
  162.8 1.0 fusion.5
  163.7 1.0 reshape.428
  164.8 3.9 %all-to-all-start.3 = ((bf16[8,360,128]{2,1,0:T(8,128)(2,1)}), bf16[8,360,128]{2,1,0:T(8,128)(2,1)S(1)}, u32[]{:S(2)}, u32[]{:S(2)}) async-start(bf16[8,360,128]{2,1,0:T(8,128)(2,1)} %reshape.428), calls=%async_computation.3 | async-start | bytes 1474560 | tf_op jit(solution)/shard_map/all_to_all | solution.py:184
  168.8 0.1 mul.212
  168.9 0.1 fusion.65
  169.0 2.4 scatter_custom_fusion
  171.5 9.7 %all-to-all-done.3 = bf16[8,360,128]{2,1,0:T(8,128)(2,1)S(1)} async-done(((bf16[8,360,128]{2,1,0:T(8,128)(2,1)}), bf16[8,360,128]{2,1,0:T(8,128)(2,1)S(1)}, u32[]{:S(2)}, u32[]{:S(2)}) %all-to-all-start.3) | async-done | bytes 737312 | tf_op jit(solution)/shard_map/all_to_all | solution.py:184
  181.2 0.1 convert_reduce_fusion.1
  181.3 0.4 convolution_convert_fusion
  181.8 0.3 copy.50
  182.1 22.2 %all_to_all.30 = bf16[16,48,360]{2,1,0:T(8,128)(2,1)S(1)} all-to-all(bf16[16,48,360]{2,1,0:T(8,128)(2,1)S(1)} %bitcast.151), channel_id=1, replica_groups=mesh['expert'=16,'mp'=8,'batch'=2] {'expert'}, dimensions={0} | all-to-all | bytes 1105920 | tf_op jit(solution)/shard_map/all_to_all | solution.py:213
  204.3 1.1 copy.51
  205.4 3.4 copy.60
  208.8 48.8 %all-gather.4.cloned.1.call-done = bf16[768,2880]{0,1:T(8,128)(2,1)} async-done(((bf16[768,360]{0,1:T(8,128)(2,1)}), bf16[768,2880]{0,1:T(8,128)(2,1)}) %all-gather.4.cloned.1.call-update) | async-done | bytes 4423696 | tf_op jit(solution)/shard_map/all_gather | solution.py:215
  257.6 3.3 fusion
  261.0 0.2 copy-done
  261.2 4.1 %fusion.19 = f32[768,360]{0,1:T(8,128)S(1)} fusion(bf16[1,2,2880,360]{2,3,1,0:T(8,128)(2,1)} %param.22, bf16[768,2880]{0,1:T(8,128)(2,1)S(1)} %copy-done, f32[2880]{0:T(1024)S(1)} %copy-done.14, f32[768]{0:T(1024)S(1)} %add_rsqrt_fusion), kind=kOutput, calls=%fused_computation.31 | convolution fusion | flops 1601648640 | bytes 7663872 | tf_op jit(solution)/shard_map/dot_general | solution.py:217
  265.3 2.4 fusion.34
  267.7 4.5 %convert_bitcast_fusion = bf16[8,768,360]{1,2,0:T(8,128)(2,1)} fusion(bf16[360,8,360]{0,2,1:T(8,128)(2,1)S(1)} %bitcast.153, bf16[768,360]{0,1:T(8,128)(2,1)S(1)} %fusion.34), kind=kOutput, calls=%fused_computation.12 | convolution fusion | flops 1594736640 | bytes 7050240 | tf_op jit(solution)/shard_map/rh,hjf->jrf/dot_general | solution.py:225
  272.2 57.1 %reduce-scatter.2.cloned.1.call-done = bf16[1,768,360]{1,2,0:T(8,128)(2,1)} async-done(((bf16[8,768,360]{1,2,0:T(8,128)(2,1)}), bf16[1,768,360]{1,2,0:T(8,128)(2,1)}) %reduce-scatter.2.cloned.1.call-update) | async-done | bytes 552976 | tf_op jit(solution)/shard_map/reduce_scatter | solution.py:231
  329.3 2.1 copy.53
  331.4 9.0 %all-to-all-start.5 = ((bf16[16,48,360]{2,1,0:T(8,128)(2,1)}), bf16[16,48,360]{2,1,0:T(8,128)(2,1)S(1)}, u32[]{:S(2)}, u32[]{:S(2)}) async-start(bf16[16,48,360]{2,1,0:T(8,128)(2,1)} %bitcast.40), calls=%async_computation.6 | async-start | bytes 1179648 | tf_op jit(solution)/shard_map/all_to_all | solution.py:235
  340.4 0.1 reduce_sum.63
  340.6 0.6 pad_maximum_fusion.2
  341.2 1.4 slice_bitcast_fusion.1
  342.6 15.2 %all-to-all-done.5 = bf16[16,48,360]{2,1,0:T(8,128)(2,1)S(1)} async-done(((bf16[16,48,360]{2,1,0:T(8,128)(2,1)}), bf16[16,48,360]{2,1,0:T(8,128)(2,1)S(1)}, u32[]{:S(2)}, u32[]{:S(2)}) %all-to-all-start.5) | async-done | bytes 552992 | tf_op jit(solution)/shard_map/all_to_all | solution.py:235
  357.8 0.6 fusion.42
  358.4 0.7 fusion.60
  (71 shorter events, 0.7 us)
Async XLA Ops:
  7.2 35.4 %copy-start.9 = (f32[2880]{0:T(1024)S(1)}, f32[2880]{0:T(1024)}, u32[]{:S(2)}) copy-start(f32[2880]{0:T(1024)} %param.15) | copy-start | bytes 34564
  7.2 136.5 %all-gather.6.cloned.1.call-start = ((), (), s32[]{:S(2)}) async-start(), calls=%async_computation.9 | async-start | bytes 6406144 | tf_op jit(solution)/shard_map/all_gather | solution.py:88
  10.9 18.3 %all-to-all-start = ((bf16[8,360,128]{2,1,0:T(8,128)(2,1)}), bf16[8,360,128]{2,1,0:T(8,128)(2,1)S(1)}, u32[]{:S(2)}, u32[]{:S(2)}) async-start(bf16[8,360,128]{2,1,0:T(8,128)(2,1)} %broadcast_in_dim.29), calls=%async_computation | async-start | bytes 1474560 | tf_op jit(solution)/shard_map/all_to_all | solution.py:45
  17.6 25.0 %copy-start.1 = (s32[1,128,4]{2,1,0:T(8,128)}, s32[1,128,4]{2,1,0:T(8,128)S(1)}, u32[]{:S(2)}) copy-start(s32[1,128,4]{2,1,0:T(8,128)S(1)} %copy.45) | copy-start | bytes 6148
  20.4 55.0 %copy-start.4 = (s32[16,4,128]{2,0,1:T(8,128)}, s32[16,4,128]{2,0,1:T(8,128)S(1)}, u32[]{:S(2)}) copy-start(s32[16,4,128]{2,0,1:T(8,128)S(1)} %reduce-window.6) | copy-start | bytes 98308
  30.2 39.0 %all-to-all-start.1 = ((bf16[16,180,128]{2,1,0:T(8,128)(2,1)}), bf16[16,180,128]{2,1,0:T(8,128)(2,1)S(1)}, u32[]{:S(2)}, u32[]{:S(2)}) async-start(bf16[16,180,128]{2,1,0:T(8,128)(2,1)} %broadcast_in_dim.30), calls=%async_computation.1 | async-start | bytes 1507328 | tf_op jit(solution)/shard_map/all_to_all | solution.py:45
  69.8 6.7 %copy-start.6 = (f32[128,128]{0,1:T(8,128)}, f32[128,128]{0,1:T(8,128)S(1)}, u32[]{:S(2)}) copy-start(f32[128,128]{0,1:T(8,128)S(1)} %fusion.85) | copy-start | bytes 196612
  71.0 82.7 %all-to-all-start.2 = ((bf16[16,128,128]{2,1,0:T(8,128)(2,1)}), bf16[16,128,128]{2,1,0:T(8,128)(2,1)S(1)}, u32[]{:S(2)}, u32[]{:S(2)}) async-start(bf16[16,128,128]{2,1,0:T(8,128)(2,1)} %broadcast_in_dim.35), calls=%async_computation.2 | async-start | bytes 1048576 | tf_op jit(solution)/shard_map/all_to_all | solution.py:45
  75.7 71.6 %copy-start.10 = (s32[16,5]{0,1:T(8,128)}, s32[16,5]{0,1:T(8,128)S(1)}, u32[]{:S(2)}) copy-start(s32[16,5]{0,1:T(8,128)S(1)} %reduce-window.9) | copy-start | bytes 964
  153.7 3.7 %copy-start.13 = (f32[8]{0:T(128)S(1)}, f32[8]{0:T(128)}, u32[]{:S(2)}) copy-start(f32[8]{0:T(128)} %param.20) | copy-start | bytes 100
  153.7 3.8 %copy-start.7 = (s32[1024]{0:T(1024)S(1)}, s32[1024]{0:T(1024)}, u32[]{:S(2)}) copy-start(s32[1024]{0:T(1024)} %get-tuple-element.59) | copy-start | bytes 12292
  153.7 3.8 %copy-start.8 = (s32[1024]{0:T(1024)S(1)}, s32[1024]{0:T(1024)}, u32[]{:S(2)}) copy-start(s32[1024]{0:T(1024)} %get-tuple-element.60) | copy-start | bytes 12292
  153.7 3.8 %copy-start.12 = (s32[1,2048]{1,0:T(1,128)S(1)}, s32[1,2048]{1,0:T(1,128)}, u32[]{:S(2)}) copy-start(s32[1,2048]{1,0:T(1,128)} %param.14) | copy-start | bytes 24580
  157.5 5.2 %slice-start = ((s8[6029312]{0:T(1024)(128)(4,1)}), s8[4194304]{0:T(1024)(128)(4,1)S(1)}, s32[]{:S(2)}) async-start(s8[6029312]{0:T(1024)(128)(4,1)} %bitcast.157), calls=%async_computation.10 | async-start | bytes 8388608
  157.5 5.2 %slice-start.1 = ((s8[6029312]{0:T(1024)(128)(4,1)}), s8[1835008]{0:T(1024)(128)(4,1)S(1)}, s32[]{:S(2)}) async-start(s8[6029312]{0:T(1024)(128)(4,1)} %bitcast.157), calls=%async_computation.11 | async-start | bytes 3670016
  162.6 6.1 %copy-start.2 = (s32[1,128,4]{2,1,0:T(8,128)S(1)}, s32[1,128,4]{2,1,0:T(8,128)}, u32[]{:S(2)}) copy-start(s32[1,128,4]{2,1,0:T(8,128)} %copy-done.1) | copy-start | bytes 6148
  162.7 6.2 %copy-start.5 = (s32[16,4,128]{2,0,1:T(8,128)S(1)}, s32[16,4,128]{2,0,1:T(8,128)}, u32[]{:S(2)}) copy-start(s32[16,4,128]{2,0,1:T(8,128)} %copy-done.4) | copy-start | bytes 98308
  162.7 6.2 %slice-start.2 = ((s32[16,5]{0,1:T(8,128)}), s32[16,4]{0,1:T(4,128)S(1)}, s32[]{:S(2)}) async-start(s32[16,5]{0,1:T(8,128)} %copy-done.10), calls=%async_computation.12 | async-start | bytes 4096 | tf_op jit(solution)/shard_map/slice.1
  162.7 6.2 %copy-start.11 = (s32[512]{0:T(512)S(1)}, s32[512]{0:T(512)}, u32[]{:S(2)}) copy-start(s32[512]{0:T(512)} %eq.110) | copy-start | bytes 6148
  162.8 18.5 %copy-start.3 = (bf16[1,128,360]{1,2,0:T(8,128)(2,1)S(1)}, bf16[1,128,360]{1,2,0:T(8,128)(2,1)}, u32[]{:S(2)}) copy-start(bf16[1,128,360]{1,2,0:T(8,128)(2,1)} %param.13) | copy-start | bytes 276484
  164.8 16.4 %all-to-all-start.3 = ((bf16[8,360,128]{2,1,0:T(8,128)(2,1)}), bf16[8,360,128]{2,1,0:T(8,128)(2,1)S(1)}, u32[]{:S(2)}, u32[]{:S(2)}) async-start(bf16[8,360,128]{2,1,0:T(8,128)(2,1)} %reshape.428), calls=%async_computation.3 | async-start | bytes 1474560 | tf_op jit(solution)/shard_map/all_to_all | solution.py:184
  168.7 88.9 %all-gather.4.cloned.1.call-start = ((), (), s32[]{:S(2)}) async-start(), calls=%async_computation.7 | async-start | bytes 4976640 | tf_op jit(solution)/shard_map/all_gather | solution.py:215
  205.4 55.6 %copy-start.14 = (f32[2880]{0:T(1024)S(1)}, f32[2880]{0:T(1024)}, u32[]{:S(2)}) copy-start(f32[2880]{0:T(1024)} %param.21) | copy-start | bytes 34564
  205.4 123.9 %reduce-scatter.2.cloned.1.call-start = ((), (), s32[]{:S(2)}) async-start(), calls=%async_computation.8 | async-start | bytes 4976640 | tf_op jit(solution)/shard_map/reduce_scatter | solution.py:231
  257.6 3.6 copy-start
  257.6 7.7 %slice-start.3 = ((s8[4239360]{0:T(1024)(128)(4,1)}), s8[4194304]{0:T(1024)(128)(4,1)S(1)}, s32[]{:S(2)}) async-start(s8[4239360]{0:T(1024)(128)(4,1)} %bitcast.175), calls=%async_computation.13 | async-start | bytes 8388608
  261.2 4.1 %slice-start.4 = ((s8[4239360]{0:T(1024)(128)(4,1)}), s8[45056]{0:T(1024)(128)(4,1)S(1)}, s32[]{:S(2)}) async-start(s8[4239360]{0:T(1024)(128)(4,1)} %bitcast.175), calls=%async_computation.14 | async-start | bytes 90112
  272.2 85.6 %copy-start.15 = (f32[1,128,4]{1,2,0:T(4,128)S(1)}, f32[1,128,4]{1,2,0:T(4,128)}, u32[]{:S(2)}) copy-start(f32[1,128,4]{1,2,0:T(4,128)} %param.25) | copy-start | bytes 6148
  331.4 26.3 %all-to-all-start.5 = ((bf16[16,48,360]{2,1,0:T(8,128)(2,1)}), bf16[16,48,360]{2,1,0:T(8,128)(2,1)S(1)}, u32[]{:S(2)}, u32[]{:S(2)}) async-start(bf16[16,48,360]{2,1,0:T(8,128)(2,1)} %bitcast.40), calls=%async_computation.6 | async-start | bytes 1179648 | tf_op jit(solution)/shard_map/all_to_all | solution.py:235
Sparse Core Ops, SparseCore 0:
  10.6 132.9 all-gather.5
  205.5 52.0 all-gather.3
  272.3 56.9 reduce-scatter.1

commit v13 on v12

--- a/solution.py
+++ b/solution.py
@@ -214,8 +214,13 @@
     arrived_rows = arrived.reshape(expert_count * capacity, arrived.shape[2])
     inputs = rms_norm(lax.all_gather(arrived_rows, "mp", axis=1, tiled=True), moe_gain)
     w_in = expert_in[0]
-    gate_val = jnp.dot(inputs, w_in[0], preferred_element_type=jnp.float32)
-    up_val = jnp.dot(inputs, w_in[1], preferred_element_type=jnp.float32)
+    hidden_cols = w_in.shape[2]
+    inputs = lax.optimization_barrier(inputs)
+    gate_up = jnp.dot(
+        inputs, jnp.concatenate([w_in[0], w_in[1]], axis=1), preferred_element_type=jnp.float32
+    )
+    gate_val = gate_up[:, :hidden_cols]
+    up_val = gate_up[:, hidden_cols:]
     gate_val = jnp.minimum(gate_val, clamp_limit)
     up_val = jnp.clip(up_val, -clamp_limit, clamp_limit)
     activated = ((up_val + 1.0) * gate_val * jax.nn.sigmoid(glu_alpha * gate_val)).astype(

time: 367 us -> 366 us (level)
  local copies, waits for them, and re-layouts: 27.6 us -> 33.1 us
  waiting for transfers between devices: 232 us -> 227 us
    squeeze x0 -> x1, local copies, waits for them, and re-layouts: none -> 4.62 us  [shards(): w_in[0]]
    all_gather x1, waiting for transfers between devices: 48.8 us -> 44.4 us  [shards(): lax.all_gather(arrived_rows, 'mp', axis=1, tiled=True)]
  transfers between devices with their start and end apart: 8 -> 8, of which waited for: 7 -> 7; matrix products, arithmetic and copies ran while one was open for 8% -> 10% of each run, Pallas kernels for 0% -> 0%
where the time goes in v13:
time: 366 us; the launch traced here: 365 us
  waiting for transfers between devices  227 us (62%)
  starting transfers between devices  34.2 us (9%)
  local copies, waits for them, and re-layouts  33.1 us (9%)
  blocking collectives  22 us (6%)
  matrix products  17.8 us (5%)
  other arithmetic  16.8 us (5%)
  between operations  14.2 us (4%)
    all_gather x1, waiting for transfers between devices, shards(): lax.all_gather(jnp.pad(jnp.concatenate([w_query, w_out.T], axis=1), ((0,...  66 us
    reduce_scatter x1, waiting for transfers between devices, shards(): lax.psum_scatter(partials.astype(jnp.bfloat16), 'mp', scatter_dimension=0...  57.1 us
    all_gather x1, waiting for transfers between devices, shards(): lax.all_gather(arrived_rows, 'mp', axis=1, tiled=True)  44.4 us
    all_to_all x3, waiting for transfers between devices, gather_by_exchange(): lax.all_to_all(spread, axis_name, split_axis=0, concat_axis=0, tiled=True)  34.9 us
    all_to_all x1, blocking collectives, shards(): lax.all_to_all(outgoing, 'expert', split_axis=0, concat_axis=0, tiled=True)  22 us
    all_to_all x3, starting transfers between devices, gather_by_exchange(): lax.all_to_all(spread, axis_name, split_axis=0, concat_axis=0, tiled=True)  21.1 us
    all_to_all x1, waiting for transfers between devices, shards(): lax.all_to_all(expert_out, 'expert', split_axis=0, concat_axis=0, tiled=T...  15.2 us
    all_to_all x1, waiting for transfers between devices, shards(): lax.all_to_all(out_pieces, 'mp', split_axis=0, concat_axis=0, tiled=True)  9.69 us
  transfers between devices with their start and end apart: 8, of which 7 were waited for; matrix products, arithmetic and copies ran while one was open for 10% of the time, Pallas kernels for 0%

profile of v13, /device:TPU:1, one launch (start us, length us, event | category | flops | bytes accessed | tf_op | source)
XLA Modules:
  0.0 365.3 jit_solution(1830637323441085088)
XLA Ops:
  7.2 1.8 fusion.37
  9.1 1.9 broadcast_in_dim.29
  10.9 5.9 %all-to-all-start = ((bf16[8,360,128]{2,1,0:T(8,128)(2,1)}), bf16[8,360,128]{2,1,0:T(8,128)(2,1)S(1)}, u32[]{:S(2)}, u32[]{:S(2)}) async-start(bf16[8,360,128]{2,1,0:T(8,128)(2,1)} %broadcast_in_dim.29), calls=%async_computation | async-start | bytes 1474560 | tf_op jit(solution)/shard_map/all_to_all | solution.py:45
  16.8 0.8 copy.45
  17.6 0.1 eq.114
  17.7 0.7 eq.110
  18.4 0.8 pad_maximum_fusion
  19.2 0.1 copy.41
  19.3 1.2 reduce-window.6
  20.5 8.8 %all-to-all-done = bf16[8,360,128]{2,1,0:T(8,128)(2,1)S(1)} async-done(((bf16[8,360,128]{2,1,0:T(8,128)(2,1)}), bf16[8,360,128]{2,1,0:T(8,128)(2,1)S(1)}, u32[]{:S(2)}, u32[]{:S(2)}) %all-to-all-start) | async-done | bytes 737312 | tf_op jit(solution)/shard_map/all_to_all | solution.py:45
  29.3 1.0 broadcast_in_dim.30
  30.2 10.6 %all-to-all-start.1 = ((bf16[16,180,128]{2,1,0:T(8,128)(2,1)}), bf16[16,180,128]{2,1,0:T(8,128)(2,1)S(1)}, u32[]{:S(2)}, u32[]{:S(2)}) async-start(bf16[16,180,128]{2,1,0:T(8,128)(2,1)} %broadcast_in_dim.30), calls=%async_computation.1 | async-start | bytes 1507328 | tf_op jit(solution)/shard_map/all_to_all | solution.py:45
  40.9 0.7 dynamic-slice_bitcast_fusion
  41.5 0.6 broadcast_bitcast_fusion
  42.1 0.4 fusion.14
  42.6 0.4 fusion.16
  43.0 26.1 %all-to-all-done.1 = bf16[16,180,128]{2,1,0:T(8,128)(2,1)S(1)} async-done(((bf16[16,180,128]{2,1,0:T(8,128)(2,1)}), bf16[16,180,128]{2,1,0:T(8,128)(2,1)S(1)}, u32[]{:S(2)}, u32[]{:S(2)}) %all-to-all-start.1) | async-done | bytes 737312 | tf_op jit(solution)/shard_map/all_to_all | solution.py:45
  69.2 0.1 reshape.423
  69.3 0.4 fusion.68
  69.8 0.1 fusion.54
  69.9 0.1 copy.42
  70.0 0.9 broadcast_in_dim.35
  70.9 4.6 %all-to-all-start.2 = ((bf16[16,128,128]{2,1,0:T(8,128)(2,1)}), bf16[16,128,128]{2,1,0:T(8,128)(2,1)S(1)}, u32[]{:S(2)}, u32[]{:S(2)}) async-start(bf16[16,128,128]{2,1,0:T(8,128)(2,1)} %broadcast_in_dim.35), calls=%async_computation.2 | async-start | bytes 1048576 | tf_op jit(solution)/shard_map/all_to_all | solution.py:45
  75.5 0.2 slice_reduce_fusion
  75.8 0.8 multiply_cosine_fusion.1
  76.6 0.1 reshape.419
  76.7 0.9 pad.10
  77.6 66.0 %all-gather.6.cloned.1.call-done = bf16[2944,1024]{1,0:T(8,128)(2,1)} async-done(((bf16[184,1024]{1,0:T(8,128)(2,1)}), bf16[2944,1024]{1,0:T(8,128)(2,1)}) %all-gather.6.cloned.1.call-update) | async-done | bytes 6029328 | tf_op jit(solution)/shard_map/all_gather | solution.py:88
  143.6 3.7 %slice.73 = bf16[16,184,512]{2,1,0:T(8,128)(2,1)} slice(bf16[16,184,1024]{2,1,0:T(8,128)(2,1)} %bitcast.143), slice={[0:16], [0:184], [0:512]} | slice | bytes 6029312 | tf_op jit(solution)/shard_map/slice | solution.py:95
  147.3 3.3 copy.38
  150.7 2.1 fusion.67
  152.8 0.8 fusion.43
  153.7 3.7 %fusion.4 = (f32[1024]{0:T(1024)S(1)}, f32[1024,2048]{1,0:T(8,128)S(1)}) fusion(s32[2048]{0:T(1024)} %bitcast.159, s32[1024]{0:T(1024)} %get-tuple-element.62, s32[1024]{0:T(1024)} %get-tuple-element.61, bf16[2048,128]{1,0:T(8,128)(2,1)S(1)} %bitcast.141, bf16[8,8,8,128]{3,2,1,0:T(8,128)(2,1)S(1)} %bitcast.152), kind=kOutput, calls=%fused_computation.11 | convolution fusion | flops 281017344 | bytes 9064448 | tf_op jit(solution)/shard_map/while/body/eval_jaxpr/hrd,hkd->hrk/dot_general | solution.py:144
  157.5 3.5 convert_reduce_fusion
  161.1 1.5 fusion.24
  162.7 1.0 fusion.9
  163.7 1.0 reshape.428
  164.7 4.0 %all-to-all-start.3 = ((bf16[8,360,128]{2,1,0:T(8,128)(2,1)}), bf16[8,360,128]{2,1,0:T(8,128)(2,1)S(1)}, u32[]{:S(2)}, u32[]{:S(2)}) async-start(bf16[8,360,128]{2,1,0:T(8,128)(2,1)} %reshape.428), calls=%async_computation.3 | async-start | bytes 1474560 | tf_op jit(solution)/shard_map/all_to_all | solution.py:184
  168.8 0.1 mul.212
  169.0 2.4 scatter_custom_fusion
  171.5 9.7 %all-to-all-done.3 = bf16[8,360,128]{2,1,0:T(8,128)(2,1)S(1)} async-done(((bf16[8,360,128]{2,1,0:T(8,128)(2,1)}), bf16[8,360,128]{2,1,0:T(8,128)(2,1)S(1)}, u32[]{:S(2)}, u32[]{:S(2)}) %all-to-all-start.3) | async-done | bytes 737312 | tf_op jit(solution)/shard_map/all_to_all | solution.py:184
  181.3 0.4 convolution_convert_fusion
  181.7 0.3 copy.50
  182.1 22.0 %all_to_all.30 = bf16[16,48,360]{2,1,0:T(8,128)(2,1)S(1)} all-to-all(bf16[16,48,360]{2,1,0:T(8,128)(2,1)S(1)} %bitcast.138), channel_id=1, replica_groups=mesh['expert'=16,'mp'=8,'batch'=2] {'expert'}, dimensions={0} | all-to-all | bytes 1105920 | tf_op jit(solution)/shard_map/all_to_all | solution.py:213
  204.1 1.1 copy.51
  205.3 3.4 copy.60
  208.6 4.6 %slice_bitcast_fusion.1 = (bf16[2880,360]{0,1:T(8,128)(2,1)}, bf16[2880,360]{0,1:T(8,128)(2,1)}) fusion(bf16[1,2,2880,360]{2,3,1,0:T(8,128)(2,1)} %param.22), kind=kLoop, calls=%fused_computation.20 | loop fusion | bytes 8294400 | tf_op jit(solution)/shard_map/squeeze | solution.py:220
  213.2 44.4 %all-gather.4.cloned.1.call-done = bf16[768,2880]{0,1:T(8,128)(2,1)} async-done(((bf16[768,360]{0,1:T(8,128)(2,1)}), bf16[768,2880]{0,1:T(8,128)(2,1)}) %all-gather.4.cloned.1.call-update) | async-done | bytes 4423696 | tf_op jit(solution)/shard_map/all_gather | solution.py:215
  257.6 3.3 fusion
  261.0 0.2 copy-done
  261.2 1.4 fusion.2
  262.7 0.2 copy-done.1
  262.8 0.6 copy-done.2
  263.5 3.6 fusion.5
  267.1 0.4 fusion.28
  267.5 4.5 %convert_bitcast_fusion = bf16[8,768,360]{1,2,0:T(8,128)(2,1)} fusion(bf16[360,8,360]{0,2,1:T(8,128)(2,1)S(1)} %bitcast.140, bf16[768,360]{0,1:T(8,128)(2,1)S(1)} %fusion.28), kind=kOutput, calls=%fused_computation.12 | convolution fusion | flops 1594736640 | bytes 7050240 | tf_op jit(solution)/shard_map/rh,hjf->jrf/dot_general | solution.py:230
  272.0 57.1 %reduce-scatter.2.cloned.1.call-done = bf16[1,768,360]{1,2,0:T(8,128)(2,1)} async-done(((bf16[8,768,360]{1,2,0:T(8,128)(2,1)}), bf16[1,768,360]{1,2,0:T(8,128)(2,1)}) %reduce-scatter.2.cloned.1.call-update) | async-done | bytes 552976 | tf_op jit(solution)/shard_map/reduce_scatter | solution.py:236
  329.0 2.1 copy.53
  331.1 9.0 %all-to-all-start.5 = ((bf16[16,48,360]{2,1,0:T(8,128)(2,1)}), bf16[16,48,360]{2,1,0:T(8,128)(2,1)S(1)}, u32[]{:S(2)}, u32[]{:S(2)}) async-start(bf16[16,48,360]{2,1,0:T(8,128)(2,1)} %bitcast.40), calls=%async_computation.6 | async-start | bytes 1179648 | tf_op jit(solution)/shard_map/all_to_all | solution.py:240
  340.3 0.6 pad_maximum_fusion.2
  340.9 1.4 slice_bitcast_fusion.3
  342.3 15.2 %all-to-all-done.5 = bf16[16,48,360]{2,1,0:T(8,128)(2,1)S(1)} async-done(((bf16[16,48,360]{2,1,0:T(8,128)(2,1)}), bf16[16,48,360]{2,1,0:T(8,128)(2,1)S(1)}, u32[]{:S(2)}, u32[]{:S(2)}) %all-to-all-start.5) | async-done | bytes 552992 | tf_op jit(solution)/shard_map/all_to_all | solution.py:240
  357.5 0.6 fusion.20
  358.1 0.7 fusion.42
  (72 shorter events, 1.0 us)
Async XLA Ops:
  7.2 35.4 %copy-start.11 = (f32[2880]{0:T(1024)S(1)}, f32[2880]{0:T(1024)}, u32[]{:S(2)}) copy-start(f32[2880]{0:T(1024)} %param.15) | copy-start | bytes 34564
  7.2 136.4 %all-gather.6.cloned.1.call-start = ((), (), s32[]{:S(2)}) async-start(), calls=%async_computation.9 | async-start | bytes 6406144 | tf_op jit(solution)/shard_map/all_gather | solution.py:88
  10.9 18.3 %all-to-all-start = ((bf16[8,360,128]{2,1,0:T(8,128)(2,1)}), bf16[8,360,128]{2,1,0:T(8,128)(2,1)S(1)}, u32[]{:S(2)}, u32[]{:S(2)}) async-start(bf16[8,360,128]{2,1,0:T(8,128)(2,1)} %broadcast_in_dim.29), calls=%async_computation | async-start | bytes 1474560 | tf_op jit(solution)/shard_map/all_to_all | solution.py:45
  17.6 25.0 %copy-start.3 = (s32[1,128,4]{2,1,0:T(8,128)}, s32[1,128,4]{2,1,0:T(8,128)S(1)}, u32[]{:S(2)}) copy-start(s32[1,128,4]{2,1,0:T(8,128)S(1)} %copy.45) | copy-start | bytes 6148
  20.4 55.1 %copy-start.6 = (s32[16,4,128]{2,0,1:T(8,128)}, s32[16,4,128]{2,0,1:T(8,128)S(1)}, u32[]{:S(2)}) copy-start(s32[16,4,128]{2,0,1:T(8,128)S(1)} %reduce-window.6) | copy-start | bytes 98308
  30.2 38.9 %all-to-all-start.1 = ((bf16[16,180,128]{2,1,0:T(8,128)(2,1)}), bf16[16,180,128]{2,1,0:T(8,128)(2,1)S(1)}, u32[]{:S(2)}, u32[]{:S(2)}) async-start(bf16[16,180,128]{2,1,0:T(8,128)(2,1)} %broadcast_in_dim.30), calls=%async_computation.1 | async-start | bytes 1507328 | tf_op jit(solution)/shard_map/all_to_all | solution.py:45
  69.7 6.8 %copy-start.8 = (f32[128,128]{0,1:T(8,128)}, f32[128,128]{0,1:T(8,128)S(1)}, u32[]{:S(2)}) copy-start(f32[128,128]{0,1:T(8,128)S(1)} %fusion.68) | copy-start | bytes 196612
  70.9 82.7 %all-to-all-start.2 = ((bf16[16,128,128]{2,1,0:T(8,128)(2,1)}), bf16[16,128,128]{2,1,0:T(8,128)(2,1)S(1)}, u32[]{:S(2)}, u32[]{:S(2)}) async-start(bf16[16,128,128]{2,1,0:T(8,128)(2,1)} %broadcast_in_dim.35), calls=%async_computation.2 | async-start | bytes 1048576 | tf_op jit(solution)/shard_map/all_to_all | solution.py:45
  75.8 71.5 %copy-start.13 = (s32[16,5]{0,1:T(8,128)}, s32[16,5]{0,1:T(8,128)S(1)}, u32[]{:S(2)}) copy-start(s32[16,5]{0,1:T(8,128)S(1)} %reduce-window.9) | copy-start | bytes 964
  153.7 3.7 %copy-start.16 = (f32[8]{0:T(128)S(1)}, f32[8]{0:T(128)}, u32[]{:S(2)}) copy-start(f32[8]{0:T(128)} %param.20) | copy-start | bytes 100
  153.7 3.8 %copy-start.9 = (s32[1024]{0:T(1024)S(1)}, s32[1024]{0:T(1024)}, u32[]{:S(2)}) copy-start(s32[1024]{0:T(1024)} %get-tuple-element.61) | copy-start | bytes 12292
  153.7 3.8 %copy-start.10 = (s32[1024]{0:T(1024)S(1)}, s32[1024]{0:T(1024)}, u32[]{:S(2)}) copy-start(s32[1024]{0:T(1024)} %get-tuple-element.62) | copy-start | bytes 12292
  153.7 3.8 %copy-start.15 = (s32[1,2048]{1,0:T(1,128)S(1)}, s32[1,2048]{1,0:T(1,128)}, u32[]{:S(2)}) copy-start(s32[1,2048]{1,0:T(1,128)} %param.14) | copy-start | bytes 24580
  157.5 5.2 %slice-start = ((s8[6029312]{0:T(1024)(128)(4,1)}), s8[4194304]{0:T(1024)(128)(4,1)S(1)}, s32[]{:S(2)}) async-start(s8[6029312]{0:T(1024)(128)(4,1)} %bitcast.144), calls=%async_computation.10 | async-start | bytes 8388608
  157.5 5.2 %slice-start.1 = ((s8[6029312]{0:T(1024)(128)(4,1)}), s8[1835008]{0:T(1024)(128)(4,1)S(1)}, s32[]{:S(2)}) async-start(s8[6029312]{0:T(1024)(128)(4,1)} %bitcast.144), calls=%async_computation.11 | async-start | bytes 3670016
  162.6 6.1 %copy-start.4 = (s32[1,128,4]{2,1,0:T(8,128)S(1)}, s32[1,128,4]{2,1,0:T(8,128)}, u32[]{:S(2)}) copy-start(s32[1,128,4]{2,1,0:T(8,128)} %copy-done.3) | copy-start | bytes 6148
  162.6 6.2 %copy-start.7 = (s32[16,4,128]{2,0,1:T(8,128)S(1)}, s32[16,4,128]{2,0,1:T(8,128)}, u32[]{:S(2)}) copy-start(s32[16,4,128]{2,0,1:T(8,128)} %copy-done.6) | copy-start | bytes 98308
  162.7 6.2 %slice-start.2 = ((s32[16,5]{0,1:T(8,128)}), s32[16,4]{0,1:T(4,128)S(1)}, s32[]{:S(2)}) async-start(s32[16,5]{0,1:T(8,128)} %copy-done.13), calls=%async_computation.12 | async-start | bytes 4096 | tf_op jit(solution)/shard_map/slice.1
  162.7 6.2 %copy-start.14 = (s32[512]{0:T(512)S(1)}, s32[512]{0:T(512)}, u32[]{:S(2)}) copy-start(s32[512]{0:T(512)} %eq.110) | copy-start | bytes 6148
  162.7 18.5 %copy-start.5 = (bf16[1,128,360]{1,2,0:T(8,128)(2,1)S(1)}, bf16[1,128,360]{1,2,0:T(8,128)(2,1)}, u32[]{:S(2)}) copy-start(bf16[1,128,360]{1,2,0:T(8,128)(2,1)} %param.13) | copy-start | bytes 276484
  164.7 16.4 %all-to-all-start.3 = ((bf16[8,360,128]{2,1,0:T(8,128)(2,1)}), bf16[8,360,128]{2,1,0:T(8,128)(2,1)S(1)}, u32[]{:S(2)}, u32[]{:S(2)}) async-start(bf16[8,360,128]{2,1,0:T(8,128)(2,1)} %reshape.428), calls=%async_computation.3 | async-start | bytes 1474560 | tf_op jit(solution)/shard_map/all_to_all | solution.py:184
  168.7 88.9 %all-gather.4.cloned.1.call-start = ((), (), s32[]{:S(2)}) async-start(), calls=%async_computation.7 | async-start | bytes 4976640 | tf_op jit(solution)/shard_map/all_gather | solution.py:215
  205.2 123.8 %reduce-scatter.2.cloned.1.call-start = ((), (), s32[]{:S(2)}) async-start(), calls=%async_computation.8 | async-start | bytes 4976640 | tf_op jit(solution)/shard_map/reduce_scatter | solution.py:236
  213.2 47.8 %copy-start.12 = (f32[2880]{0:T(1024)S(1)}, f32[2880]{0:T(1024)}, u32[]{:S(2)}) copy-start(f32[2880]{0:T(1024)} %param.21) | copy-start | bytes 34564
  257.6 3.6 copy-start
  261.2 1.6 copy-start.1
  261.2 2.2 copy-start.2
  271.9 85.5 %copy-start.17 = (f32[1,128,4]{1,2,0:T(4,128)S(1)}, f32[1,128,4]{1,2,0:T(4,128)}, u32[]{:S(2)}) copy-start(f32[1,128,4]{1,2,0:T(4,128)} %param.25) | copy-start | bytes 6148
  331.1 26.4 %all-to-all-start.5 = ((bf16[16,48,360]{2,1,0:T(8,128)(2,1)}), bf16[16,48,360]{2,1,0:T(8,128)(2,1)S(1)}, u32[]{:S(2)}, u32[]{:S(2)}) async-start(bf16[16,48,360]{2,1,0:T(8,128)(2,1)} %bitcast.40), calls=%async_computation.6 | async-start | bytes 1179648 | tf_op jit(solution)/shard_map/all_to_all | solution.py:240
Sparse Core Ops, SparseCore 0:
  10.6 132.9 all-gather.5
  205.3 52.2 all-gather.3
  272.1 56.8 reduce-scatter.1

commit v14 on v13

--- a/solution.py
+++ b/solution.py
@@ -194,21 +194,17 @@
     )
     ranks = jnp.sum((jnp.cumsum(onehot, axis=0) - onehot) * onehot, axis=1)
     target = chosen * capacity + ranks
-    source_row = (
-        jnp.full((expert_count * capacity,), tok_count, jnp.int32)
-        .at[target]
-        .set(jnp.arange(tok_count * top_count, dtype=jnp.int32) // top_count)
-    )
-    padded = jnp.concatenate(
-        [first_out, jnp.zeros((1, first_out.shape[1]), jnp.bfloat16)], axis=0
-    )
-    pick = (source_row[:, None] == jnp.arange(tok_count + 1, dtype=jnp.int32)[None, :]).astype(
-        jnp.bfloat16
-    )
+    slot_of_route = (
+        target[None, :] == jnp.arange(expert_count * capacity, dtype=jnp.int32)[:, None]
+    ).astype(jnp.bfloat16)
     outgoing = (
-        jnp.dot(pick, padded, preferred_element_type=jnp.float32)
+        jnp.dot(
+            slot_of_route,
+            jnp.repeat(first_out, top_count, axis=0),
+            preferred_element_type=jnp.float32,
+        )
         .astype(jnp.bfloat16)
-        .reshape(expert_count, capacity, padded.shape[1])
+        .reshape(expert_count, capacity, first_out.shape[1])
     )
     arrived = lax.all_to_all(outgoing, "expert", split_axis=0, concat_axis=0, tiled=True)
     arrived_rows = arrived.reshape(expert_count * capacity, arrived.shape[2])

time: 366 us -> 367 us (level)
    all_to_all x3, waiting for transfers between devices: 34.9 us -> 39.1 us  [gather_by_exchange(): lax.all_to_all(spread, axis_name, split_axis=0, concat_axis=0, tiled=True)]
  transfers between devices with their start and end apart: 8 -> 8, of which waited for: 7 -> 7; matrix products, arithmetic and copies ran while one was open for 10% -> 9% of each run, Pallas kernels for 0% -> 0%
where the time goes in v14:
time: 367 us; the launch traced here: 366 us
  waiting for transfers between devices  229 us (62%)
  starting transfers between devices  33.4 us (9%)
  local copies, waits for them, and re-layouts  31.4 us (9%)
  blocking collectives  23 us (6%)
  matrix products  17.8 us (5%)
  other arithmetic  16.8 us (5%)
  between operations  14.2 us (4%)
    all_gather x1, waiting for transfers between devices, shards(): lax.all_gather(jnp.pad(jnp.concatenate([w_query, w_out.T], axis=1), ((0,...  63.4 us
    reduce_scatter x1, waiting for transfers between devices, shards(): lax.psum_scatter(partials.astype(jnp.bfloat16), 'mp', scatter_dimension=0...  57.1 us
    all_gather x1, waiting for transfers between devices, shards(): lax.all_gather(arrived_rows, 'mp', axis=1, tiled=True)  44.1 us
    all_to_all x3, waiting for transfers between devices, gather_by_exchange(): lax.all_to_all(spread, axis_name, split_axis=0, concat_axis=0, tiled=True)  39.1 us
    all_to_all x1, blocking collectives, shards(): lax.all_to_all(outgoing, 'expert', split_axis=0, concat_axis=0, tiled=True)  23 us
    all_to_all x3, starting transfers between devices, gather_by_exchange(): lax.all_to_all(spread, axis_name, split_axis=0, concat_axis=0, tiled=True)  20.6 us
    all_to_all x1, waiting for transfers between devices, shards(): lax.all_to_all(expert_out, 'expert', split_axis=0, concat_axis=0, tiled=T...  15.2 us
    all_to_all x1, waiting for transfers between devices, shards(): lax.all_to_all(out_pieces, 'mp', split_axis=0, concat_axis=0, tiled=True)  10.6 us
  transfers between devices with their start and end apart: 8, of which 7 were waited for; matrix products, arithmetic and copies ran while one was open for 9% of the time, Pallas kernels for 0%

profile of v14, /device:TPU:1, one launch (start us, length us, event | category | flops | bytes accessed | tf_op | source)
XLA Modules:
  0.0 366.1 jit_solution(14832277778042871753)
XLA Ops:
  7.2 1.8 fusion.39
  9.1 1.9 broadcast_in_dim.33
  10.9 5.9 %all-to-all-start = ((bf16[8,360,128]{2,1,0:T(8,128)(2,1)}), bf16[8,360,128]{2,1,0:T(8,128)(2,1)S(1)}, u32[]{:S(2)}, u32[]{:S(2)}) async-start(bf16[8,360,128]{2,1,0:T(8,128)(2,1)} %broadcast_in_dim.33), calls=%async_computation | async-start | bytes 1474560 | tf_op jit(solution)/shard_map/all_to_all | solution.py:45
  16.8 0.8 pad_maximum_fusion
  17.7 11.6 %all-to-all-done = bf16[8,360,128]{2,1,0:T(8,128)(2,1)S(1)} async-done(((bf16[8,360,128]{2,1,0:T(8,128)(2,1)}), bf16[8,360,128]{2,1,0:T(8,128)(2,1)S(1)}, u32[]{:S(2)}, u32[]{:S(2)}) %all-to-all-start) | async-done | bytes 737312 | tf_op jit(solution)/shard_map/all_to_all | solution.py:45
  29.3 1.0 broadcast_in_dim.34
  30.2 10.8 %all-to-all-start.1 = ((bf16[16,180,128]{2,1,0:T(8,128)(2,1)}), bf16[16,180,128]{2,1,0:T(8,128)(2,1)S(1)}, u32[]{:S(2)}, u32[]{:S(2)}) async-start(bf16[16,180,128]{2,1,0:T(8,128)(2,1)} %broadcast_in_dim.34), calls=%async_computation.1 | async-start | bytes 1507328 | tf_op jit(solution)/shard_map/all_to_all | solution.py:45
  41.0 0.7 dynamic-slice_bitcast_fusion
  41.7 0.4 fusion.15
  42.2 0.4 fusion.17
  42.6 27.5 %all-to-all-done.1 = bf16[16,180,128]{2,1,0:T(8,128)(2,1)S(1)} async-done(((bf16[16,180,128]{2,1,0:T(8,128)(2,1)}), bf16[16,180,128]{2,1,0:T(8,128)(2,1)S(1)}, u32[]{:S(2)}, u32[]{:S(2)}) %all-to-all-start.1) | async-done | bytes 737312 | tf_op jit(solution)/shard_map/all_to_all | solution.py:45
  70.1 0.1 reshape.408
  70.2 0.4 fusion.63
  70.7 0.6 copy-done.6
  71.3 0.1 fusion.55
  71.6 0.9 broadcast_in_dim.35
  72.5 4.0 %all-to-all-start.2 = ((bf16[16,128,128]{2,1,0:T(8,128)(2,1)}), bf16[16,128,128]{2,1,0:T(8,128)(2,1)S(1)}, u32[]{:S(2)}, u32[]{:S(2)}) async-start(bf16[16,128,128]{2,1,0:T(8,128)(2,1)} %broadcast_in_dim.35), calls=%async_computation.2 | async-start | bytes 1048576 | tf_op jit(solution)/shard_map/all_to_all | solution.py:45
  76.4 0.6 broadcast_bitcast_fusion
  77.0 0.1 copy.47
  77.2 0.6 eq.114
  77.8 0.6 eq.110
  78.5 0.8 multiply_cosine_fusion.1
  79.2 0.1 reshape.404
  79.3 0.9 pad.9
  80.3 63.4 %all-gather.6.cloned.1.call-done = bf16[2944,1024]{1,0:T(8,128)(2,1)} async-done(((bf16[184,1024]{1,0:T(8,128)(2,1)}), bf16[2944,1024]{1,0:T(8,128)(2,1)}) %all-gather.6.cloned.1.call-update) | async-done | bytes 6029328 | tf_op jit(solution)/shard_map/all_gather | solution.py:88
  143.6 3.7 %slice.73 = bf16[16,184,512]{2,1,0:T(8,128)(2,1)} slice(bf16[16,184,1024]{2,1,0:T(8,128)(2,1)} %bitcast.142), slice={[0:16], [0:184], [0:512]} | slice | bytes 6029312 | tf_op jit(solution)/shard_map/slice | solution.py:95
  147.4 3.3 copy.40
  150.7 2.1 fusion.62
  152.8 0.8 fusion.44
  153.7 3.7 %fusion.4 = (f32[1024]{0:T(1024)S(1)}, f32[1024,2048]{1,0:T(8,128)S(1)}) fusion(s32[2048]{0:T(1024)} %bitcast.157, s32[1024]{0:T(1024)} %get-tuple-element.62, s32[1024]{0:T(1024)} %get-tuple-element.61, bf16[2048,128]{1,0:T(8,128)(2,1)S(1)} %bitcast.140, bf16[8,8,8,128]{3,2,1,0:T(8,128)(2,1)S(1)} %bitcast.151), kind=kOutput, calls=%fused_computation.10 | convolution fusion | flops 281017344 | bytes 9064448 | tf_op jit(solution)/shard_map/while/body/eval_jaxpr/hrd,hkd->hrk/dot_general | solution.py:144
  157.5 3.5 convert_reduce_fusion
  161.2 1.5 fusion.26
  162.7 1.0 fusion.9
  163.7 1.0 reshape.413
  164.7 3.5 all-to-all-start.3
  168.3 0.2 all-gather.4.cloned.1.call-start
  168.5 1.2 reduce-window.6
  169.7 0.2 slice_reduce_fusion
  170.0 10.6 %all-to-all-done.3 = bf16[8,360,128]{2,1,0:T(8,128)(2,1)S(1)} async-done(((bf16[8,360,128]{2,1,0:T(8,128)(2,1)}), bf16[8,360,128]{2,1,0:T(8,128)(2,1)S(1)}, u32[]{:S(2)}, u32[]{:S(2)}) %all-to-all-start.3) | async-done | bytes 737312 | tf_op jit(solution)/shard_map/all_to_all | solution.py:184
  180.8 0.1 copy.52
  181.1 0.2 reshape.415
  181.2 0.6 fusion.18
  181.8 0.3 copy.53
  182.1 23.0 %all_to_all.30 = bf16[16,48,360]{2,1,0:T(8,128)(2,1)S(1)} all-to-all(bf16[16,48,360]{2,1,0:T(8,128)(2,1)S(1)} %bitcast.137), channel_id=1, replica_groups=mesh['expert'=16,'mp'=8,'batch'=2] {'expert'}, dimensions={0} | all-to-all | bytes 1105920 | tf_op jit(solution)/shard_map/all_to_all | solution.py:209
  205.1 1.1 copy.54
  206.3 3.4 copy.63
  209.7 4.6 %slice_bitcast_fusion.1 = (bf16[2880,360]{0,1:T(8,128)(2,1)}, bf16[2880,360]{0,1:T(8,128)(2,1)}) fusion(bf16[1,2,2880,360]{2,3,1,0:T(8,128)(2,1)} %param.22), kind=kLoop, calls=%fused_computation.19 | loop fusion | bytes 8294400 | tf_op jit(solution)/shard_map/squeeze | solution.py:216
  214.3 44.1 %all-gather.4.cloned.1.call-done = bf16[768,2880]{0,1:T(8,128)(2,1)} async-done(((bf16[768,360]{0,1:T(8,128)(2,1)}), bf16[768,2880]{0,1:T(8,128)(2,1)}) %all-gather.4.cloned.1.call-update) | async-done | bytes 4423696 | tf_op jit(solution)/shard_map/all_gather | solution.py:211
  258.5 3.3 fusion
  261.8 0.2 copy-done
  262.0 1.4 fusion.2
  263.5 0.2 copy-done.1
  263.6 0.6 copy-done.2
  264.3 3.6 fusion.5
  267.9 0.4 fusion.30
  268.3 4.5 %convert_bitcast_fusion = bf16[8,768,360]{1,2,0:T(8,128)(2,1)} fusion(bf16[360,8,360]{0,2,1:T(8,128)(2,1)S(1)} %bitcast.139, bf16[768,360]{0,1:T(8,128)(2,1)S(1)} %fusion.30), kind=kOutput, calls=%fused_computation.11 | convolution fusion | flops 1594736640 | bytes 7050240 | tf_op jit(solution)/shard_map/rh,hjf->jrf/dot_general | solution.py:226
  272.8 57.1 %reduce-scatter.2.cloned.1.call-done = bf16[1,768,360]{1,2,0:T(8,128)(2,1)} async-done(((bf16[8,768,360]{1,2,0:T(8,128)(2,1)}), bf16[1,768,360]{1,2,0:T(8,128)(2,1)}) %reduce-scatter.2.cloned.1.call-update) | async-done | bytes 552976 | tf_op jit(solution)/shard_map/reduce_scatter | solution.py:232
  329.8 2.1 copy.56
  331.9 9.0 %all-to-all-start.5 = ((bf16[16,48,360]{2,1,0:T(8,128)(2,1)}), bf16[16,48,360]{2,1,0:T(8,128)(2,1)S(1)}, u32[]{:S(2)}, u32[]{:S(2)}) async-start(bf16[16,48,360]{2,1,0:T(8,128)(2,1)} %bitcast.38), calls=%async_computation.6 | async-start | bytes 1179648 | tf_op jit(solution)/shard_map/all_to_all | solution.py:236
  341.1 0.6 pad_maximum_fusion.2
  341.8 1.4 slice_bitcast_fusion.3
  343.1 15.2 %all-to-all-done.5 = bf16[16,48,360]{2,1,0:T(8,128)(2,1)S(1)} async-done(((bf16[16,48,360]{2,1,0:T(8,128)(2,1)}), bf16[16,48,360]{2,1,0:T(8,128)(2,1)S(1)}, u32[]{:S(2)}, u32[]{:S(2)}) %all-to-all-start.5) | async-done | bytes 552992 | tf_op jit(solution)/shard_map/all_to_all | solution.py:236
  358.3 0.6 fusion.22
  358.9 0.7 fusion.43
  (68 shorter events, 1.3 us)
Async XLA Ops:
  7.2 35.0 %copy-start.10 = (f32[2880]{0:T(1024)S(1)}, f32[2880]{0:T(1024)}, u32[]{:S(2)}) copy-start(f32[2880]{0:T(1024)} %param.15) | copy-start | bytes 34564
  7.2 136.4 %all-gather.6.cloned.1.call-start = ((), (), s32[]{:S(2)}) async-start(), calls=%async_computation.9 | async-start | bytes 6406144 | tf_op jit(solution)/shard_map/all_gather | solution.py:88
  10.9 18.3 %all-to-all-start = ((bf16[8,360,128]{2,1,0:T(8,128)(2,1)}), bf16[8,360,128]{2,1,0:T(8,128)(2,1)S(1)}, u32[]{:S(2)}, u32[]{:S(2)}) async-start(bf16[8,360,128]{2,1,0:T(8,128)(2,1)} %broadcast_in_dim.33), calls=%async_computation | async-start | bytes 1474560 | tf_op jit(solution)/shard_map/all_to_all | solution.py:45
  30.2 46.8 %copy-start.14 = (s32[1,128,4]{1,2,0:T(4,128)S(1)}, s32[1,128,4]{1,2,0:T(4,128)}, u32[]{:S(2)}) copy-start(s32[1,128,4]{1,2,0:T(4,128)} %param.24) | copy-start | bytes 6148
  30.2 39.9 %all-to-all-start.1 = ((bf16[16,180,128]{2,1,0:T(8,128)(2,1)}), bf16[16,180,128]{2,1,0:T(8,128)(2,1)S(1)}, u32[]{:S(2)}, u32[]{:S(2)}) async-start(bf16[16,180,128]{2,1,0:T(8,128)(2,1)} %broadcast_in_dim.34), calls=%async_computation.1 | async-start | bytes 1507328 | tf_op jit(solution)/shard_map/all_to_all | solution.py:45
  70.7 0.6 copy-start.6
  72.5 81.2 %all-to-all-start.2 = ((bf16[16,128,128]{2,1,0:T(8,128)(2,1)}), bf16[16,128,128]{2,1,0:T(8,128)(2,1)S(1)}, u32[]{:S(2)}, u32[]{:S(2)}) async-start(bf16[16,128,128]{2,1,0:T(8,128)(2,1)} %broadcast_in_dim.35), calls=%async_computation.2 | async-start | bytes 1048576 | tf_op jit(solution)/shard_map/all_to_all | solution.py:45
  77.2 2.1 copy-start.3
  153.7 3.7 %copy-start.15 = (f32[8]{0:T(128)S(1)}, f32[8]{0:T(128)}, u32[]{:S(2)}) copy-start(f32[8]{0:T(128)} %param.20) | copy-start | bytes 100
  153.7 3.8 %copy-start.8 = (s32[1024]{0:T(1024)S(1)}, s32[1024]{0:T(1024)}, u32[]{:S(2)}) copy-start(s32[1024]{0:T(1024)} %get-tuple-element.61) | copy-start | bytes 12292
  153.7 3.8 %copy-start.9 = (s32[1024]{0:T(1024)S(1)}, s32[1024]{0:T(1024)}, u32[]{:S(2)}) copy-start(s32[1024]{0:T(1024)} %get-tuple-element.62) | copy-start | bytes 12292
  153.7 3.8 %copy-start.13 = (s32[1,2048]{1,0:T(1,128)S(1)}, s32[1,2048]{1,0:T(1,128)}, u32[]{:S(2)}) copy-start(s32[1,2048]{1,0:T(1,128)} %param.14) | copy-start | bytes 24580
  157.5 5.2 %slice-start = ((s8[6029312]{0:T(1024)(128)(4,1)}), s8[4194304]{0:T(1024)(128)(4,1)S(1)}, s32[]{:S(2)}) async-start(s8[6029312]{0:T(1024)(128)(4,1)} %bitcast.143), calls=%async_computation.10 | async-start | bytes 8388608
  157.5 5.2 %slice-start.1 = ((s8[6029312]{0:T(1024)(128)(4,1)}), s8[1835008]{0:T(1024)(128)(4,1)S(1)}, s32[]{:S(2)}) async-start(s8[6029312]{0:T(1024)(128)(4,1)} %bitcast.143), calls=%async_computation.11 | async-start | bytes 3670016
  162.6 5.9 %copy-start.12 = (s32[4,128]{1,0:T(4,128)S(1)}, s32[4,128]{1,0:T(4,128)}, u32[]{:S(2)}) copy-start(s32[4,128]{1,0:T(4,128)} %eq.114) | copy-start | bytes 6148
  162.7 7.3 %copy-start.7 = (s32[512]{0:T(512)S(1)}, s32[512]{0:T(512)}, u32[]{:S(2)}) copy-start(s32[512]{0:T(512)} %eq.110) | copy-start | bytes 6148
  162.7 18.0 %copy-start.5 = (bf16[1,128,360]{1,2,0:T(8,128)(2,1)S(1)}, bf16[1,128,360]{1,2,0:T(8,128)(2,1)}, u32[]{:S(2)}) copy-start(bf16[1,128,360]{1,2,0:T(8,128)(2,1)} %param.13) | copy-start | bytes 276484
  164.7 16.0 %all-to-all-start.3 = ((bf16[8,360,128]{2,1,0:T(8,128)(2,1)}), bf16[8,360,128]{2,1,0:T(8,128)(2,1)S(1)}, u32[]{:S(2)}, u32[]{:S(2)}) async-start(bf16[8,360,128]{2,1,0:T(8,128)(2,1)} %reshape.413), calls=%async_computation.3 | async-start | bytes 1474560 | tf_op jit(solution)/shard_map/all_to_all | solution.py:184
  168.3 90.2 %all-gather.4.cloned.1.call-start = ((), (), s32[]{:S(2)}) async-start(), calls=%async_computation.7 | async-start | bytes 4976640 | tf_op jit(solution)/shard_map/all_gather | solution.py:211
  206.3 123.6 %reduce-scatter.2.cloned.1.call-start = ((), (), s32[]{:S(2)}) async-start(), calls=%async_computation.8 | async-start | bytes 4976640 | tf_op jit(solution)/shard_map/reduce_scatter | solution.py:232
  214.3 47.5 %copy-start.11 = (f32[2880]{0:T(1024)S(1)}, f32[2880]{0:T(1024)}, u32[]{:S(2)}) copy-start(f32[2880]{0:T(1024)} %param.21) | copy-start | bytes 34564
  258.5 3.6 copy-start
  262.0 1.6 copy-start.1
  262.0 2.2 copy-start.2
  272.7 68.3 %copy-start.4 = (s32[1,128,4]{2,1,0:T(8,128)S(1)}, s32[1,128,4]{2,1,0:T(8,128)}, u32[]{:S(2)}) copy-start(s32[1,128,4]{2,1,0:T(8,128)} %copy-done.3) | copy-start | bytes 6148
  272.7 85.6 %copy-start.16 = (f32[1,128,4]{1,2,0:T(4,128)S(1)}, f32[1,128,4]{1,2,0:T(4,128)}, u32[]{:S(2)}) copy-start(f32[1,128,4]{1,2,0:T(4,128)} %param.25) | copy-start | bytes 6148
  331.9 26.4 %all-to-all-start.5 = ((bf16[16,48,360]{2,1,0:T(8,128)(2,1)}), bf16[16,48,360]{2,1,0:T(8,128)(2,1)S(1)}, u32[]{:S(2)}, u32[]{:S(2)}) async-start(bf16[16,48,360]{2,1,0:T(8,128)(2,1)} %bitcast.38), calls=%async_computation.6 | async-start | bytes 1179648 | tf_op jit(solution)/shard_map/all_to_all | solution.py:236
Sparse Core Ops, SparseCore 0:
  10.6 132.9 all-gather.5
  206.4 52.0 all-gather.3
  272.9 56.9 reduce-scatter.1

commit v15 on v13

--- a/solution.py
+++ b/solution.py
@@ -234,8 +234,10 @@
         preferred_element_type=jnp.float32,
     )
     expert_out = lax.psum_scatter(
-        partials.astype(jnp.bfloat16), "mp", scatter_dimension=0, tiled=True
-    ).reshape(expert_count, capacity, -1)
+        partials.astype(jnp.bfloat16).reshape(mp_devs, expert_count, capacity, -1),
+        "mp",
+        scatter_dimension=0,
+    )
     local_width = expert_out.shape[2]
     returned = lax.all_to_all(expert_out, "expert", split_axis=0, concat_axis=0, tiled=True)
     slot_pick = (

time: 366 us -> 374 us (1.022)
  local copies, waits for them, and re-layouts: 33.1 us -> 37.6 us
    convert_element_type x0 -> x1, local copies, waits for them, and re-layouts: none -> 6.59 us  [shards(): partials.astype(jnp.bfloat16).reshape(mp_devs, expert_count, capacity, -1)]
  transfers between devices with their start and end apart: 8 -> 8, of which waited for: 7 -> 7; matrix products, arithmetic and copies ran while one was open for 10% -> 9% of each run, Pallas kernels for 0% -> 0%
where the time goes in v15:
time: 374 us; the launch traced here: 372 us
  waiting for transfers between devices  230 us (61%)
  local copies, waits for them, and re-layouts  37.6 us (10%)
  starting transfers between devices  34.2 us (9%)
  blocking collectives  22 us (6%)
  matrix products  17.8 us (5%)
  other arithmetic  16.8 us (4%)
  between operations  14.2 us (4%)
    all_gather x1, waiting for transfers between devices, shards(): lax.all_gather(jnp.pad(jnp.concatenate([w_query, w_out.T], axis=1), ((0,...  66 us
    reduce_scatter x1, waiting for transfers between devices, shards(): lax.psum_scatter(partials.astype(jnp.bfloat16).reshape(mp_devs, expert_co...  59.6 us
    all_gather x1, waiting for transfers between devices, shards(): lax.all_gather(arrived_rows, 'mp', axis=1, tiled=True)  44.4 us
    all_to_all x3, waiting for transfers between devices, gather_by_exchange(): lax.all_to_all(spread, axis_name, split_axis=0, concat_axis=0, tiled=True)  34.9 us
    all_to_all x1, blocking collectives, shards(): lax.all_to_all(outgoing, 'expert', split_axis=0, concat_axis=0, tiled=True)  22 us
    all_to_all x3, starting transfers between devices, gather_by_exchange(): lax.all_to_all(spread, axis_name, split_axis=0, concat_axis=0, tiled=True)  21.1 us
    all_to_all x1, waiting for transfers between devices, shards(): lax.all_to_all(expert_out, 'expert', split_axis=0, concat_axis=0, tiled=T...  15.2 us
    all_to_all x1, waiting for transfers between devices, shards(): lax.all_to_all(out_pieces, 'mp', split_axis=0, concat_axis=0, tiled=True)  9.69 us
  transfers between devices with their start and end apart: 8, of which 7 were waited for; matrix products, arithmetic and copies ran while one was open for 9% of the time, Pallas kernels for 0%

profile of v15, /device:TPU:1, one launch (start us, length us, event | category | flops | bytes accessed | tf_op | source)
XLA Modules:
  0.0 372.4 jit_solution(15334289996880697100)
XLA Ops:
  7.2 1.8 fusion.37
  9.1 1.9 broadcast_in_dim.29
  10.9 5.9 %all-to-all-start = ((bf16[8,360,128]{2,1,0:T(8,128)(2,1)}), bf16[8,360,128]{2,1,0:T(8,128)(2,1)S(1)}, u32[]{:S(2)}, u32[]{:S(2)}) async-start(bf16[8,360,128]{2,1,0:T(8,128)(2,1)} %broadcast_in_dim.29), calls=%async_computation | async-start | bytes 1474560 | tf_op jit(solution)/shard_map/all_to_all | solution.py:45
  16.8 0.8 copy.45
  17.6 0.1 eq.114
  17.7 0.7 eq.110
  18.4 0.8 pad_maximum_fusion
  19.2 0.1 copy.41
  19.3 1.2 reduce-window.6
  20.5 8.8 %all-to-all-done = bf16[8,360,128]{2,1,0:T(8,128)(2,1)S(1)} async-done(((bf16[8,360,128]{2,1,0:T(8,128)(2,1)}), bf16[8,360,128]{2,1,0:T(8,128)(2,1)S(1)}, u32[]{:S(2)}, u32[]{:S(2)}) %all-to-all-start) | async-done | bytes 737312 | tf_op jit(solution)/shard_map/all_to_all | solution.py:45
  29.3 1.0 broadcast_in_dim.30
  30.2 10.6 %all-to-all-start.1 = ((bf16[16,180,128]{2,1,0:T(8,128)(2,1)}), bf16[16,180,128]{2,1,0:T(8,128)(2,1)S(1)}, u32[]{:S(2)}, u32[]{:S(2)}) async-start(bf16[16,180,128]{2,1,0:T(8,128)(2,1)} %broadcast_in_dim.30), calls=%async_computation.1 | async-start | bytes 1507328 | tf_op jit(solution)/shard_map/all_to_all | solution.py:45
  40.9 0.7 dynamic-slice_bitcast_fusion
  41.5 0.6 broadcast_bitcast_fusion
  42.1 0.4 fusion.14
  42.6 0.4 fusion.16
  43.0 26.1 %all-to-all-done.1 = bf16[16,180,128]{2,1,0:T(8,128)(2,1)S(1)} async-done(((bf16[16,180,128]{2,1,0:T(8,128)(2,1)}), bf16[16,180,128]{2,1,0:T(8,128)(2,1)S(1)}, u32[]{:S(2)}, u32[]{:S(2)}) %all-to-all-start.1) | async-done | bytes 737312 | tf_op jit(solution)/shard_map/all_to_all | solution.py:45
  69.2 0.1 reshape.423
  69.3 0.4 fusion.68
  69.8 0.1 fusion.54
  69.9 0.1 copy.42
  70.0 0.9 broadcast_in_dim.35
  70.9 4.6 %all-to-all-start.2 = ((bf16[16,128,128]{2,1,0:T(8,128)(2,1)}), bf16[16,128,128]{2,1,0:T(8,128)(2,1)S(1)}, u32[]{:S(2)}, u32[]{:S(2)}) async-start(bf16[16,128,128]{2,1,0:T(8,128)(2,1)} %broadcast_in_dim.35), calls=%async_computation.2 | async-start | bytes 1048576 | tf_op jit(solution)/shard_map/all_to_all | solution.py:45
  75.5 0.2 slice_reduce_fusion
  75.8 0.8 multiply_cosine_fusion.1
  76.6 0.1 reshape.419
  76.7 0.9 pad.10
  77.6 66.0 %all-gather.6.cloned.1.call-done = bf16[2944,1024]{1,0:T(8,128)(2,1)} async-done(((bf16[184,1024]{1,0:T(8,128)(2,1)}), bf16[2944,1024]{1,0:T(8,128)(2,1)}) %all-gather.6.cloned.1.call-update) | async-done | bytes 6029328 | tf_op jit(solution)/shard_map/all_gather | solution.py:88
  143.6 3.7 %slice.73 = bf16[16,184,512]{2,1,0:T(8,128)(2,1)} slice(bf16[16,184,1024]{2,1,0:T(8,128)(2,1)} %bitcast.145), slice={[0:16], [0:184], [0:512]} | slice | bytes 6029312 | tf_op jit(solution)/shard_map/slice | solution.py:95
  147.3 3.3 copy.38
  150.7 2.1 fusion.67
  152.8 0.8 fusion.43
  153.7 3.7 fusion.4
  157.5 3.5 convert_reduce_fusion
  161.1 1.5 fusion.24
  162.7 1.0 fusion.9
  163.7 1.0 reshape.428
  164.7 4.0 %all-to-all-start.3 = ((bf16[8,360,128]{2,1,0:T(8,128)(2,1)}), bf16[8,360,128]{2,1,0:T(8,128)(2,1)S(1)}, u32[]{:S(2)}, u32[]{:S(2)}) async-start(bf16[8,360,128]{2,1,0:T(8,128)(2,1)} %reshape.428), calls=%async_computation.3 | async-start | bytes 1474560 | tf_op jit(solution)/shard_map/all_to_all | solution.py:184
  168.8 0.1 mul.212
  169.0 2.4 scatter_custom_fusion
  171.5 9.7 %all-to-all-done.3 = bf16[8,360,128]{2,1,0:T(8,128)(2,1)S(1)} async-done(((bf16[8,360,128]{2,1,0:T(8,128)(2,1)}), bf16[8,360,128]{2,1,0:T(8,128)(2,1)S(1)}, u32[]{:S(2)}, u32[]{:S(2)}) %all-to-all-start.3) | async-done | bytes 737312 | tf_op jit(solution)/shard_map/all_to_all | solution.py:184
  181.3 0.4 convolution_convert_fusion
  181.7 0.3 copy.50
  182.1 22.0 %all_to_all.30 = bf16[16,48,360]{2,1,0:T(8,128)(2,1)S(1)} all-to-all(bf16[16,48,360]{2,1,0:T(8,128)(2,1)S(1)} %bitcast.140), channel_id=1, replica_groups=mesh['expert'=16,'mp'=8,'batch'=2] {'expert'}, dimensions={0} | all-to-all | bytes 1105920 | tf_op jit(solution)/shard_map/all_to_all | solution.py:213
  204.1 1.1 copy.51
  205.3 3.4 copy.60
  208.6 4.6 %slice_bitcast_fusion.1 = (bf16[2880,360]{0,1:T(8,128)(2,1)}, bf16[2880,360]{0,1:T(8,128)(2,1)}) fusion(bf16[1,2,2880,360]{2,3,1,0:T(8,128)(2,1)} %param.22), kind=kLoop, calls=%fused_computation.20 | loop fusion | bytes 8294400 | tf_op jit(solution)/shard_map/squeeze | solution.py:220
  213.2 44.4 %all-gather.4.cloned.1.call-done = bf16[768,2880]{0,1:T(8,128)(2,1)} async-done(((bf16[768,360]{0,1:T(8,128)(2,1)}), bf16[768,2880]{0,1:T(8,128)(2,1)}) %all-gather.4.cloned.1.call-update) | async-done | bytes 4423696 | tf_op jit(solution)/shard_map/all_gather | solution.py:215
  257.6 3.3 fusion
  261.0 0.2 copy-done
  261.2 1.4 fusion.2
  262.7 0.2 copy-done.1
  262.8 0.6 copy-done.2
  263.5 3.6 fusion.5
  267.1 0.4 fusion.28
  267.5 4.5 %convert_bitcast_fusion = bf16[8,768,360]{1,2,0:T(8,128)(2,1)} fusion(bf16[360,8,360]{0,2,1:T(8,128)(2,1)S(1)} %bitcast.142, bf16[768,360]{0,1:T(8,128)(2,1)S(1)} %fusion.28), kind=kOutput, calls=%fused_computation.12 | convolution fusion | flops 1594736640 | bytes 7050240 | tf_op jit(solution)/shard_map/rh,hjf->jrf/dot_general | solution.py:230
  272.0 6.6 %copy.53 = bf16[8,768,360]{2,1,0:T(8,128)(2,1)} copy(bf16[8,768,360]{1,2,0:T(8,128)(2,1)} %convert_bitcast_fusion) | data formatting | bytes 8847360 | tf_op jit(solution)/shard_map/convert_element_type | solution.py:237
  278.6 59.6 %reduce-scatter.2.cloned.1.call-done = bf16[1,16,48,360]{3,2,1,0:T(8,128)(2,1)} async-done(((bf16[8,16,48,360]{3,2,1,0:T(8,128)(2,1)}), bf16[1,16,48,360]{3,2,1,0:T(8,128)(2,1)}) %reduce-scatter.2.cloned.1.call-update) | async-done | bytes 552976 | tf_op jit(solution)/shard_map/reduce_scatter | solution.py:236
  338.2 9.0 %all-to-all-start.5 = ((bf16[16,48,360]{2,1,0:T(8,128)(2,1)}), bf16[16,48,360]{2,1,0:T(8,128)(2,1)S(1)}, u32[]{:S(2)}, u32[]{:S(2)}) async-start(bf16[16,48,360]{2,1,0:T(8,128)(2,1)} %bitcast.150), calls=%async_computation.6 | async-start | bytes 1179648 | tf_op jit(solution)/shard_map/all_to_all | solution.py:242
  347.4 0.6 pad_maximum_fusion.2
  348.0 1.4 slice_bitcast_fusion.3
  349.4 15.2 %all-to-all-done.5 = bf16[16,48,360]{2,1,0:T(8,128)(2,1)S(1)} async-done(((bf16[16,48,360]{2,1,0:T(8,128)(2,1)}), bf16[16,48,360]{2,1,0:T(8,128)(2,1)S(1)}, u32[]{:S(2)}, u32[]{:S(2)}) %all-to-all-start.5) | async-done | bytes 552992 | tf_op jit(solution)/shard_map/all_to_all | solution.py:242
  364.5 0.6 fusion.20
  365.2 0.7 fusion.42
  (72 shorter events, 1.0 us)
Async XLA Ops:
  7.2 35.4 %copy-start.11 = (f32[2880]{0:T(1024)S(1)}, f32[2880]{0:T(1024)}, u32[]{:S(2)}) copy-start(f32[2880]{0:T(1024)} %param.15) | copy-start | bytes 34564
  7.2 136.4 %all-gather.6.cloned.1.call-start = ((), (), s32[]{:S(2)}) async-start(), calls=%async_computation.9 | async-start | bytes 6406144 | tf_op jit(solution)/shard_map/all_gather | solution.py:88
  10.9 18.3 %all-to-all-start = ((bf16[8,360,128]{2,1,0:T(8,128)(2,1)}), bf16[8,360,128]{2,1,0:T(8,128)(2,1)S(1)}, u32[]{:S(2)}, u32[]{:S(2)}) async-start(bf16[8,360,128]{2,1,0:T(8,128)(2,1)} %broadcast_in_dim.29), calls=%async_computation | async-start | bytes 1474560 | tf_op jit(solution)/shard_map/all_to_all | solution.py:45
  17.6 25.0 %copy-start.3 = (s32[1,128,4]{2,1,0:T(8,128)}, s32[1,128,4]{2,1,0:T(8,128)S(1)}, u32[]{:S(2)}) copy-start(s32[1,128,4]{2,1,0:T(8,128)S(1)} %copy.45) | copy-start | bytes 6148
  20.4 55.1 %copy-start.6 = (s32[16,4,128]{2,0,1:T(8,128)}, s32[16,4,128]{2,0,1:T(8,128)S(1)}, u32[]{:S(2)}) copy-start(s32[16,4,128]{2,0,1:T(8,128)S(1)} %reduce-window.6) | copy-start | bytes 98308
  30.2 38.9 %all-to-all-start.1 = ((bf16[16,180,128]{2,1,0:T(8,128)(2,1)}), bf16[16,180,128]{2,1,0:T(8,128)(2,1)S(1)}, u32[]{:S(2)}, u32[]{:S(2)}) async-start(bf16[16,180,128]{2,1,0:T(8,128)(2,1)} %broadcast_in_dim.30), calls=%async_computation.1 | async-start | bytes 1507328 | tf_op jit(solution)/shard_map/all_to_all | solution.py:45
  69.7 6.8 %copy-start.8 = (f32[128,128]{0,1:T(8,128)}, f32[128,128]{0,1:T(8,128)S(1)}, u32[]{:S(2)}) copy-start(f32[128,128]{0,1:T(8,128)S(1)} %fusion.68) | copy-start | bytes 196612
  70.9 82.7 %all-to-all-start.2 = ((bf16[16,128,128]{2,1,0:T(8,128)(2,1)}), bf16[16,128,128]{2,1,0:T(8,128)(2,1)S(1)}, u32[]{:S(2)}, u32[]{:S(2)}) async-start(bf16[16,128,128]{2,1,0:T(8,128)(2,1)} %broadcast_in_dim.35), calls=%async_computation.2 | async-start | bytes 1048576 | tf_op jit(solution)/shard_map/all_to_all | solution.py:45
  75.8 71.5 %copy-start.13 = (s32[16,5]{0,1:T(8,128)}, s32[16,5]{0,1:T(8,128)S(1)}, u32[]{:S(2)}) copy-start(s32[16,5]{0,1:T(8,128)S(1)} %reduce-window.9) | copy-start | bytes 964
  153.7 3.7 %copy-start.16 = (f32[8]{0:T(128)S(1)}, f32[8]{0:T(128)}, u32[]{:S(2)}) copy-start(f32[8]{0:T(128)} %param.20) | copy-start | bytes 100
  153.7 3.8 %copy-start.9 = (s32[1024]{0:T(1024)S(1)}, s32[1024]{0:T(1024)}, u32[]{:S(2)}) copy-start(s32[1024]{0:T(1024)} %get-tuple-element.61) | copy-start | bytes 12292
  153.7 3.8 %copy-start.10 = (s32[1024]{0:T(1024)S(1)}, s32[1024]{0:T(1024)}, u32[]{:S(2)}) copy-start(s32[1024]{0:T(1024)} %get-tuple-element.62) | copy-start | bytes 12292
  153.7 3.8 %copy-start.15 = (s32[1,2048]{1,0:T(1,128)S(1)}, s32[1,2048]{1,0:T(1,128)}, u32[]{:S(2)}) copy-start(s32[1,2048]{1,0:T(1,128)} %param.14) | copy-start | bytes 24580
  157.5 5.2 %slice-start = ((s8[6029312]{0:T(1024)(128)(4,1)}), s8[4194304]{0:T(1024)(128)(4,1)S(1)}, s32[]{:S(2)}) async-start(s8[6029312]{0:T(1024)(128)(4,1)} %bitcast.146), calls=%async_computation.10 | async-start | bytes 8388608
  157.5 5.2 %slice-start.1 = ((s8[6029312]{0:T(1024)(128)(4,1)}), s8[1835008]{0:T(1024)(128)(4,1)S(1)}, s32[]{:S(2)}) async-start(s8[6029312]{0:T(1024)(128)(4,1)} %bitcast.146), calls=%async_computation.11 | async-start | bytes 3670016
  162.6 6.1 %copy-start.4 = (s32[1,128,4]{2,1,0:T(8,128)S(1)}, s32[1,128,4]{2,1,0:T(8,128)}, u32[]{:S(2)}) copy-start(s32[1,128,4]{2,1,0:T(8,128)} %copy-done.3) | copy-start | bytes 6148
  162.6 6.2 %copy-start.7 = (s32[16,4,128]{2,0,1:T(8,128)S(1)}, s32[16,4,128]{2,0,1:T(8,128)}, u32[]{:S(2)}) copy-start(s32[16,4,128]{2,0,1:T(8,128)} %copy-done.6) | copy-start | bytes 98308
  162.7 6.2 %slice-start.2 = ((s32[16,5]{0,1:T(8,128)}), s32[16,4]{0,1:T(4,128)S(1)}, s32[]{:S(2)}) async-start(s32[16,5]{0,1:T(8,128)} %copy-done.13), calls=%async_computation.12 | async-start | bytes 4096 | tf_op jit(solution)/shard_map/slice.1
  162.7 6.2 %copy-start.14 = (s32[512]{0:T(512)S(1)}, s32[512]{0:T(512)}, u32[]{:S(2)}) copy-start(s32[512]{0:T(512)} %eq.110) | copy-start | bytes 6148
  162.7 18.5 %copy-start.5 = (bf16[1,128,360]{1,2,0:T(8,128)(2,1)S(1)}, bf16[1,128,360]{1,2,0:T(8,128)(2,1)}, u32[]{:S(2)}) copy-start(bf16[1,128,360]{1,2,0:T(8,128)(2,1)} %param.13) | copy-start | bytes 276484
  164.7 16.4 %all-to-all-start.3 = ((bf16[8,360,128]{2,1,0:T(8,128)(2,1)}), bf16[8,360,128]{2,1,0:T(8,128)(2,1)S(1)}, u32[]{:S(2)}, u32[]{:S(2)}) async-start(bf16[8,360,128]{2,1,0:T(8,128)(2,1)} %reshape.428), calls=%async_computation.3 | async-start | bytes 1474560 | tf_op jit(solution)/shard_map/all_to_all | solution.py:184
  168.7 88.9 %all-gather.4.cloned.1.call-start = ((), (), s32[]{:S(2)}) async-start(), calls=%async_computation.7 | async-start | bytes 4976640 | tf_op jit(solution)/shard_map/all_gather | solution.py:215
  205.2 133.0 %reduce-scatter.2.cloned.1.call-start = ((), (), s32[]{:S(2)}) async-start(), calls=%async_computation.8 | async-start | bytes 5308416 | tf_op jit(solution)/shard_map/reduce_scatter | solution.py:236
  213.2 47.8 %copy-start.12 = (f32[2880]{0:T(1024)S(1)}, f32[2880]{0:T(1024)}, u32[]{:S(2)}) copy-start(f32[2880]{0:T(1024)} %param.21) | copy-start | bytes 34564
  257.6 3.6 copy-start
  261.2 1.6 copy-start.1
  261.2 2.2 copy-start.2
  278.6 86.0 %copy-start.17 = (f32[1,128,4]{1,2,0:T(4,128)S(1)}, f32[1,128,4]{1,2,0:T(4,128)}, u32[]{:S(2)}) copy-start(f32[1,128,4]{1,2,0:T(4,128)} %param.25) | copy-start | bytes 6148
  338.2 26.4 %all-to-all-start.5 = ((bf16[16,48,360]{2,1,0:T(8,128)(2,1)}), bf16[16,48,360]{2,1,0:T(8,128)(2,1)S(1)}, u32[]{:S(2)}, u32[]{:S(2)}) async-start(bf16[16,48,360]{2,1,0:T(8,128)(2,1)} %bitcast.150), calls=%async_computation.6 | async-start | bytes 1179648 | tf_op jit(solution)/shard_map/all_to_all | solution.py:242
Sparse Core Ops, SparseCore 0:
  10.6 132.9 all-gather.5
  205.3 52.2 all-gather.3
  278.7 59.4 reduce-scatter.1
